TPU v7x, 1024 devices: a whole 4x4x32 slice. The times are simulated.
1024 devices in a mesh: space: 128 (over z, x), wave: 8 (over y, core).
Axes of the slice: x: 4, y: 4, z: 32, core: 2. Of those that a mesh axis runs over, the one named last changes fastest.
Arguments:
- wavefunctions: bfloat16 [256, 131072], P('wave', 'space'), may hold values from -48 to 48
- filter_cells: bfloat16 [256, 729, 729], P('space'), may hold values from -1 to 1, as said below
- connectivity: int32 [256, 729], P('space'), may hold values from 0 to 1151, as said below
- owner_list: int32 [16384], P('space'), may hold values from 0 to 1023, as said below
Outputs:
- rotated_block: bfloat16 [256, 131072], P('wave', 'space')
Inputs may be any that keep to these rules, and one draw needn't show every extreme that they name: `connectivity`: the cells of each slab form a 2 x 1 x 1 block of cells of degree 8 in a box that is periodic in all three directions, the slabs following one another along the third. Entry l of a cell is the label of its node in that slab (each slab's 1024 labels a permutation of its nodes), or, for a node on the first node plane of the next slab, 1024 plus the node's position in that plane. `owner_list`: entry t * 128 + p is slab t's label of the node at position p of its first node plane. `filter_cells`: each cell's matrix is symmetric.
All inputs are finite; a program needn't handle non-finite values.
Results may differ from a plain program's by a relative error of at most 0.012.
Values may be sent and summed in bfloat16 or wider, within the bound.
No kernel may reach another device: no remote copies, remote signals or barrier semaphores. Data moves between devices by JAX's collectives and lax.ppermute only.
A program may use at most 32 MiB of HBM per device.

v0:
```python
import jax
import jax.numpy as jnp
from jax import lax
from jax.sharding import PartitionSpec as P

DEGREE = 4
NS_ITERS = 4


def from_behind(shard, axis, by):
    peers = lax.axis_size(axis)
    return lax.ppermute(shard, axis, [(i, (i + by) % peers) for i in range(peers)])


def apply_filter(wave_block, cell_matrices, connectivity, owner_list):
    column_count = wave_block.shape[0]
    node_count = wave_block.shape[1]
    plane_count = owner_list.shape[0]
    own_plane = jnp.take(wave_block, owner_list, axis=1)
    upper_plane = from_behind(own_plane, "space", -1)
    extended = jnp.concatenate([wave_block, upper_plane], axis=1)
    gathered = jnp.take(extended, connectivity, axis=1)
    products = jnp.einsum(
        "bcn,cnm->bcm", gathered, cell_matrices, preferred_element_type=jnp.float32
    )
    flat_index = connectivity.reshape(-1)
    summed = jnp.zeros((column_count, node_count + plane_count), jnp.float32)
    summed = summed.at[:, flat_index].add(products.reshape(column_count, flat_index.shape[0]))
    returned = from_behind(summed[:, node_count:], "space", 1)
    return summed[:, :node_count].at[:, owner_list].add(returned)


def newton_schulz(margin):
    highest = lax.Precision.HIGHEST
    size_cols = margin.shape[0]
    scale = jnp.sqrt(jnp.sum(margin * margin) + 1e-06)
    approx = margin / scale
    identity = jnp.eye(size_cols, dtype=jnp.float32)
    inverse = identity
    for iteration in range(NS_ITERS):
        middle = 1.5 * identity - 0.5 * jnp.dot(
            inverse, approx, precision=highest, preferred_element_type=jnp.float32
        )
        approx = jnp.dot(approx, middle, precision=highest, preferred_element_type=jnp.float32)
        inverse = jnp.dot(middle, inverse, precision=highest, preferred_element_type=jnp.float32)
    return (inverse / jnp.sqrt(scale)).astype(jnp.bfloat16)


def body(wavefunctions, filter_cells, connectivity, owner_list):
    previous = wavefunctions.astype(jnp.float32)
    current = apply_filter(wavefunctions, filter_cells, connectivity, owner_list)
    for degree_step in range(DEGREE - 1):
        following = (
            2.0 * apply_filter(current.astype(jnp.bfloat16), filter_cells, connectivity, owner_list)
            - previous
        )
        previous, current = (current, following)
    filtered = current.astype(jnp.bfloat16)
    node_total = filtered.shape[1] * lax.axis_size("space")
    column_count = filtered.shape[0]
    every_column = lax.all_gather(filtered, "wave", axis=0, tiled=True)
    partial_gram = jnp.dot(every_column, every_column.T, preferred_element_type=jnp.float32)
    margin = lax.psum(partial_gram, "space") / node_total
    rotation = newton_schulz(margin)
    own_rotation = lax.dynamic_slice_in_dim(
        rotation, lax.axis_index("wave") * column_count, column_count, 1
    )
    return jnp.dot(own_rotation.T, every_column, preferred_element_type=jnp.float32).astype(
        jnp.bfloat16
    )


def solution(mesh):
    return jax.shard_map(
        body,
        mesh=mesh,
        in_specs=(P("wave", "space"), P("space", None, None), P("space", None), P("space")),
        out_specs=P("wave", "space"),
        check_vma=False,
    )
```

profile of v0, /device:TPU:16, one launch (start us, length us, event | category | flops | bytes accessed | tf_op | source)
XLA Modules:
  0.0 711.2 jit_solution(18128010191553453087)
XLA Ops:
  9.9 20.9 %collective-permute-start = (bf16[32,128]{0,1:T(8,128)(2,1)S(1)}, bf16[32,128]{0,1:T(8,128)(2,1)S(1)}, u32[]{:S(2)}, u32[]{:S(2)}) collective-permute-start(bf16[32,128]{0,1:T(8,128)(2,1)S(1)} %select_bitcast_fusion.3), channel_id=1, source_target_pairs={{0,1016},{8,0},{16,8},{24,16},{32,24},{40,32},{48,40},{56,48},{64,... | collective-permute-start | bytes 24584 | tf_op jit(solution)/shard_map/ppermute | solution.py:12
  33.2 3.4 gather_fusion.1
  39.0 9.3 %scatter_custom_fusion = f32[32,1152]{0,1:T(8,128)S(1)} fusion(s32[1458]{0:T(1024)S(1)} %fusion.54, f32[1458,32]{1,0:T(8,128)} %copy.79, f32[]{:T(128)} %constant.29.clone.1), kind=kCustom, calls=%fused_computation.51 | custom fusion | flops 46656 | bytes 147968 | tf_op jit(solution)/shard_map/scatter-add | solution.py:28
  49.1 1.9 collective-permute-start.1
  52.1 6.6 collective-permute-done.1
  62.0 3.4 collective-permute-start.2
  65.5 2.4 collective-permute-done.2
  68.8 4.4 gather_fusion.3
  76.6 10.0 %scatter_custom_fusion.2 = f32[32,1152]{0,1:T(8,128)} fusion(s32[1458]{0:T(1024)} %copy-done.6, f32[1458,32]{1,0:T(8,128)} %copy.84, f32[]{:T(128)} %constant.29.clone.1), kind=kCustom, calls=%fused_computation.49 | custom fusion | flops 46656 | bytes 147968 | tf_op jit(solution)/shard_map/scatter-add | solution.py:28
  87.4 1.9 collective-permute-start.3
  90.4 6.6 collective-permute-done.3
  99.5 2.4 gather_fusion.4
  102.7 3.6 collective-permute-start.4
  106.3 2.2 collective-permute-done.4
  110.3 5.0 gather_fusion.5
  115.3 1.8 copy.86
  121.0 1.8 reshape.158
  122.8 2.1 copy.90
  124.9 10.0 %scatter_custom_fusion.4 = f32[32,1152]{0,1:T(8,128)} fusion(s32[1458]{0:T(1024)} %copy-done.6, f32[1458,32]{1,0:T(8,128)} %copy.90, f32[]{:T(128)} %constant.29.clone.1), kind=kCustom, calls=%fused_computation.47 | custom fusion | flops 46656 | bytes 147968 | tf_op jit(solution)/shard_map/scatter-add | solution.py:28
  135.7 1.9 collective-permute-start.5
  137.6 1.9 slice.52
  139.5 5.8 collective-permute-done.5
  145.3 3.3 scatter_custom_fusion.5
  148.6 1.8 subtract_convert_fusion.1
  152.8 3.4 collective-permute-start.6
  156.2 2.4 collective-permute-done.6
  159.6 4.4 gather_fusion.7
  167.4 10.0 %scatter_custom_fusion.6 = f32[32,1152]{0,1:T(8,128)} fusion(s32[1458]{0:T(1024)} %copy-done.6, f32[1458,32]{1,0:T(8,128)} %copy.95, f32[]{:T(128)} %constant.29.clone.1), kind=kCustom, calls=%fused_computation.45 | custom fusion | flops 46656 | bytes 147968 | tf_op jit(solution)/shard_map/scatter-add | solution.py:28
  178.2 1.9 collective-permute-start.7
  181.2 6.6 collective-permute-done.7
  191.4 12.1 %all_gather.3 = bf16[256,1024]{1,0:T(8,128)(2,1)S(1)} all-gather(bf16[32,1024]{1,0:T(8,128)(2,1)S(1)} %copy.96), channel_id=1, replica_groups=mesh['space'=128,'wave'=8] {'wave'}, dimensions={0}, use_global_device_ids=true | all-gather | bytes 589824 | tf_op jit(solution)/shard_map/all_gather | solution.py:61
  204.6 490.3 %all-reduce.2.cloned.1.call-done = f32[256,256]{1,0:T(8,128)} async-done(((f32[256,256]{1,0:T(8,128)}), f32[256,256]{1,0:T(8,128)}) %all-reduce.2.cloned.1.call-update) | async-done | bytes 262160 | tf_op jit(solution)/shard_map/psum | solution.py:63
  (93 shorter events, 51.4 us)
Async XLA Ops:
  6.5 30.5 %copy-start = (bf16[2,729,729]{2,0,1:T(2,128)(2,1)S(1)}, bf16[2,729,729]{2,0,1:T(2,128)(2,1)}, u32[]{:S(2)}) copy-start(bf16[2,729,729]{2,0,1:T(2,128)(2,1)} %param.9) | copy-start | bytes 6377296
  6.5 688.4 %all-reduce.2.cloned.1.call-start = ((), (), s32[]{:S(2)}) async-start(), calls=%async_computation | async-start | bytes 524288 | tf_op jit(solution)/shard_map/psum | solution.py:63
  7.3 0.7 copy-start.7
  8.0 25.1 %copy-start.5 = (pred[128]{0:T(512)(128)(4,1)}, pred[128]{0:T(512)(128)(4,1)S(1)}, u32[]{:S(2)}) copy-start(pred[128]{0:T(512)(128)(4,1)S(1)} %compare_and_fusion.1) | copy-start | bytes 388
  8.0 25.0 %copy-start.4 = (s32[1024]{0:T(1024)}, s32[1024]{0:T(1024)S(1)}, u32[]{:S(2)}) copy-start(s32[1024]{0:T(1024)S(1)} %pad_clamp_fusion.1) | copy-start | bytes 12292
  9.9 23.2 %collective-permute-start = (bf16[32,128]{0,1:T(8,128)(2,1)S(1)}, bf16[32,128]{0,1:T(8,128)(2,1)S(1)}, u32[]{:S(2)}, u32[]{:S(2)}) collective-permute-start(bf16[32,128]{0,1:T(8,128)(2,1)S(1)} %select_bitcast_fusion.3), channel_id=1, source_target_pairs={{0,1016},{8,0},{16,8},{24,16},{32,24},{40,32},{48,40},{56,48},{64,... | collective-permute-start | bytes 24584 | tf_op jit(solution)/shard_map/ppermute | solution.py:12
  33.0 6.0 copy-start.6
  33.1 4.4 copy-start.3
  48.3 0.8 copy-start.1
  49.1 9.6 %collective-permute-start.1 = (f32[32,128]{0,1:T(8,128)S(1)}, f32[32,128]{0,1:T(8,128)}, u32[]{:S(2)}, u32[]{:S(2)}) collective-permute-start(f32[32,128]{0,1:T(8,128)S(1)} %slice.49), channel_id=1, source_target_pairs={{0,8},{8,16},{16,24},{24,32},{32,40},{40,48},{48,56},{56,64},{64,7... | collective-permute-start | bytes 49160 | tf_op jit(solution)/shard_map/ppermute | solution.py:12
  60.5 4.9 copy-start.2
  62.0 5.8 collective-permute-start.2
  87.4 9.6 %collective-permute-start.3 = (f32[32,128]{0,1:T(8,128)S(1)}, f32[32,128]{0,1:T(8,128)}, u32[]{:S(2)}, u32[]{:S(2)}) collective-permute-start(f32[32,128]{0,1:T(8,128)S(1)} %slice.51), channel_id=1, source_target_pairs={{0,8},{8,16},{16,24},{24,32},{32,40},{40,48},{48,56},{56,64},{64,7... | collective-permute-start | bytes 49160 | tf_op jit(solution)/shard_map/ppermute | solution.py:12
  102.7 5.8 collective-permute-start.4
  135.7 9.6 %collective-permute-start.5 = (f32[32,128]{0,1:T(8,128)S(1)}, f32[32,128]{0,1:T(8,128)}, u32[]{:S(2)}, u32[]{:S(2)}) collective-permute-start(f32[32,128]{0,1:T(8,128)S(1)} %slice.53), channel_id=1, source_target_pairs={{0,8},{8,16},{16,24},{24,32},{32,40},{40,48},{48,56},{56,64},{64,7... | collective-permute-start | bytes 49160 | tf_op jit(solution)/shard_map/ppermute | solution.py:12
  152.8 5.8 collective-permute-start.6
  178.2 9.6 %collective-permute-start.7 = (f32[32,128]{0,1:T(8,128)S(1)}, f32[32,128]{0,1:T(8,128)}, u32[]{:S(2)}, u32[]{:S(2)}) collective-permute-start(f32[32,128]{0,1:T(8,128)S(1)} %slice.55), channel_id=1, source_target_pairs={{0,8},{8,16},{16,24},{24,32},{32,40},{40,48},{48,56},{56,64},{64,7... | collective-permute-start | bytes 49160 | tf_op jit(solution)/shard_map/ppermute | solution.py:12
Sparse Core Ops, SparseCore 0:
  204.7 490.1 all-reduce.1
where the time goes:
time: 713 us; the launch traced here: 711 us
  waiting for transfers between devices  523 us (73%)
  other arithmetic  62.9 us (9%)
  local copies, waits for them, and re-layouts  49.8 us (7%)
  starting transfers between devices  39 us (5%)
  between operations  14.6 us (2%)
  blocking collectives  12.1 us (2%)
  matrix products  9.95 us (1%)
    psum x1, waiting for transfers between devices, body(): margin = lax.psum(partial_gram, 'space') / node_total  490 us
    scatter-add x4, other arithmetic, apply_filter(): summed.at[:, flat_index]  39.1 us
    ppermute x8, starting transfers between devices, from_behind(): lax.ppermute(shard, axis, [(i, (i + by) % peers) for i in range(peers)])  39 us
    ppermute x8, waiting for transfers between devices, from_behind(): lax.ppermute(shard, axis, [(i, (i + by) % peers) for i in range(peers)])  32.4 us
    gather x12, local copies, waits for them, and re-layouts, apply_filter(): gathered = jnp.take(extended, connectivity, axis=1)  23.6 us
  transfers between devices with their start and end apart: 9, of which 8 were waited for; matrix products, arithmetic and copies ran while one was open for 1% of the time, Pallas kernels for 0%

commit v1 on v0

--- a/solution.py
+++ b/solution.py
@@ -30,6 +30,15 @@
     return summed[:, :node_count].at[:, owner_list].add(returned)
 
 
+def butterfly_sum(block, axis):
+    peers = lax.axis_size(axis)
+    stride = 1
+    while stride < peers:
+        block = block + lax.ppermute(block, axis, [(i, i ^ stride) for i in range(peers)])
+        stride *= 2
+    return block
+
+
 def newton_schulz(margin):
     highest = lax.Precision.HIGHEST
     size_cols = margin.shape[0]
@@ -59,8 +68,9 @@
     node_total = filtered.shape[1] * lax.axis_size("space")
     column_count = filtered.shape[0]
     every_column = lax.all_gather(filtered, "wave", axis=0, tiled=True)
-    partial_gram = jnp.dot(every_column, every_column.T, preferred_element_type=jnp.float32)
-    margin = lax.psum(partial_gram, "space") / node_total
+    own_rows = jnp.dot(filtered, every_column.T, preferred_element_type=jnp.float32)
+    own_rows = butterfly_sum(own_rows, "space")
+    margin = lax.all_gather(own_rows, "wave", axis=0, tiled=True) / node_total
     rotation = newton_schulz(margin)
     own_rotation = lax.dynamic_slice_in_dim(
         rotation, lax.axis_index("wave") * column_count, column_count, 1

time: 713 us -> 298 us (0.42)
  the two profiles are of different devices: /device:TPU:16 before, /device:TPU:1 now
where the time goes in v1:
time: 298 us; the launch traced here: 295 us
  waiting for transfers between devices  71.6 us (24%)
  other arithmetic  63.7 us (21%)
  starting transfers between devices  58.9 us (20%)
  local copies, waits for them, and re-layouts  49.7 us (17%)
  blocking collectives  43 us (14%)
  matrix products  7.26 us (2%)
    ppermute x7, waiting for transfers between devices, butterfly_sum(): lax.ppermute(block, axis, [(i, i ^ stride) for i in range(peers)])  44.7 us
    scatter-add x4, other arithmetic, apply_filter(): summed.at[:, flat_index]  39.1 us
    ppermute x8, starting transfers between devices, from_behind(): lax.ppermute(shard, axis, [(i, (i + by) % peers) for i in range(peers)])  36.1 us
    ppermute x8, waiting for transfers between devices, from_behind(): lax.ppermute(shard, axis, [(i, (i + by) % peers) for i in range(peers)])  26.9 us
    gather x12, local copies, waits for them, and re-layouts, apply_filter(): gathered = jnp.take(extended, connectivity, axis=1)  23.6 us
    ppermute x7, starting transfers between devices, butterfly_sum(): lax.ppermute(block, axis, [(i, i ^ stride) for i in range(peers)])  22.8 us
    all_gather x1, blocking collectives, body(): every_column = lax.all_gather(filtered, 'wave', axis=0, tiled=True)  22.5 us
    all_gather x1, blocking collectives, body(): margin = lax.all_gather(own_rows, 'wave', axis=0, tiled=True) / node_total  20.5 us
  transfers between devices with their start and end apart: 15, of which 14 were waited for; matrix products, arithmetic and copies ran while one was open for 3% of the time, Pallas kernels for 0%

profile of v1, /device:TPU:1, one launch (start us, length us, event | category | flops | bytes accessed | tf_op | source)
XLA Modules:
  0.0 295.4 jit_solution(8179560036134981811)
XLA Ops:
  3.3 21.4 %collective-permute-start = (bf16[32,128]{0,1:T(8,128)(2,1)S(1)}, bf16[32,128]{0,1:T(8,128)(2,1)S(1)}, u32[]{:S(2)}, u32[]{:S(2)}) collective-permute-start(bf16[32,128]{0,1:T(8,128)(2,1)S(1)} %select_bitcast_fusion.3), channel_id=1, source_target_pairs={{0,1016},{8,0},{16,8},{24,16},{32,24},{40,32},{48,40},{56,48},{64,... | collective-permute-start | bytes 24584 | tf_op jit(solution)/shard_map/ppermute | solution.py:12
  27.2 3.4 %gather_fusion.1 = bf16[1458,32]{1,0:T(8,128)(2,1)S(1)} fusion(bf16[32,1152]{0,1:T(8,128)(2,1)S(1)} %pad_maximum_fusion, s32[2048]{0:T(1024)S(1)} %pad_clamp_fusion), kind=kCustom, calls=%fused_computation.1.clone | custom fusion | bytes 192456 | tf_op jit(solution)/shard_map/jit(_take)/gather | solution.py:22
  33.0 9.3 %scatter_custom_fusion = f32[32,1152]{0,1:T(8,128)S(1)} fusion(s32[1458]{0:T(1024)S(1)} %fusion.54, f32[1458,32]{1,0:T(8,128)} %copy.79, f32[]{:T(128)} %constant.29.clone.1), kind=kCustom, calls=%fused_computation.51 | custom fusion | flops 46656 | bytes 147968 | tf_op jit(solution)/shard_map/scatter-add | solution.py:28
  46.1 5.4 %collective-permute-done.1 = f32[32,128]{0,1:T(8,128)} collective-permute-done((f32[32,128]{0,1:T(8,128)S(1)}, f32[32,128]{0,1:T(8,128)}, u32[]{:S(2)}, u32[]{:S(2)}) %collective-permute-start.1) | collective-permute-done | bytes 16416 | tf_op jit(solution)/shard_map/ppermute | solution.py:12
  54.9 2.3 collective-permute-start.2
  57.2 2.4 collective-permute-done.2
  60.5 4.4 %gather_fusion.3 = bf16[1458,32]{1,0:T(8,128)(2,1)} fusion(bf16[32,1152]{0,1:T(8,128)(2,1)S(1)} %pad_maximum_fusion.1, s32[2048]{0:T(1024)} %copy-done.3), kind=kCustom, calls=%fused_computation.5.clone | custom fusion | bytes 192456 | tf_op jit(solution)/shard_map/jit(_take)/gather | solution.py:22
  68.3 10.0 %scatter_custom_fusion.2 = f32[32,1152]{0,1:T(8,128)} fusion(s32[1458]{0:T(1024)} %copy-done.6, f32[1458,32]{1,0:T(8,128)} %copy.84, f32[]{:T(128)} %constant.29.clone.1), kind=kCustom, calls=%fused_computation.49 | custom fusion | flops 46656 | bytes 147968 | tf_op jit(solution)/shard_map/scatter-add | solution.py:28
  82.1 5.4 %collective-permute-done.3 = f32[32,128]{0,1:T(8,128)} collective-permute-done((f32[32,128]{0,1:T(8,128)S(1)}, f32[32,128]{0,1:T(8,128)}, u32[]{:S(2)}, u32[]{:S(2)}) %collective-permute-start.3) | collective-permute-done | bytes 16416 | tf_op jit(solution)/shard_map/ppermute | solution.py:12
  90.1 2.4 gather_fusion.4
  93.3 2.5 collective-permute-start.4
  95.8 2.2 collective-permute-done.4
  99.7 5.0 %gather_fusion.5 = bf16[1458,32]{1,0:T(8,128)(2,1)} fusion(bf16[32,1152]{0,1:T(8,128)(2,1)} %pad_maximum_fusion.2, s32[2048]{0:T(1024)} %copy-done.3), kind=kCustom, calls=%fused_computation.6.clone | custom fusion | bytes 192456 | tf_op jit(solution)/shard_map/jit(_take)/gather | solution.py:22
  114.3 10.0 %scatter_custom_fusion.4 = f32[32,1152]{0,1:T(8,128)} fusion(s32[1458]{0:T(1024)} %copy-done.6, f32[1458,32]{1,0:T(8,128)} %copy.90, f32[]{:T(128)} %constant.29.clone.1), kind=kCustom, calls=%fused_computation.47 | custom fusion | flops 46656 | bytes 147968 | tf_op jit(solution)/shard_map/scatter-add | solution.py:28
  128.9 4.6 %collective-permute-done.5 = f32[32,128]{0,1:T(8,128)} collective-permute-done((f32[32,128]{0,1:T(8,128)S(1)}, f32[32,128]{0,1:T(8,128)}, u32[]{:S(2)}, u32[]{:S(2)}) %collective-permute-start.5) | collective-permute-done | bytes 16416 | tf_op jit(solution)/shard_map/ppermute | solution.py:12
  133.5 3.3 %scatter_custom_fusion.5 = f32[32,1024]{0,1:T(8,128)} fusion(f32[32,1024]{0,1:T(8,128)} %slice.52, s32[128]{0:T(128)} %copy-done.7, f32[32,128]{0,1:T(8,128)} %collective-permute-done.5), kind=kCustom, calls=%fused_computation.72 | custom fusion | flops 4096 | bytes 196608 | tf_op jit(solution)/shard_map/scatter-add | solution.py:30
  141.0 2.3 collective-permute-start.6
  143.3 2.4 collective-permute-done.6
  146.7 4.4 %gather_fusion.7 = bf16[1458,32]{1,0:T(8,128)(2,1)} fusion(bf16[32,1152]{0,1:T(8,128)(2,1)S(1)} %pad_maximum_fusion.3, s32[2048]{0:T(1024)} %copy-done.3), kind=kCustom, calls=%fused_computation.7.clone | custom fusion | bytes 192456 | tf_op jit(solution)/shard_map/jit(_take)/gather | solution.py:22
  154.5 10.0 %scatter_custom_fusion.6 = f32[32,1152]{0,1:T(8,128)} fusion(s32[1458]{0:T(1024)} %copy-done.6, f32[1458,32]{1,0:T(8,128)} %copy.95, f32[]{:T(128)} %constant.29.clone.1), kind=kCustom, calls=%fused_computation.45 | custom fusion | flops 46656 | bytes 147968 | tf_op jit(solution)/shard_map/scatter-add | solution.py:28
  169.1 4.5 %collective-permute-done.7 = f32[32,128]{0,1:T(8,128)S(1)} collective-permute-done((f32[32,128]{0,1:T(8,128)S(1)}, f32[32,128]{0,1:T(8,128)S(1)}, u32[]{:S(2)}, u32[]{:S(2)}) %collective-permute-start.7) | collective-permute-done | bytes 16416 | tf_op jit(solution)/shard_map/ppermute | solution.py:12
  173.6 3.1 %scatter_custom_fusion.7 = f32[32,1024]{0,1:T(8,128)} fusion(f32[32,1024]{0,1:T(8,128)} %slice.54, s32[128]{0:T(128)} %copy-done.7, f32[32,128]{0,1:T(8,128)S(1)} %collective-permute-done.7), kind=kCustom, calls=%fused_computation.70 | custom fusion | flops 4096 | bytes 147456 | tf_op jit(solution)/shard_map/scatter-add | solution.py:30
  178.0 22.5 %all_gather.6 = bf16[256,1024]{1,0:T(8,128)(2,1)S(1)} all-gather(bf16[32,1024]{1,0:T(8,128)(2,1)S(1)} %copy.96), channel_id=1, replica_groups=mesh['space'=128,'wave'=8] {'wave'}, dimensions={0}, use_global_device_ids=true | all-gather | bytes 589824 | tf_op jit(solution)/shard_map/all_gather | solution.py:70
  202.7 2.7 collective-permute-done.8
  207.3 4.2 %collective-permute-done.9 = f32[32,256]{1,0:T(8,128)S(1)} collective-permute-done((f32[32,256]{1,0:T(8,128)S(1)}, f32[32,256]{1,0:T(8,128)S(1)}, u32[]{:S(2)}, u32[]{:S(2)}) %collective-permute-start.9) | collective-permute-done | bytes 32800 | tf_op jit(solution)/shard_map/ppermute | solution.py:37
  213.5 2.7 collective-permute-done.10
  218.1 3.7 %collective-permute-done.11 = f32[32,256]{1,0:T(8,128)S(1)} collective-permute-done((f32[32,256]{1,0:T(8,128)S(1)}, f32[32,256]{1,0:T(8,128)S(1)}, u32[]{:S(2)}, u32[]{:S(2)}) %collective-permute-start.11) | collective-permute-done | bytes 32800 | tf_op jit(solution)/shard_map/ppermute | solution.py:37
  223.8 7.1 %collective-permute-done.12 = f32[32,256]{1,0:T(8,128)S(1)} collective-permute-done((f32[32,256]{1,0:T(8,128)S(1)}, f32[32,256]{1,0:T(8,128)S(1)}, u32[]{:S(2)}, u32[]{:S(2)}) %collective-permute-start.12) | collective-permute-done | bytes 32800 | tf_op jit(solution)/shard_map/ppermute | solution.py:37
  232.8 12.6 %collective-permute-done.13 = f32[32,256]{1,0:T(8,128)S(1)} collective-permute-done((f32[32,256]{1,0:T(8,128)S(1)}, f32[32,256]{1,0:T(8,128)S(1)}, u32[]{:S(2)}, u32[]{:S(2)}) %collective-permute-start.13) | collective-permute-done | bytes 32800 | tf_op jit(solution)/shard_map/ppermute | solution.py:37
  245.4 11.3 %collective-permute-start.14 = (f32[32,256]{1,0:T(8,128)S(1)}, f32[32,256]{1,0:T(8,128)S(1)}, u32[]{:S(2)}, u32[]{:S(2)}) collective-permute-start(f32[32,256]{1,0:T(8,128)S(1)} %add.81), channel_id=1, source_target_pairs={{0,512},{8,520},{16,528},{24,536},{32,544},{40,552},{48,560},{56,5... | collective-permute-start | bytes 98312 | tf_op jit(solution)/shard_map/ppermute | solution.py:37
  256.7 11.6 %collective-permute-done.14 = f32[32,256]{1,0:T(8,128)S(1)} collective-permute-done((f32[32,256]{1,0:T(8,128)S(1)}, f32[32,256]{1,0:T(8,128)S(1)}, u32[]{:S(2)}, u32[]{:S(2)}) %collective-permute-start.14) | collective-permute-done | bytes 32800 | tf_op jit(solution)/shard_map/ppermute | solution.py:37
  268.3 20.5 %all_gather.7 = f32[256,256]{1,0:T(8,128)S(1)} all-gather(f32[32,256]{1,0:T(8,128)S(1)} %add.82), channel_id=1, replica_groups=mesh['space'=128,'wave'=8] {'wave'}, dimensions={0}, use_global_device_ids=true | all-gather | bytes 294912 | tf_op jit(solution)/shard_map/all_gather | solution.py:73
  (112 shorter events, 74.7 us)
Async XLA Ops:
  0.0 31.0 %copy-start = (bf16[2,729,729]{2,0,1:T(2,128)(2,1)S(1)}, bf16[2,729,729]{2,0,1:T(2,128)(2,1)}, u32[]{:S(2)}) copy-start(bf16[2,729,729]{2,0,1:T(2,128)(2,1)} %param.9) | copy-start | bytes 6377296
  0.8 0.7 copy-start.7
  1.5 25.6 %copy-start.5 = (pred[128]{0:T(512)(128)(4,1)}, pred[128]{0:T(512)(128)(4,1)S(1)}, u32[]{:S(2)}) copy-start(pred[128]{0:T(512)(128)(4,1)S(1)} %compare_and_fusion.1) | copy-start | bytes 388
  1.5 25.6 %copy-start.4 = (s32[1024]{0:T(1024)}, s32[1024]{0:T(1024)S(1)}, u32[]{:S(2)}) copy-start(s32[1024]{0:T(1024)S(1)} %pad_clamp_fusion.1) | copy-start | bytes 12292
  3.3 23.8 %collective-permute-start = (bf16[32,128]{0,1:T(8,128)(2,1)S(1)}, bf16[32,128]{0,1:T(8,128)(2,1)S(1)}, u32[]{:S(2)}, u32[]{:S(2)}) collective-permute-start(bf16[32,128]{0,1:T(8,128)(2,1)S(1)} %select_bitcast_fusion.3), channel_id=1, source_target_pairs={{0,1016},{8,0},{16,8},{24,16},{32,24},{40,32},{48,40},{56,48},{64,... | collective-permute-start | bytes 24584 | tf_op jit(solution)/shard_map/ppermute | solution.py:12
  27.1 6.0 %copy-start.6 = (s32[1458]{0:T(1024)}, s32[1458]{0:T(1024)S(1)}, u32[]{:S(2)}) copy-start(s32[1458]{0:T(1024)S(1)} %fusion.54) | copy-start | bytes 17500
  27.1 4.4 %copy-start.3 = (s32[2048]{0:T(1024)}, s32[2048]{0:T(1024)S(1)}, u32[]{:S(2)}) copy-start(s32[2048]{0:T(1024)S(1)} %pad_clamp_fusion) | copy-start | bytes 24580
  42.3 0.8 copy-start.1
  43.1 8.4 %collective-permute-start.1 = (f32[32,128]{0,1:T(8,128)S(1)}, f32[32,128]{0,1:T(8,128)}, u32[]{:S(2)}, u32[]{:S(2)}) collective-permute-start(f32[32,128]{0,1:T(8,128)S(1)} %slice.49), channel_id=1, source_target_pairs={{0,8},{8,16},{16,24},{24,32},{32,40},{40,48},{48,56},{56,64},{64,7... | collective-permute-start | bytes 49160 | tf_op jit(solution)/shard_map/ppermute | solution.py:12
  53.4 3.8 %copy-start.2 = (bf16[32,1024]{0,1:T(8,128)(2,1)}, bf16[32,1024]{0,1:T(8,128)(2,1)S(1)}, u32[]{:S(2)}) copy-start(bf16[32,1024]{0,1:T(8,128)(2,1)S(1)} %convert_element_type.22) | copy-start | bytes 196612
  54.9 4.7 %collective-permute-start.2 = (bf16[32,128]{0,1:T(8,128)(2,1)S(1)}, bf16[32,128]{0,1:T(8,128)(2,1)S(1)}, u32[]{:S(2)}, u32[]{:S(2)}) collective-permute-start(bf16[32,128]{0,1:T(8,128)(2,1)S(1)} %select_bitcast_fusion.2), channel_id=1, source_target_pairs={{0,1016},{8,0},{16,8},{24,16},{32,24},{40,32},{48,40},{56,48},{64,... | collective-permute-start | bytes 24584 | tf_op jit(solution)/shard_map/ppermute | solution.py:12
  79.1 8.4 %collective-permute-start.3 = (f32[32,128]{0,1:T(8,128)S(1)}, f32[32,128]{0,1:T(8,128)}, u32[]{:S(2)}, u32[]{:S(2)}) collective-permute-start(f32[32,128]{0,1:T(8,128)S(1)} %slice.51), channel_id=1, source_target_pairs={{0,8},{8,16},{16,24},{24,32},{32,40},{40,48},{48,56},{56,64},{64,7... | collective-permute-start | bytes 49160 | tf_op jit(solution)/shard_map/ppermute | solution.py:12
  93.3 4.7 %collective-permute-start.4 = (bf16[32,128]{0,1:T(8,128)(2,1)S(1)}, bf16[32,128]{0,1:T(8,128)(2,1)S(1)}, u32[]{:S(2)}, u32[]{:S(2)}) collective-permute-start(bf16[32,128]{0,1:T(8,128)(2,1)S(1)} %select_bitcast_fusion.1), channel_id=1, source_target_pairs={{0,1016},{8,0},{16,8},{24,16},{32,24},{40,32},{48,40},{56,48},{64,... | collective-permute-start | bytes 24584 | tf_op jit(solution)/shard_map/ppermute | solution.py:12
  125.1 8.4 %collective-permute-start.5 = (f32[32,128]{0,1:T(8,128)S(1)}, f32[32,128]{0,1:T(8,128)}, u32[]{:S(2)}, u32[]{:S(2)}) collective-permute-start(f32[32,128]{0,1:T(8,128)S(1)} %slice.53), channel_id=1, source_target_pairs={{0,8},{8,16},{16,24},{24,32},{32,40},{40,48},{48,56},{56,64},{64,7... | collective-permute-start | bytes 49160 | tf_op jit(solution)/shard_map/ppermute | solution.py:12
  141.0 4.7 %collective-permute-start.6 = (bf16[32,128]{0,1:T(8,128)(2,1)S(1)}, bf16[32,128]{0,1:T(8,128)(2,1)S(1)}, u32[]{:S(2)}, u32[]{:S(2)}) collective-permute-start(bf16[32,128]{0,1:T(8,128)(2,1)S(1)} %select_bitcast_fusion), channel_id=1, source_target_pairs={{0,1016},{8,0},{16,8},{24,16},{32,24},{40,32},{48,40},{56,48},{64,... | collective-permute-start | bytes 24584 | tf_op jit(solution)/shard_map/ppermute | solution.py:12
  165.3 8.3 %collective-permute-start.7 = (f32[32,128]{0,1:T(8,128)S(1)}, f32[32,128]{0,1:T(8,128)S(1)}, u32[]{:S(2)}, u32[]{:S(2)}) collective-permute-start(f32[32,128]{0,1:T(8,128)S(1)} %slice.55), channel_id=1, source_target_pairs={{0,8},{8,16},{16,24},{24,32},{32,40},{40,48},{48,56},{56,64},{64,7... | collective-permute-start | bytes 49160 | tf_op jit(solution)/shard_map/ppermute | solution.py:12
  200.8 4.7 %collective-permute-start.8 = (f32[32,256]{1,0:T(8,128)S(1)}, f32[32,256]{1,0:T(8,128)S(1)}, u32[]{:S(2)}, u32[]{:S(2)}) collective-permute-start(f32[32,256]{1,0:T(8,128)S(1)} %fusion.58), channel_id=1, source_target_pairs={{0,8},{8,0},{16,24},{24,16},{32,40},{40,32},{48,56},{56,48},{64,72... | collective-permute-start | bytes 98312 | tf_op jit(solution)/shard_map/ppermute | solution.py:37
  205.4 6.2 %collective-permute-start.9 = (f32[32,256]{1,0:T(8,128)S(1)}, f32[32,256]{1,0:T(8,128)S(1)}, u32[]{:S(2)}, u32[]{:S(2)}) collective-permute-start(f32[32,256]{1,0:T(8,128)S(1)} %add.76), channel_id=1, source_target_pairs={{0,16},{8,24},{16,0},{24,8},{32,48},{40,56},{48,32},{56,40},{64,80... | collective-permute-start | bytes 98312 | tf_op jit(solution)/shard_map/ppermute | solution.py:37
  211.6 4.6 %collective-permute-start.10 = (f32[32,256]{1,0:T(8,128)S(1)}, f32[32,256]{1,0:T(8,128)S(1)}, u32[]{:S(2)}, u32[]{:S(2)}) collective-permute-start(f32[32,256]{1,0:T(8,128)S(1)} %add.77), channel_id=1, source_target_pairs={{0,32},{8,40},{16,48},{24,56},{32,0},{40,8},{48,16},{56,24},{64,96... | collective-permute-start | bytes 98312 | tf_op jit(solution)/shard_map/ppermute | solution.py:37
  216.2 5.6 %collective-permute-start.11 = (f32[32,256]{1,0:T(8,128)S(1)}, f32[32,256]{1,0:T(8,128)S(1)}, u32[]{:S(2)}, u32[]{:S(2)}) collective-permute-start(f32[32,256]{1,0:T(8,128)S(1)} %add.78), channel_id=1, source_target_pairs={{0,64},{8,72},{16,80},{24,88},{32,96},{40,104},{48,112},{56,120},{... | collective-permute-start | bytes 98312 | tf_op jit(solution)/shard_map/ppermute | solution.py:37
  221.9 9.0 %collective-permute-start.12 = (f32[32,256]{1,0:T(8,128)S(1)}, f32[32,256]{1,0:T(8,128)S(1)}, u32[]{:S(2)}, u32[]{:S(2)}) collective-permute-start(f32[32,256]{1,0:T(8,128)S(1)} %add.79), channel_id=1, source_target_pairs={{0,128},{8,136},{16,144},{24,152},{32,160},{40,168},{48,176},{56,1... | collective-permute-start | bytes 98312 | tf_op jit(solution)/shard_map/ppermute | solution.py:37
  230.9 14.5 %collective-permute-start.13 = (f32[32,256]{1,0:T(8,128)S(1)}, f32[32,256]{1,0:T(8,128)S(1)}, u32[]{:S(2)}, u32[]{:S(2)}) collective-permute-start(f32[32,256]{1,0:T(8,128)S(1)} %add.80), channel_id=1, source_target_pairs={{0,256},{8,264},{16,272},{24,280},{32,288},{40,296},{48,304},{56,3... | collective-permute-start | bytes 98312 | tf_op jit(solution)/shard_map/ppermute | solution.py:37
  245.4 23.0 %collective-permute-start.14 = (f32[32,256]{1,0:T(8,128)S(1)}, f32[32,256]{1,0:T(8,128)S(1)}, u32[]{:S(2)}, u32[]{:S(2)}) collective-permute-start(f32[32,256]{1,0:T(8,128)S(1)} %add.81), channel_id=1, source_target_pairs={{0,512},{8,520},{16,528},{24,536},{32,544},{40,552},{48,560},{56,5... | collective-permute-start | bytes 98312 | tf_op jit(solution)/shard_map/ppermute | solution.py:37

commit v2 on v1

--- a/solution.py
+++ b/solution.py
@@ -12,22 +12,57 @@
     return lax.ppermute(shard, axis, [(i, (i + by) % peers) for i in range(peers)])
 
 
-def apply_filter(wave_block, cell_matrices, connectivity, owner_list):
+def split_three(values):
+    pieces = []
+    rest = values
+    for piece in range(3):
+        head = lax.reduce_precision(rest, exponent_bits=8, mantissa_bits=7)
+        pieces.append(head.astype(jnp.bfloat16))
+        rest = rest - head
+    return jnp.concatenate(pieces, axis=0)
+
+
+def sum_three(stacked):
+    rows = stacked.shape[0] // 3
+    return (stacked[:rows] + stacked[rows : 2 * rows]) + stacked[2 * rows :]
+
+
+def selectors(connectivity, owner_list, node_count):
+    plane_count = owner_list.shape[0]
+    slots = jnp.arange(node_count + plane_count, dtype=connectivity.dtype)
+    pick = (connectivity.reshape(-1)[:, None] == slots[None, :]).astype(jnp.bfloat16)
+    owner = (slots[:node_count, None] == owner_list[None, :]).astype(jnp.bfloat16)
+    return pick, owner
+
+
+def apply_filter(wave_block, cell_matrices, pick, owner):
     column_count = wave_block.shape[0]
     node_count = wave_block.shape[1]
-    plane_count = owner_list.shape[0]
-    own_plane = jnp.take(wave_block, owner_list, axis=1)
+    cell_count, cell_nodes, _ = cell_matrices.shape
+    own_plane = jnp.dot(wave_block, owner, preferred_element_type=jnp.float32).astype(jnp.bfloat16)
     upper_plane = from_behind(own_plane, "space", -1)
-    extended = jnp.concatenate([wave_block, upper_plane], axis=1)
-    gathered = jnp.take(extended, connectivity, axis=1)
+    contract_nodes = (((1,), (1,)), ((), ()))
+    gathered = lax.dot_general(
+        wave_block, pick[:, :node_count], contract_nodes, preferred_element_type=jnp.float32
+    ) + lax.dot_general(
+        upper_plane, pick[:, node_count:], contract_nodes, preferred_element_type=jnp.float32
+    )
+    gathered = gathered.astype(jnp.bfloat16).reshape(column_count, cell_count, cell_nodes)
     products = jnp.einsum(
         "bcn,cnm->bcm", gathered, cell_matrices, preferred_element_type=jnp.float32
     )
-    flat_index = connectivity.reshape(-1)
-    summed = jnp.zeros((column_count, node_count + plane_count), jnp.float32)
-    summed = summed.at[:, flat_index].add(products.reshape(column_count, flat_index.shape[0]))
-    returned = from_behind(summed[:, node_count:], "space", 1)
-    return summed[:, :node_count].at[:, owner_list].add(returned)
+    stacked = split_three(products.reshape(column_count, cell_count * cell_nodes))
+    plane_part = sum_three(
+        jnp.dot(stacked, pick[:, node_count:], preferred_element_type=jnp.float32)
+    )
+    returned = from_behind(plane_part, "space", 1)
+    local_part = sum_three(
+        jnp.dot(stacked, pick[:, :node_count], preferred_element_type=jnp.float32)
+    )
+    back = sum_three(
+        lax.dot_general(split_three(returned), owner, contract_nodes, preferred_element_type=jnp.float32)
+    )
+    return local_part + back
 
 
 def butterfly_sum(block, axis):
@@ -56,11 +91,12 @@
 
 
 def body(wavefunctions, filter_cells, connectivity, owner_list):
+    pick, owner = selectors(connectivity, owner_list, wavefunctions.shape[1])
     previous = wavefunctions.astype(jnp.float32)
-    current = apply_filter(wavefunctions, filter_cells, connectivity, owner_list)
+    current = apply_filter(wavefunctions, filter_cells, pick, owner)
     for degree_step in range(DEGREE - 1):
         following = (
-            2.0 * apply_filter(current.astype(jnp.bfloat16), filter_cells, connectivity, owner_list)
+            2.0 * apply_filter(current.astype(jnp.bfloat16), filter_cells, pick, owner)
             - previous
         )
         previous, current = (current, following)

time: 298 us -> 202 us (0.68)
  other arithmetic: 63.7 us -> 2.65 us
  local copies, waits for them, and re-layouts: 49.7 us -> 2.99 us
  matrix products: 7.26 us -> 25 us
    scatter-add x8 -> x0, other arithmetic: 49 us -> none  [the longest x4 39.1 us: apply_filter(): summed.at[:, flat_index]]
    gather x16 -> x0, local copies, waits for them, and re-layouts: 29.3 us -> none  [the longest x12 23.6 us: apply_filter(): gathered = jnp.take(extended, connectivity, axis=1)]
    dot_general x0 -> x24, matrix products: none -> 17.8 us  [the longest x4 5.13 us: apply_filter(): jnp.dot(stacked, pick[:, node_count:], preferred_element_type=jnp.float32)]
    slice x8 -> x0, local copies, waits for them, and re-layouts: 8.42 us -> none  [the longest x4 5.88 us: apply_filter(): return summed[:, :node_count].at[:, owner_list].add(returned)]
    reshape x9 -> x8, local copies, waits for them, and re-layouts: 8.64 us -> 1.36 us  [the longest x4 0.75 us: apply_filter(): products.reshape(column_count, cell_count * cell_nodes)]
    select_n x11 -> x0, other arithmetic: 5.02 us -> none  [the longest x5 3.05 us: apply_filter(): own_plane = jnp.take(wave_block, owner_list, axis=1)]
    concatenate x4 -> x0, other arithmetic: 3.81 us -> none  [apply_filter(): extended = jnp.concatenate([wave_block, upper_plane], axis=1)]
  transfers between devices with their start and end apart: 15 -> 15, of which waited for: 14 -> 14; matrix products, arithmetic and copies ran while one was open for 3% -> 5% of each run, Pallas kernels for 0% -> 0%
where the time goes in v2:
time: 202 us; the launch traced here: 201 us
  waiting for transfers between devices  68.9 us (34%)
  starting transfers between devices  57.8 us (29%)
  blocking collectives  42.5 us (21%)
  matrix products  25 us (12%)
  local copies, waits for them, and re-layouts  2.99 us (1%)
  other arithmetic  2.65 us (1%)
    ppermute x7, waiting for transfers between devices, butterfly_sum(): lax.ppermute(block, axis, [(i, i ^ stride) for i in range(peers)])  44.7 us
    ppermute x8, starting transfers between devices, from_behind(): lax.ppermute(shard, axis, [(i, (i + by) % peers) for i in range(peers)])  35 us
    ppermute x8, waiting for transfers between devices, from_behind(): lax.ppermute(shard, axis, [(i, (i + by) % peers) for i in range(peers)])  24.2 us
    ppermute x7, starting transfers between devices, butterfly_sum(): lax.ppermute(block, axis, [(i, i ^ stride) for i in range(peers)])  22.8 us
    all_gather x1, blocking collectives, body(): every_column = lax.all_gather(filtered, 'wave', axis=0, tiled=True)  22.2 us
    all_gather x1, blocking collectives, body(): margin = lax.all_gather(own_rows, 'wave', axis=0, tiled=True) / node_total  20.3 us
    dot_general x4, matrix products, apply_filter(): jnp.dot(stacked, pick[:, node_count:], preferred_element_type=jnp.float32)  5.13 us
  transfers between devices with their start and end apart: 15, of which 14 were waited for; matrix products, arithmetic and copies ran while one was open for 5% of the time, Pallas kernels for 0%

profile of v2, /device:TPU:1, one launch (start us, length us, event | category | flops | bytes accessed | tf_op | source)
XLA Modules:
  0.0 201.1 jit_solution(13630621284829174879)
XLA Ops:
  1.5 21.4 %collective-permute-start = (bf16[32,128]{0,1:T(8,128)(2,1)S(1)}, bf16[32,128]{0,1:T(8,128)(2,1)S(1)}, u32[]{:S(2)}, u32[]{:S(2)}) collective-permute-start(bf16[32,128]{0,1:T(8,128)(2,1)S(1)} %fusion.42), channel_id=1, source_target_pairs={{0,1016},{8,0},{16,8},{24,16},{32,24},{40,32},{48,40},{56,48},{64,... | collective-permute-start | bytes 24584 | tf_op jit(solution)/shard_map/ppermute | solution.py:12
  23.7 1.5 iota_compare_fusion
  29.0 1.9 collective-permute-start.1
  31.9 4.9 %collective-permute-done.1 = f32[32,128]{1,0:T(8,128)S(1)} collective-permute-done((f32[32,128]{1,0:T(8,128)S(1)}, f32[32,128]{1,0:T(8,128)S(1)}, u32[]{:S(2)}, u32[]{:S(2)}) %collective-permute-start.1) | collective-permute-done | bytes 16416 | tf_op jit(solution)/shard_map/ppermute | solution.py:12
  37.6 1.9 collective-permute-start.2
  40.5 1.5 collective-permute-done.2
  44.6 1.9 collective-permute-start.3
  47.5 4.9 %collective-permute-done.3 = f32[32,128]{1,0:T(8,128)S(1)} collective-permute-done((f32[32,128]{1,0:T(8,128)S(1)}, f32[32,128]{1,0:T(8,128)S(1)}, u32[]{:S(2)}, u32[]{:S(2)}) %collective-permute-start.3) | collective-permute-done | bytes 16416 | tf_op jit(solution)/shard_map/ppermute | solution.py:12
  53.2 1.9 collective-permute-start.4
  56.1 1.5 collective-permute-done.4
  60.2 1.9 collective-permute-start.5
  63.1 4.9 %collective-permute-done.5 = f32[32,128]{1,0:T(8,128)S(1)} collective-permute-done((f32[32,128]{1,0:T(8,128)S(1)}, f32[32,128]{1,0:T(8,128)S(1)}, u32[]{:S(2)}, u32[]{:S(2)}) %collective-permute-start.5) | collective-permute-done | bytes 16416 | tf_op jit(solution)/shard_map/ppermute | solution.py:12
  68.8 2.1 %collective-permute-start.6 = (bf16[32,128]{1,0:T(8,128)(2,1)S(1)}, bf16[32,128]{1,0:T(8,128)(2,1)S(1)}, u32[]{:S(2)}, u32[]{:S(2)}) collective-permute-start(bf16[32,128]{1,0:T(8,128)(2,1)S(1)} %fusion.49), channel_id=1, source_target_pairs={{0,1016},{8,0},{16,8},{24,16},{32,24},{40,32},{48,40},{56,48},{64,... | collective-permute-start | bytes 24584 | tf_op jit(solution)/shard_map/ppermute | solution.py:12
  71.9 1.6 collective-permute-done.6
  76.1 1.9 collective-permute-start.7
  79.0 4.9 %collective-permute-done.7 = f32[32,128]{1,0:T(8,128)S(1)} collective-permute-done((f32[32,128]{1,0:T(8,128)S(1)}, f32[32,128]{1,0:T(8,128)S(1)}, u32[]{:S(2)}, u32[]{:S(2)}) %collective-permute-start.7) | collective-permute-done | bytes 16416 | tf_op jit(solution)/shard_map/ppermute | solution.py:12
  84.4 22.2 %all_gather.6 = bf16[256,1024]{1,0:T(8,128)(2,1)S(1)} all-gather(bf16[32,1024]{1,0:T(8,128)(2,1)S(1)} %fusion.81), channel_id=1, replica_groups=mesh['space'=128,'wave'=8] {'wave'}, dimensions={0}, use_global_device_ids=true | all-gather | bytes 589824 | tf_op jit(solution)/shard_map/all_gather | solution.py:106
  106.8 1.9 collective-permute-start.8
  108.7 2.7 %collective-permute-done.8 = f32[32,256]{1,0:T(8,128)S(1)} collective-permute-done((f32[32,256]{1,0:T(8,128)S(1)}, f32[32,256]{1,0:T(8,128)S(1)}, u32[]{:S(2)}, u32[]{:S(2)}) %collective-permute-start.8) | collective-permute-done | bytes 32800 | tf_op jit(solution)/shard_map/ppermute | solution.py:72
  111.5 1.9 collective-permute-start.9
  113.4 4.2 %collective-permute-done.9 = f32[32,256]{1,0:T(8,128)S(1)} collective-permute-done((f32[32,256]{1,0:T(8,128)S(1)}, f32[32,256]{1,0:T(8,128)S(1)}, u32[]{:S(2)}, u32[]{:S(2)}) %collective-permute-start.9) | collective-permute-done | bytes 32800 | tf_op jit(solution)/shard_map/ppermute | solution.py:72
  117.6 1.9 collective-permute-start.10
  119.6 2.7 %collective-permute-done.10 = f32[32,256]{1,0:T(8,128)S(1)} collective-permute-done((f32[32,256]{1,0:T(8,128)S(1)}, f32[32,256]{1,0:T(8,128)S(1)}, u32[]{:S(2)}, u32[]{:S(2)}) %collective-permute-start.10) | collective-permute-done | bytes 32800 | tf_op jit(solution)/shard_map/ppermute | solution.py:72
  122.3 1.9 collective-permute-start.11
  124.2 3.7 %collective-permute-done.11 = f32[32,256]{1,0:T(8,128)S(1)} collective-permute-done((f32[32,256]{1,0:T(8,128)S(1)}, f32[32,256]{1,0:T(8,128)S(1)}, u32[]{:S(2)}, u32[]{:S(2)}) %collective-permute-start.11) | collective-permute-done | bytes 32800 | tf_op jit(solution)/shard_map/ppermute | solution.py:72
  127.9 1.9 collective-permute-start.12
  129.8 7.1 %collective-permute-done.12 = f32[32,256]{1,0:T(8,128)S(1)} collective-permute-done((f32[32,256]{1,0:T(8,128)S(1)}, f32[32,256]{1,0:T(8,128)S(1)}, u32[]{:S(2)}, u32[]{:S(2)}) %collective-permute-start.12) | collective-permute-done | bytes 32800 | tf_op jit(solution)/shard_map/ppermute | solution.py:72
  136.9 1.9 collective-permute-start.13
  138.8 12.6 %collective-permute-done.13 = f32[32,256]{1,0:T(8,128)S(1)} collective-permute-done((f32[32,256]{1,0:T(8,128)S(1)}, f32[32,256]{1,0:T(8,128)S(1)}, u32[]{:S(2)}, u32[]{:S(2)}) %collective-permute-start.13) | collective-permute-done | bytes 32800 | tf_op jit(solution)/shard_map/ppermute | solution.py:72
  151.4 11.3 %collective-permute-start.14 = (f32[32,256]{1,0:T(8,128)S(1)}, f32[32,256]{1,0:T(8,128)S(1)}, u32[]{:S(2)}, u32[]{:S(2)}) collective-permute-start(f32[32,256]{1,0:T(8,128)S(1)} %add.160), channel_id=1, source_target_pairs={{0,512},{8,520},{16,528},{24,536},{32,544},{40,552},{48,560},{56,5... | collective-permute-start | bytes 98312 | tf_op jit(solution)/shard_map/ppermute | solution.py:72
  162.7 11.7 %collective-permute-done.14 = f32[32,256]{1,0:T(8,128)S(1)} collective-permute-done((f32[32,256]{1,0:T(8,128)S(1)}, f32[32,256]{1,0:T(8,128)S(1)}, u32[]{:S(2)}, u32[]{:S(2)}) %collective-permute-start.14) | collective-permute-done | bytes 32800 | tf_op jit(solution)/shard_map/ppermute | solution.py:72
  174.4 20.3 %all_gather.7 = f32[256,256]{1,0:T(8,128)S(1)} all-gather(f32[32,256]{1,0:T(8,128)S(1)} %add.161), channel_id=1, replica_groups=mesh['space'=128,'wave'=8] {'wave'}, dimensions={0}, use_global_device_ids=true | all-gather | bytes 294912 | tf_op jit(solution)/shard_map/all_gather | solution.py:109
  (96 shorter events, 29.2 us)
Async XLA Ops:
  0.0 26.8 %copy-start = (bf16[2,729,729]{2,0,1:T(2,128)(2,1)S(1)}, bf16[2,729,729]{2,0,1:T(2,128)(2,1)}, u32[]{:S(2)}) copy-start(bf16[2,729,729]{2,0,1:T(2,128)(2,1)} %param.5) | copy-start | bytes 6377296
  0.0 25.1 %copy-start.6 = (bf16[32,1024]{1,0:T(8,128)(2,1)S(1)}, bf16[32,1024]{1,0:T(8,128)(2,1)}, u32[]{:S(2)}) copy-start(bf16[32,1024]{1,0:T(8,128)(2,1)} %param.4) | copy-start | bytes 196612
  1.5 24.7 %collective-permute-start = (bf16[32,128]{0,1:T(8,128)(2,1)S(1)}, bf16[32,128]{0,1:T(8,128)(2,1)S(1)}, u32[]{:S(2)}, u32[]{:S(2)}) collective-permute-start(bf16[32,128]{0,1:T(8,128)(2,1)S(1)} %fusion.42), channel_id=1, source_target_pairs={{0,1016},{8,0},{16,8},{24,16},{32,24},{40,32},{48,40},{56,48},{64,... | collective-permute-start | bytes 24584 | tf_op jit(solution)/shard_map/ppermute | solution.py:12
  25.1 1.2 copy-start.1
  27.6 3.3 %copy-start.2 = (pred[1458,1152]{1,0:T(8,128)(4,1)S(1)}, pred[1458,1152]{1,0:T(8,128)(4,1)}, u32[]{:S(2)}) copy-start(pred[1458,1152]{1,0:T(8,128)(4,1)} %copy-done.1) | copy-start | bytes 5038852
  29.0 7.8 %copy-start.7 = (s32[128]{0:T(128)S(1)}, s32[128]{0:T(128)}, u32[]{:S(2)}) copy-start(s32[128]{0:T(128)} %param.7) | copy-start | bytes 1540
  29.0 7.8 %collective-permute-start.1 = (f32[32,128]{1,0:T(8,128)S(1)}, f32[32,128]{1,0:T(8,128)S(1)}, u32[]{:S(2)}, u32[]{:S(2)}) collective-permute-start(f32[32,128]{1,0:T(8,128)S(1)} %slice_add_fusion.22), channel_id=1, source_target_pairs={{0,8},{8,16},{16,24},{24,32},{32,40},{40,48},{48,56},{56,64},{64,7... | collective-permute-start | bytes 49160 | tf_op jit(solution)/shard_map/ppermute | solution.py:12
  37.6 4.4 %collective-permute-start.2 = (bf16[32,128]{1,0:T(8,128)(2,1)S(1)}, bf16[32,128]{1,0:T(8,128)(2,1)S(1)}, u32[]{:S(2)}, u32[]{:S(2)}) collective-permute-start(bf16[32,128]{1,0:T(8,128)(2,1)S(1)} %fusion.43), channel_id=1, source_target_pairs={{0,1016},{8,0},{16,8},{24,16},{32,24},{40,32},{48,40},{56,48},{64,... | collective-permute-start | bytes 24584 | tf_op jit(solution)/shard_map/ppermute | solution.py:12
  43.3 3.3 %copy-start.3 = (pred[1458,1152]{1,0:T(8,128)(4,1)S(1)}, pred[1458,1152]{1,0:T(8,128)(4,1)}, u32[]{:S(2)}) copy-start(pred[1458,1152]{1,0:T(8,128)(4,1)} %copy-done.1) | copy-start | bytes 5038852
  44.6 7.8 %collective-permute-start.3 = (f32[32,128]{1,0:T(8,128)S(1)}, f32[32,128]{1,0:T(8,128)S(1)}, u32[]{:S(2)}, u32[]{:S(2)}) collective-permute-start(f32[32,128]{1,0:T(8,128)S(1)} %slice_add_fusion.20), channel_id=1, source_target_pairs={{0,8},{8,16},{16,24},{24,32},{32,40},{40,48},{48,56},{56,64},{64,7... | collective-permute-start | bytes 49160 | tf_op jit(solution)/shard_map/ppermute | solution.py:12
  53.2 4.4 %collective-permute-start.4 = (bf16[32,128]{1,0:T(8,128)(2,1)S(1)}, bf16[32,128]{1,0:T(8,128)(2,1)S(1)}, u32[]{:S(2)}, u32[]{:S(2)}) collective-permute-start(bf16[32,128]{1,0:T(8,128)(2,1)S(1)} %fusion.46), channel_id=1, source_target_pairs={{0,1016},{8,0},{16,8},{24,16},{32,24},{40,32},{48,40},{56,48},{64,... | collective-permute-start | bytes 24584 | tf_op jit(solution)/shard_map/ppermute | solution.py:12
  58.9 3.3 %copy-start.4 = (pred[1458,1152]{1,0:T(8,128)(4,1)S(1)}, pred[1458,1152]{1,0:T(8,128)(4,1)}, u32[]{:S(2)}) copy-start(pred[1458,1152]{1,0:T(8,128)(4,1)} %copy-done.1) | copy-start | bytes 5038852
  60.2 7.8 %collective-permute-start.5 = (f32[32,128]{1,0:T(8,128)S(1)}, f32[32,128]{1,0:T(8,128)S(1)}, u32[]{:S(2)}, u32[]{:S(2)}) collective-permute-start(f32[32,128]{1,0:T(8,128)S(1)} %slice_add_fusion.18), channel_id=1, source_target_pairs={{0,8},{8,16},{16,24},{24,32},{32,40},{40,48},{48,56},{56,64},{64,7... | collective-permute-start | bytes 49160 | tf_op jit(solution)/shard_map/ppermute | solution.py:12
  68.8 4.7 %collective-permute-start.6 = (bf16[32,128]{1,0:T(8,128)(2,1)S(1)}, bf16[32,128]{1,0:T(8,128)(2,1)S(1)}, u32[]{:S(2)}, u32[]{:S(2)}) collective-permute-start(bf16[32,128]{1,0:T(8,128)(2,1)S(1)} %fusion.49), channel_id=1, source_target_pairs={{0,1016},{8,0},{16,8},{24,16},{32,24},{40,32},{48,40},{56,48},{64,... | collective-permute-start | bytes 24584 | tf_op jit(solution)/shard_map/ppermute | solution.py:12
  74.8 3.3 %copy-start.5 = (pred[1458,1152]{1,0:T(8,128)(4,1)S(1)}, pred[1458,1152]{1,0:T(8,128)(4,1)}, u32[]{:S(2)}) copy-start(pred[1458,1152]{1,0:T(8,128)(4,1)} %copy-done.1) | copy-start | bytes 5038852
  76.1 7.8 %collective-permute-start.7 = (f32[32,128]{1,0:T(8,128)S(1)}, f32[32,128]{1,0:T(8,128)S(1)}, u32[]{:S(2)}, u32[]{:S(2)}) collective-permute-start(f32[32,128]{1,0:T(8,128)S(1)} %slice_add_fusion.16), channel_id=1, source_target_pairs={{0,8},{8,16},{16,24},{24,32},{32,40},{40,48},{48,56},{56,64},{64,7... | collective-permute-start | bytes 49160 | tf_op jit(solution)/shard_map/ppermute | solution.py:12
  106.8 4.7 %collective-permute-start.8 = (f32[32,256]{1,0:T(8,128)S(1)}, f32[32,256]{1,0:T(8,128)S(1)}, u32[]{:S(2)}, u32[]{:S(2)}) collective-permute-start(f32[32,256]{1,0:T(8,128)S(1)} %fusion.171), channel_id=1, source_target_pairs={{0,8},{8,0},{16,24},{24,16},{32,40},{40,32},{48,56},{56,48},{64,72... | collective-permute-start | bytes 98312 | tf_op jit(solution)/shard_map/ppermute | solution.py:72
  111.5 6.2 %collective-permute-start.9 = (f32[32,256]{1,0:T(8,128)S(1)}, f32[32,256]{1,0:T(8,128)S(1)}, u32[]{:S(2)}, u32[]{:S(2)}) collective-permute-start(f32[32,256]{1,0:T(8,128)S(1)} %add.155), channel_id=1, source_target_pairs={{0,16},{8,24},{16,0},{24,8},{32,48},{40,56},{48,32},{56,40},{64,80... | collective-permute-start | bytes 98312 | tf_op jit(solution)/shard_map/ppermute | solution.py:72
  117.6 4.6 %collective-permute-start.10 = (f32[32,256]{1,0:T(8,128)S(1)}, f32[32,256]{1,0:T(8,128)S(1)}, u32[]{:S(2)}, u32[]{:S(2)}) collective-permute-start(f32[32,256]{1,0:T(8,128)S(1)} %add.156), channel_id=1, source_target_pairs={{0,32},{8,40},{16,48},{24,56},{32,0},{40,8},{48,16},{56,24},{64,96... | collective-permute-start | bytes 98312 | tf_op jit(solution)/shard_map/ppermute | solution.py:72
  122.3 5.6 %collective-permute-start.11 = (f32[32,256]{1,0:T(8,128)S(1)}, f32[32,256]{1,0:T(8,128)S(1)}, u32[]{:S(2)}, u32[]{:S(2)}) collective-permute-start(f32[32,256]{1,0:T(8,128)S(1)} %add.157), channel_id=1, source_target_pairs={{0,64},{8,72},{16,80},{24,88},{32,96},{40,104},{48,112},{56,120},{... | collective-permute-start | bytes 98312 | tf_op jit(solution)/shard_map/ppermute | solution.py:72
  127.9 9.0 %collective-permute-start.12 = (f32[32,256]{1,0:T(8,128)S(1)}, f32[32,256]{1,0:T(8,128)S(1)}, u32[]{:S(2)}, u32[]{:S(2)}) collective-permute-start(f32[32,256]{1,0:T(8,128)S(1)} %add.158), channel_id=1, source_target_pairs={{0,128},{8,136},{16,144},{24,152},{32,160},{40,168},{48,176},{56,1... | collective-permute-start | bytes 98312 | tf_op jit(solution)/shard_map/ppermute | solution.py:72
  136.9 14.5 %collective-permute-start.13 = (f32[32,256]{1,0:T(8,128)S(1)}, f32[32,256]{1,0:T(8,128)S(1)}, u32[]{:S(2)}, u32[]{:S(2)}) collective-permute-start(f32[32,256]{1,0:T(8,128)S(1)} %add.159), channel_id=1, source_target_pairs={{0,256},{8,264},{16,272},{24,280},{32,288},{40,296},{48,304},{56,3... | collective-permute-start | bytes 98312 | tf_op jit(solution)/shard_map/ppermute | solution.py:72
  151.4 23.0 %collective-permute-start.14 = (f32[32,256]{1,0:T(8,128)S(1)}, f32[32,256]{1,0:T(8,128)S(1)}, u32[]{:S(2)}, u32[]{:S(2)}) collective-permute-start(f32[32,256]{1,0:T(8,128)S(1)} %add.160), channel_id=1, source_target_pairs={{0,512},{8,520},{16,528},{24,536},{32,544},{40,552},{48,560},{56,5... | collective-permute-start | bytes 98312 | tf_op jit(solution)/shard_map/ppermute | solution.py:72

commit v3 on v2

--- a/solution.py
+++ b/solution.py
@@ -65,13 +65,36 @@
     return local_part + back
 
 
-def butterfly_sum(block, axis):
+def butterfly_sum(block, axis, spread):
     peers = lax.axis_size(axis)
+    me = lax.axis_index(axis)
+
+    def partner(stride):
+        return [(i, i ^ stride) for i in range(peers)]
+
+    rows = block
     stride = 1
+    while stride < spread:
+        half = rows.shape[0] // 2
+        upper = (me // stride) % 2 == 1
+        keep = jnp.where(upper, rows[half:], rows[:half])
+        send = jnp.where(upper, rows[:half], rows[half:])
+        rows = keep + lax.ppermute(send, axis, partner(stride))
+        stride *= 2
     while stride < peers:
-        block = block + lax.ppermute(block, axis, [(i, i ^ stride) for i in range(peers)])
+        rows = rows + lax.ppermute(rows, axis, partner(stride))
         stride *= 2
-    return block
+    stride = spread // 2
+    while stride >= 1:
+        upper = (me // stride) % 2 == 1
+        other = lax.ppermute(rows, axis, partner(stride))
+        rows = jnp.where(
+            upper,
+            jnp.concatenate([other, rows], axis=0),
+            jnp.concatenate([rows, other], axis=0),
+        )
+        stride //= 2
+    return rows
 
 
 def newton_schulz(margin):
@@ -105,7 +128,7 @@
     column_count = filtered.shape[0]
     every_column = lax.all_gather(filtered, "wave", axis=0, tiled=True)
     own_rows = jnp.dot(filtered, every_column.T, preferred_element_type=jnp.float32)
-    own_rows = butterfly_sum(own_rows, "space")
+    own_rows = butterfly_sum(own_rows, "space", 4)
     margin = lax.all_gather(own_rows, "wave", axis=0, tiled=True) / node_total
     rotation = newton_schulz(margin)
     own_rotation = lax.dynamic_slice_in_dim(

time: 202 us -> 213 us (1.054)
  starting transfers between devices: 57.8 us -> 62.4 us
  waiting for transfers between devices: 68.9 us -> 71.6 us
  blocking collectives: 42.5 us -> 45 us
    ppermute x7 -> x9, starting transfers between devices: 22.8 us -> 27.3 us  [the longest x5 19.7 us: butterfly_sum(): rows = rows + lax.ppermute(rows, axis, partner(stride))]
    ppermute x7 -> x9, waiting for transfers between devices: 44.7 us -> 47.4 us  [the longest x5 34.1 us: butterfly_sum(): rows = rows + lax.ppermute(rows, axis, partner(stride))]
    all_gather x1, blocking collectives: 20.3 us -> 22.9 us  [body(): margin = lax.all_gather(own_rows, 'wave', axis=0, tiled=True) / node_total]
  transfers between devices with their start and end apart: 15 -> 17, of which waited for: 14 -> 16; matrix products, arithmetic and copies ran while one was open for 5% -> 5% of each run, Pallas kernels for 0% -> 0%
where the time goes in v3:
time: 213 us; the launch traced here: 212 us
  waiting for transfers between devices  71.6 us (34%)
  starting transfers between devices  62.4 us (29%)
  blocking collectives  45 us (21%)
  matrix products  25.9 us (12%)
  local copies, waits for them, and re-layouts  3.04 us (1%)
  other arithmetic  2.68 us (1%)
    ppermute x8, starting transfers between devices, from_behind(): lax.ppermute(shard, axis, [(i, (i + by) % peers) for i in range(peers)])  35 us
    ppermute x5, waiting for transfers between devices, butterfly_sum(): rows = rows + lax.ppermute(rows, axis, partner(stride))  34.1 us
    ppermute x8, waiting for transfers between devices, from_behind(): lax.ppermute(shard, axis, [(i, (i + by) % peers) for i in range(peers)])  24.2 us
    all_gather x1, blocking collectives, body(): margin = lax.all_gather(own_rows, 'wave', axis=0, tiled=True) / node_total  22.9 us
    all_gather x1, blocking collectives, body(): every_column = lax.all_gather(filtered, 'wave', axis=0, tiled=True)  22.2 us
    ppermute x5, starting transfers between devices, butterfly_sum(): rows = rows + lax.ppermute(rows, axis, partner(stride))  19.7 us
    ppermute x2, waiting for transfers between devices, butterfly_sum(): other = lax.ppermute(rows, axis, partner(stride))  6.82 us
    ppermute x2, waiting for transfers between devices, butterfly_sum(): rows = keep + lax.ppermute(send, axis, partner(stride))  6.49 us
  transfers between devices with their start and end apart: 17, of which 16 were waited for; matrix products, arithmetic and copies ran while one was open for 5% of the time, Pallas kernels for 0%

profile of v3, /device:TPU:1, one launch (start us, length us, event | category | flops | bytes accessed | tf_op | source)
XLA Modules:
  0.0 212.0 jit_solution(11312543910592257926)
XLA Ops:
  1.5 21.4 %collective-permute-start = (bf16[32,128]{0,1:T(8,128)(2,1)S(1)}, bf16[32,128]{0,1:T(8,128)(2,1)S(1)}, u32[]{:S(2)}, u32[]{:S(2)}) collective-permute-start(bf16[32,128]{0,1:T(8,128)(2,1)S(1)} %fusion.42), channel_id=1, source_target_pairs={{0,1016},{8,0},{16,8},{24,16},{32,24},{40,32},{48,40},{56,48},{64,... | collective-permute-start | bytes 24584 | tf_op jit(solution)/shard_map/ppermute | solution.py:12
  29.9 1.9 collective-permute-start.1
  32.9 4.9 %collective-permute-done.1 = f32[32,128]{1,0:T(8,128)S(1)} collective-permute-done((f32[32,128]{1,0:T(8,128)S(1)}, f32[32,128]{1,0:T(8,128)S(1)}, u32[]{:S(2)}, u32[]{:S(2)}) %collective-permute-start.1) | collective-permute-done | bytes 16416 | tf_op jit(solution)/shard_map/ppermute | solution.py:12
  38.6 1.9 collective-permute-start.2
  45.6 1.9 collective-permute-start.3
  48.5 4.9 %collective-permute-done.3 = f32[32,128]{1,0:T(8,128)S(1)} collective-permute-done((f32[32,128]{1,0:T(8,128)S(1)}, f32[32,128]{1,0:T(8,128)S(1)}, u32[]{:S(2)}, u32[]{:S(2)}) %collective-permute-start.3) | collective-permute-done | bytes 16416 | tf_op jit(solution)/shard_map/ppermute | solution.py:12
  54.1 1.9 collective-permute-start.4
  61.2 1.9 collective-permute-start.5
  64.1 4.9 %collective-permute-done.5 = f32[32,128]{1,0:T(8,128)S(1)} collective-permute-done((f32[32,128]{1,0:T(8,128)S(1)}, f32[32,128]{1,0:T(8,128)S(1)}, u32[]{:S(2)}, u32[]{:S(2)}) %collective-permute-start.5) | collective-permute-done | bytes 16416 | tf_op jit(solution)/shard_map/ppermute | solution.py:12
  69.7 2.1 collective-permute-start.6
  77.0 1.9 collective-permute-start.7
  80.0 4.9 %collective-permute-done.7 = f32[32,128]{1,0:T(8,128)S(1)} collective-permute-done((f32[32,128]{1,0:T(8,128)S(1)}, f32[32,128]{1,0:T(8,128)S(1)}, u32[]{:S(2)}, u32[]{:S(2)}) %collective-permute-start.7) | collective-permute-done | bytes 16416 | tf_op jit(solution)/shard_map/ppermute | solution.py:12
  85.3 22.2 %all_gather.6 = bf16[256,1024]{1,0:T(8,128)(2,1)S(1)} all-gather(bf16[32,1024]{1,0:T(8,128)(2,1)S(1)} %fusion.81), channel_id=1, replica_groups=mesh['space'=128,'wave'=8] {'wave'}, dimensions={0}, use_global_device_ids=true | all-gather | bytes 589824 | tf_op jit(solution)/shard_map/all_gather | solution.py:129
  107.8 1.9 collective-permute-start.8
  109.7 2.5 %collective-permute-done.8 = f32[16,256]{1,0:T(8,128)S(1)} collective-permute-done((f32[16,256]{1,0:T(8,128)S(1)}, f32[16,256]{1,0:T(8,128)S(1)}, u32[]{:S(2)}, u32[]{:S(2)}) %collective-permute-start.8) | collective-permute-done | bytes 16416 | tf_op jit(solution)/shard_map/ppermute | solution.py:82
  112.3 1.9 collective-permute-start.9
  114.2 4.0 %collective-permute-done.9 = f32[8,256]{1,0:T(8,128)S(1)} collective-permute-done((f32[8,256]{1,0:T(8,128)S(1)}, f32[8,256]{1,0:T(8,128)S(1)}, u32[]{:S(2)}, u32[]{:S(2)}) %collective-permute-start.9) | collective-permute-done | bytes 8224 | tf_op jit(solution)/shard_map/ppermute | solution.py:82
  118.2 1.9 collective-permute-start.10
  120.1 2.5 %collective-permute-done.10 = f32[8,256]{1,0:T(8,128)S(1)} collective-permute-done((f32[8,256]{1,0:T(8,128)S(1)}, f32[8,256]{1,0:T(8,128)S(1)}, u32[]{:S(2)}, u32[]{:S(2)}) %collective-permute-start.10) | collective-permute-done | bytes 8224 | tf_op jit(solution)/shard_map/ppermute | solution.py:85
  122.6 1.9 collective-permute-start.11
  124.5 3.4 %collective-permute-done.11 = f32[8,256]{1,0:T(8,128)S(1)} collective-permute-done((f32[8,256]{1,0:T(8,128)S(1)}, f32[8,256]{1,0:T(8,128)S(1)}, u32[]{:S(2)}, u32[]{:S(2)}) %collective-permute-start.11) | collective-permute-done | bytes 8224 | tf_op jit(solution)/shard_map/ppermute | solution.py:85
  127.8 1.9 collective-permute-start.12
  129.8 6.4 %collective-permute-done.12 = f32[8,256]{1,0:T(8,128)S(1)} collective-permute-done((f32[8,256]{1,0:T(8,128)S(1)}, f32[8,256]{1,0:T(8,128)S(1)}, u32[]{:S(2)}, u32[]{:S(2)}) %collective-permute-start.12) | collective-permute-done | bytes 8224 | tf_op jit(solution)/shard_map/ppermute | solution.py:85
  136.1 1.9 collective-permute-start.13
  138.1 11.2 %collective-permute-done.13 = f32[8,256]{1,0:T(8,128)S(1)} collective-permute-done((f32[8,256]{1,0:T(8,128)S(1)}, f32[8,256]{1,0:T(8,128)S(1)}, u32[]{:S(2)}, u32[]{:S(2)}) %collective-permute-start.13) | collective-permute-done | bytes 8224 | tf_op jit(solution)/shard_map/ppermute | solution.py:85
  149.2 12.0 %collective-permute-start.14 = (f32[8,256]{1,0:T(8,128)S(1)}, f32[8,256]{1,0:T(8,128)S(1)}, u32[]{:S(2)}, u32[]{:S(2)}) collective-permute-start(f32[8,256]{1,0:T(8,128)S(1)} %add.173), channel_id=1, source_target_pairs={{0,512},{8,520},{16,528},{24,536},{32,544},{40,552},{48,560},{56,5... | collective-permute-start | bytes 24584 | tf_op jit(solution)/shard_map/ppermute | solution.py:85
  161.3 10.7 %collective-permute-done.14 = f32[8,256]{1,0:T(8,128)S(1)} collective-permute-done((f32[8,256]{1,0:T(8,128)S(1)}, f32[8,256]{1,0:T(8,128)S(1)}, u32[]{:S(2)}, u32[]{:S(2)}) %collective-permute-start.14) | collective-permute-done | bytes 8224 | tf_op jit(solution)/shard_map/ppermute | solution.py:85
  172.0 1.9 collective-permute-start.15
  173.9 4.3 %collective-permute-done.15 = f32[8,256]{1,0:T(8,128)S(1)} collective-permute-done((f32[8,256]{1,0:T(8,128)S(1)}, f32[8,256]{1,0:T(8,128)S(1)}, u32[]{:S(2)}, u32[]{:S(2)}) %collective-permute-start.15) | collective-permute-done | bytes 8224 | tf_op jit(solution)/shard_map/ppermute | solution.py:90
  178.1 1.9 collective-permute-start.16
  180.1 2.5 %collective-permute-done.16 = f32[16,256]{1,0:T(8,128)S(1)} collective-permute-done((f32[16,256]{1,0:T(8,128)S(1)}, f32[16,256]{1,0:T(8,128)S(1)}, u32[]{:S(2)}, u32[]{:S(2)}) %collective-permute-start.16) | collective-permute-done | bytes 16416 | tf_op jit(solution)/shard_map/ppermute | solution.py:90
  182.6 22.9 %all_gather.7 = f32[256,256]{1,0:T(8,128)S(1)} all-gather(f32[32,256]{1,0:T(8,128)S(1)} %maximum_select_fusion), channel_id=1, replica_groups=mesh['space'=128,'wave'=8] {'wave'}, dimensions={0}, use_global_device_ids=true | all-gather | bytes 294912 | tf_op jit(solution)/shard_map/all_gather | solution.py:132
  (104 shorter events, 36.2 us)
Async XLA Ops:
  0.0 27.7 %copy-start = (bf16[2,729,729]{2,0,1:T(2,128)(2,1)S(1)}, bf16[2,729,729]{2,0,1:T(2,128)(2,1)}, u32[]{:S(2)}) copy-start(bf16[2,729,729]{2,0,1:T(2,128)(2,1)} %param.5) | copy-start | bytes 6377296
  0.0 25.1 %copy-start.6 = (bf16[32,1024]{1,0:T(8,128)(2,1)S(1)}, bf16[32,1024]{1,0:T(8,128)(2,1)}, u32[]{:S(2)}) copy-start(bf16[32,1024]{1,0:T(8,128)(2,1)} %param.4) | copy-start | bytes 196612
  1.5 24.9 %collective-permute-start = (bf16[32,128]{0,1:T(8,128)(2,1)S(1)}, bf16[32,128]{0,1:T(8,128)(2,1)S(1)}, u32[]{:S(2)}, u32[]{:S(2)}) collective-permute-start(bf16[32,128]{0,1:T(8,128)(2,1)S(1)} %fusion.42), channel_id=1, source_target_pairs={{0,1016},{8,0},{16,8},{24,16},{32,24},{40,32},{48,40},{56,48},{64,... | collective-permute-start | bytes 24584 | tf_op jit(solution)/shard_map/ppermute | solution.py:12
  25.1 1.2 copy-start.1
  28.6 3.3 %copy-start.2 = (pred[1458,1152]{1,0:T(8,128)(4,1)S(1)}, pred[1458,1152]{1,0:T(8,128)(4,1)}, u32[]{:S(2)}) copy-start(pred[1458,1152]{1,0:T(8,128)(4,1)} %copy-done.1) | copy-start | bytes 5038852
  29.9 7.8 %copy-start.7 = (s32[128]{0:T(128)S(1)}, s32[128]{0:T(128)}, u32[]{:S(2)}) copy-start(s32[128]{0:T(128)} %param.7) | copy-start | bytes 1540
  29.9 7.8 %collective-permute-start.1 = (f32[32,128]{1,0:T(8,128)S(1)}, f32[32,128]{1,0:T(8,128)S(1)}, u32[]{:S(2)}, u32[]{:S(2)}) collective-permute-start(f32[32,128]{1,0:T(8,128)S(1)} %slice_add_fusion.22), channel_id=1, source_target_pairs={{0,8},{8,16},{16,24},{24,32},{32,40},{40,48},{48,56},{56,64},{64,7... | collective-permute-start | bytes 49160 | tf_op jit(solution)/shard_map/ppermute | solution.py:12
  38.6 4.4 %collective-permute-start.2 = (bf16[32,128]{1,0:T(8,128)(2,1)S(1)}, bf16[32,128]{1,0:T(8,128)(2,1)S(1)}, u32[]{:S(2)}, u32[]{:S(2)}) collective-permute-start(bf16[32,128]{1,0:T(8,128)(2,1)S(1)} %fusion.43), channel_id=1, source_target_pairs={{0,1016},{8,0},{16,8},{24,16},{32,24},{40,32},{48,40},{56,48},{64,... | collective-permute-start | bytes 24584 | tf_op jit(solution)/shard_map/ppermute | solution.py:12
  44.2 3.3 %copy-start.3 = (pred[1458,1152]{1,0:T(8,128)(4,1)S(1)}, pred[1458,1152]{1,0:T(8,128)(4,1)}, u32[]{:S(2)}) copy-start(pred[1458,1152]{1,0:T(8,128)(4,1)} %copy-done.1) | copy-start | bytes 5038852
  45.6 7.8 %collective-permute-start.3 = (f32[32,128]{1,0:T(8,128)S(1)}, f32[32,128]{1,0:T(8,128)S(1)}, u32[]{:S(2)}, u32[]{:S(2)}) collective-permute-start(f32[32,128]{1,0:T(8,128)S(1)} %slice_add_fusion.20), channel_id=1, source_target_pairs={{0,8},{8,16},{16,24},{24,32},{32,40},{40,48},{48,56},{56,64},{64,7... | collective-permute-start | bytes 49160 | tf_op jit(solution)/shard_map/ppermute | solution.py:12
  54.1 4.4 %collective-permute-start.4 = (bf16[32,128]{1,0:T(8,128)(2,1)S(1)}, bf16[32,128]{1,0:T(8,128)(2,1)S(1)}, u32[]{:S(2)}, u32[]{:S(2)}) collective-permute-start(bf16[32,128]{1,0:T(8,128)(2,1)S(1)} %fusion.46), channel_id=1, source_target_pairs={{0,1016},{8,0},{16,8},{24,16},{32,24},{40,32},{48,40},{56,48},{64,... | collective-permute-start | bytes 24584 | tf_op jit(solution)/shard_map/ppermute | solution.py:12
  59.8 3.3 %copy-start.4 = (pred[1458,1152]{1,0:T(8,128)(4,1)S(1)}, pred[1458,1152]{1,0:T(8,128)(4,1)}, u32[]{:S(2)}) copy-start(pred[1458,1152]{1,0:T(8,128)(4,1)} %copy-done.1) | copy-start | bytes 5038852
  61.2 7.8 %collective-permute-start.5 = (f32[32,128]{1,0:T(8,128)S(1)}, f32[32,128]{1,0:T(8,128)S(1)}, u32[]{:S(2)}, u32[]{:S(2)}) collective-permute-start(f32[32,128]{1,0:T(8,128)S(1)} %slice_add_fusion.18), channel_id=1, source_target_pairs={{0,8},{8,16},{16,24},{24,32},{32,40},{40,48},{48,56},{56,64},{64,7... | collective-permute-start | bytes 49160 | tf_op jit(solution)/shard_map/ppermute | solution.py:12
  69.7 4.7 %collective-permute-start.6 = (bf16[32,128]{1,0:T(8,128)(2,1)S(1)}, bf16[32,128]{1,0:T(8,128)(2,1)S(1)}, u32[]{:S(2)}, u32[]{:S(2)}) collective-permute-start(bf16[32,128]{1,0:T(8,128)(2,1)S(1)} %fusion.49), channel_id=1, source_target_pairs={{0,1016},{8,0},{16,8},{24,16},{32,24},{40,32},{48,40},{56,48},{64,... | collective-permute-start | bytes 24584 | tf_op jit(solution)/shard_map/ppermute | solution.py:12
  75.7 3.3 %copy-start.5 = (pred[1458,1152]{1,0:T(8,128)(4,1)S(1)}, pred[1458,1152]{1,0:T(8,128)(4,1)}, u32[]{:S(2)}) copy-start(pred[1458,1152]{1,0:T(8,128)(4,1)} %copy-done.1) | copy-start | bytes 5038852
  77.0 7.8 %collective-permute-start.7 = (f32[32,128]{1,0:T(8,128)S(1)}, f32[32,128]{1,0:T(8,128)S(1)}, u32[]{:S(2)}, u32[]{:S(2)}) collective-permute-start(f32[32,128]{1,0:T(8,128)S(1)} %slice_add_fusion.16), channel_id=1, source_target_pairs={{0,8},{8,16},{16,24},{24,32},{32,40},{40,48},{48,56},{56,64},{64,7... | collective-permute-start | bytes 49160 | tf_op jit(solution)/shard_map/ppermute | solution.py:12
  107.8 4.5 %collective-permute-start.8 = (f32[16,256]{1,0:T(8,128)S(1)}, f32[16,256]{1,0:T(8,128)S(1)}, u32[]{:S(2)}, u32[]{:S(2)}) collective-permute-start(f32[16,256]{1,0:T(8,128)S(1)} %slice_select_fusion), channel_id=1, source_target_pairs={{0,8},{8,0},{16,24},{24,16},{32,40},{40,32},{48,56},{56,48},{64,72... | collective-permute-start | bytes 49160 | tf_op jit(solution)/shard_map/ppermute | solution.py:82
  112.3 5.9 %collective-permute-start.9 = (f32[8,256]{1,0:T(8,128)S(1)}, f32[8,256]{1,0:T(8,128)S(1)}, u32[]{:S(2)}, u32[]{:S(2)}) collective-permute-start(f32[8,256]{1,0:T(8,128)S(1)} %slice_select_fusion.1), channel_id=1, source_target_pairs={{0,16},{8,24},{16,0},{24,8},{32,48},{40,56},{48,32},{56,40},{64,80... | collective-permute-start | bytes 24584 | tf_op jit(solution)/shard_map/ppermute | solution.py:82
  118.2 4.4 %collective-permute-start.10 = (f32[8,256]{1,0:T(8,128)S(1)}, f32[8,256]{1,0:T(8,128)S(1)}, u32[]{:S(2)}, u32[]{:S(2)}) collective-permute-start(f32[8,256]{1,0:T(8,128)S(1)} %select_add_fusion.1), channel_id=1, source_target_pairs={{0,32},{8,40},{16,48},{24,56},{32,0},{40,8},{48,16},{56,24},{64,96... | collective-permute-start | bytes 24584 | tf_op jit(solution)/shard_map/ppermute | solution.py:85
  122.6 5.3 %collective-permute-start.11 = (f32[8,256]{1,0:T(8,128)S(1)}, f32[8,256]{1,0:T(8,128)S(1)}, u32[]{:S(2)}, u32[]{:S(2)}) collective-permute-start(f32[8,256]{1,0:T(8,128)S(1)} %add.170), channel_id=1, source_target_pairs={{0,64},{8,72},{16,80},{24,88},{32,96},{40,104},{48,112},{56,120},{... | collective-permute-start | bytes 24584 | tf_op jit(solution)/shard_map/ppermute | solution.py:85
  127.8 8.3 %collective-permute-start.12 = (f32[8,256]{1,0:T(8,128)S(1)}, f32[8,256]{1,0:T(8,128)S(1)}, u32[]{:S(2)}, u32[]{:S(2)}) collective-permute-start(f32[8,256]{1,0:T(8,128)S(1)} %add.171), channel_id=1, source_target_pairs={{0,128},{8,136},{16,144},{24,152},{32,160},{40,168},{48,176},{56,1... | collective-permute-start | bytes 24584 | tf_op jit(solution)/shard_map/ppermute | solution.py:85
  136.1 13.1 %collective-permute-start.13 = (f32[8,256]{1,0:T(8,128)S(1)}, f32[8,256]{1,0:T(8,128)S(1)}, u32[]{:S(2)}, u32[]{:S(2)}) collective-permute-start(f32[8,256]{1,0:T(8,128)S(1)} %add.172), channel_id=1, source_target_pairs={{0,256},{8,264},{16,272},{24,280},{32,288},{40,296},{48,304},{56,3... | collective-permute-start | bytes 24584 | tf_op jit(solution)/shard_map/ppermute | solution.py:85
  149.2 22.7 %collective-permute-start.14 = (f32[8,256]{1,0:T(8,128)S(1)}, f32[8,256]{1,0:T(8,128)S(1)}, u32[]{:S(2)}, u32[]{:S(2)}) collective-permute-start(f32[8,256]{1,0:T(8,128)S(1)} %add.173), channel_id=1, source_target_pairs={{0,512},{8,520},{16,528},{24,536},{32,544},{40,552},{48,560},{56,5... | collective-permute-start | bytes 24584 | tf_op jit(solution)/shard_map/ppermute | solution.py:85
  172.0 6.2 %collective-permute-start.15 = (f32[8,256]{1,0:T(8,128)S(1)}, f32[8,256]{1,0:T(8,128)S(1)}, u32[]{:S(2)}, u32[]{:S(2)}) collective-permute-start(f32[8,256]{1,0:T(8,128)S(1)} %add.174), channel_id=1, source_target_pairs={{0,16},{8,24},{16,0},{24,8},{32,48},{40,56},{48,32},{56,40},{64,80... | collective-permute-start | bytes 24584 | tf_op jit(solution)/shard_map/ppermute | solution.py:90
  178.1 4.5 %collective-permute-start.16 = (f32[16,256]{1,0:T(8,128)S(1)}, f32[16,256]{1,0:T(8,128)S(1)}, u32[]{:S(2)}, u32[]{:S(2)}) collective-permute-start(f32[16,256]{1,0:T(8,128)S(1)} %maximum_select_fusion.1), channel_id=1, source_target_pairs={{0,8},{8,0},{16,24},{24,16},{32,40},{40,32},{48,56},{56,48},{64,72... | collective-permute-start | bytes 49160 | tf_op jit(solution)/shard_map/ppermute | solution.py:90

commit v4 on v2

--- a/solution.py
+++ b/solution.py
@@ -35,32 +35,62 @@
     return pick, owner
 
 
-def apply_filter(wave_block, cell_matrices, pick, owner):
+def plane_coupling(cell_matrices, pick, node_count):
+    cell_count, cell_nodes, _ = cell_matrices.shape
+    plane_pick = pick[:, node_count:]
+    per_cell = plane_pick.reshape(cell_count, cell_nodes, plane_pick.shape[1])
+    halfway = jnp.einsum("clq,clm->qcm", per_cell, cell_matrices, preferred_element_type=jnp.float32)
+    halfway = halfway.reshape(plane_pick.shape[1], cell_count * cell_nodes)
+    coupling = sum_three(jnp.dot(split_three(halfway), plane_pick, preferred_element_type=jnp.float32))
+    return from_behind(split_three(coupling), "space", 1)
+
+
+def apply_filter(wave_block, cell_matrices, pick, owner, coupling_below):
     column_count = wave_block.shape[0]
     node_count = wave_block.shape[1]
     cell_count, cell_nodes, _ = cell_matrices.shape
+    plane_count = owner.shape[1]
+    contract_nodes = (((1,), (1,)), ((), ()))
     own_plane = jnp.dot(wave_block, owner, preferred_element_type=jnp.float32).astype(jnp.bfloat16)
     upper_plane = from_behind(own_plane, "space", -1)
-    contract_nodes = (((1,), (1,)), ((), ()))
-    gathered = lax.dot_general(
+    from_own = lax.dot_general(
         wave_block, pick[:, :node_count], contract_nodes, preferred_element_type=jnp.float32
-    ) + lax.dot_general(
+    ).astype(jnp.bfloat16)
+    own_products = jnp.einsum(
+        "bcn,cnm->bcm",
+        from_own.reshape(column_count, cell_count, cell_nodes),
+        cell_matrices,
+        preferred_element_type=jnp.float32,
+    )
+    sent_up = sum_three(
+        jnp.dot(
+            split_three(own_products.reshape(column_count, cell_count * cell_nodes)),
+            pick[:, node_count:],
+            preferred_element_type=jnp.float32,
+        )
+    )
+    received = from_behind(sent_up, "space", 1)
+    from_upper = lax.dot_general(
         upper_plane, pick[:, node_count:], contract_nodes, preferred_element_type=jnp.float32
+    ).astype(jnp.bfloat16)
+    products = jnp.einsum(
+        "bcn,cnm->bcm",
+        (from_own + from_upper).reshape(column_count, cell_count, cell_nodes),
+        cell_matrices,
+        preferred_element_type=jnp.float32,
     )
-    gathered = gathered.astype(jnp.bfloat16).reshape(column_count, cell_count, cell_nodes)
-    products = jnp.einsum(
-        "bcn,cnm->bcm", gathered, cell_matrices, preferred_element_type=jnp.float32
+    local_part = sum_three(
+        jnp.dot(
+            split_three(products.reshape(column_count, cell_count * cell_nodes)),
+            pick[:, :node_count],
+            preferred_element_type=jnp.float32,
+        )
     )
-    stacked = split_three(products.reshape(column_count, cell_count * cell_nodes))
-    plane_part = sum_three(
-        jnp.dot(stacked, pick[:, node_count:], preferred_element_type=jnp.float32)
-    )
-    returned = from_behind(plane_part, "space", 1)
-    local_part = sum_three(
-        jnp.dot(stacked, pick[:, :node_count], preferred_element_type=jnp.float32)
-    )
+    pieces = coupling_below.reshape(3, plane_count, plane_count)
+    coupled = jnp.einsum("bq,kqp->kbp", own_plane, pieces, preferred_element_type=jnp.float32)
+    plane_total = received + ((coupled[0] + coupled[1]) + coupled[2])
     back = sum_three(
-        lax.dot_general(split_three(returned), owner, contract_nodes, preferred_element_type=jnp.float32)
+        lax.dot_general(split_three(plane_total), owner, contract_nodes, preferred_element_type=jnp.float32)
     )
     return local_part + back
 
@@ -92,11 +122,13 @@
 
 def body(wavefunctions, filter_cells, connectivity, owner_list):
     pick, owner = selectors(connectivity, owner_list, wavefunctions.shape[1])
+    coupling_below = plane_coupling(filter_cells, pick, wavefunctions.shape[1])
     previous = wavefunctions.astype(jnp.float32)
-    current = apply_filter(wavefunctions, filter_cells, pick, owner)
+    current = apply_filter(wavefunctions, filter_cells, pick, owner, coupling_below)
     for degree_step in range(DEGREE - 1):
         following = (
-            2.0 * apply_filter(current.astype(jnp.bfloat16), filter_cells, pick, owner)
+            2.0
+            * apply_filter(current.astype(jnp.bfloat16), filter_cells, pick, owner, coupling_below)
             - previous
         )
         previous, current = (current, following)

time: 202 us -> 211 us (1.045)
  waiting for transfers between devices: 68.9 us -> 45.3 us
  starting transfers between devices: 57.8 us -> 75.2 us
  matrix products: 25 us -> 38 us
  local copies, waits for them, and re-layouts: 2.99 us -> 8.7 us
  blocking collectives: 42.5 us -> 37.9 us
    ppermute x8 -> x9, waiting for transfers between devices: 24.2 us -> 4.4 us  [from_behind(): lax.ppermute(shard, axis, [(i, (i + by) % peers) for i in range(peers)])]
    ppermute x8 -> x9, starting transfers between devices: 35 us -> 48.2 us  [from_behind(): lax.ppermute(shard, axis, [(i, (i + by) % peers) for i in range(peers)])]
    dot_general x16 -> x26, matrix products: 12.4 us -> 22.8 us  [the longest x4 9.82 us: apply_filter(): jnp.dot(split_three(products.reshape(column_count, cell_count * cell_node...]
    all_gather x1, blocking collectives: 22.2 us -> 17.3 us  [body(): every_column = lax.all_gather(filtered, 'wave', axis=0, tiled=True)]
    ppermute x7, starting transfers between devices: 22.8 us -> 27.1 us  [butterfly_sum(): lax.ppermute(block, axis, [(i, i ^ stride) for i in range(peers)])]
    ppermute x7, waiting for transfers between devices: 44.7 us -> 41 us  [butterfly_sum(): lax.ppermute(block, axis, [(i, i ^ stride) for i in range(peers)])]
    dot_general x4, matrix products: 1.01 us -> 4.69 us  [apply_filter(): lax.dot_general(upper_plane, pick[:, node_count:], contract_nodes, prefer...]
    reshape x4 -> x14, local copies, waits for them, and re-layouts: 0.61 us -> 3.23 us  [the longest x1 1.17 us: plane_coupling(): halfway = halfway.reshape(plane_pick.shape[1], cell_count * cell_nodes)]
  transfers between devices with their start and end apart: 15 -> 16, of which waited for: 14 -> 11; matrix products, arithmetic and copies ran while one was open for 5% -> 14% of each run, Pallas kernels for 0% -> 0%
where the time goes in v4:
time: 211 us; the launch traced here: 210 us
  starting transfers between devices  75.2 us (36%)
  waiting for transfers between devices  45.3 us (21%)
  matrix products  38 us (18%)
  blocking collectives  37.9 us (18%)
  local copies, waits for them, and re-layouts  8.7 us (4%)
  other arithmetic  3.09 us (1%)
    ppermute x9, starting transfers between devices, from_behind(): lax.ppermute(shard, axis, [(i, (i + by) % peers) for i in range(peers)])  48.2 us
    ppermute x7, waiting for transfers between devices, butterfly_sum(): lax.ppermute(block, axis, [(i, i ^ stride) for i in range(peers)])  41 us
    ppermute x7, starting transfers between devices, butterfly_sum(): lax.ppermute(block, axis, [(i, i ^ stride) for i in range(peers)])  27.1 us
    all_gather x1, blocking collectives, body(): margin = lax.all_gather(own_rows, 'wave', axis=0, tiled=True) / node_total  20.6 us
    all_gather x1, blocking collectives, body(): every_column = lax.all_gather(filtered, 'wave', axis=0, tiled=True)  17.3 us
    dot_general x4, matrix products, apply_filter(): jnp.dot(split_three(products.reshape(column_count, cell_count * cell_node...  9.82 us
    dot_general x4, matrix products, apply_filter(): lax.dot_general(upper_plane, pick[:, node_count:], contract_nodes, prefer...  4.69 us
    dot_general x4, matrix products, apply_filter(): jnp.dot(split_three(own_products.reshape(column_count, cell_count * cell_...  4.67 us
  transfers between devices with their start and end apart: 16, of which 11 were waited for; matrix products, arithmetic and copies ran while one was open for 14% of the time, Pallas kernels for 0%

profile of v4, /device:TPU:1, one launch (start us, length us, event | category | flops | bytes accessed | tf_op | source)
XLA Modules:
  0.0 209.8 jit_solution(9086085470081105912)
XLA Ops:
  0.9 1.5 iota_compare_fusion
  3.8 1.9 convolution_bitcast_fusion
  8.9 4.0 %collective-permute-start.2 = (bf16[384,128]{1,0:T(8,128)(2,1)S(1)}, bf16[384,128]{1,0:T(8,128)(2,1)S(1)}, u32[]{:S(2)}, u32[]{:S(2)}) collective-permute-start(bf16[384,128]{1,0:T(8,128)(2,1)S(1)} %pad_maximum_fusion), channel_id=1, source_target_pairs={{0,8},{8,16},{16,24},{24,32},{32,40},{40,48},{48,56},{56,64},{64,7... | collective-permute-start | bytes 294920 | tf_op jit(solution)/shard_map/ppermute | solution.py:12
  13.2 19.4 %collective-permute-start = (bf16[32,128]{1,0:T(8,128)(2,1)S(1)}, bf16[32,128]{1,0:T(8,128)(2,1)S(1)}, u32[]{:S(2)}, u32[]{:S(2)}) collective-permute-start(bf16[32,128]{1,0:T(8,128)(2,1)S(1)} %bitcast.102), channel_id=1, source_target_pairs={{0,1016},{8,0},{16,8},{24,16},{32,24},{40,32},{48,40},{56,48},{64,... | collective-permute-start | bytes 24584 | tf_op jit(solution)/shard_map/ppermute | solution.py:12
  35.9 1.9 collective-permute-start.1
  40.1 2.5 %fusion.45 = f32[96,1024]{1,0:T(8,128)S(1)} fusion(bf16[32,1458]{1,0:T(8,128)(2,1)S(1)} %get-tuple-element.37, bf16[32,1458]{1,0:T(8,128)(2,1)S(1)} %get-tuple-element.38, bf16[32,1458]{1,0:T(8,128)(2,1)S(1)} %get-tuple-element.36, pred[1458,1152]{1,0:T(8,128)(4,1)} %copy-done.1), kind=kOutput, calls=%fused_computation.68 | convolution fusion | flops 287494272 | bytes 2172288 | tf_op jit(solution)/shard_map/dot_general | solution.py:83
  45.5 5.7 %collective-permute-start.3 = (bf16[32,128]{1,0:T(8,128)(2,1)S(1)}, bf16[32,128]{1,0:T(8,128)(2,1)S(1)}, u32[]{:S(2)}, u32[]{:S(2)}) collective-permute-start(bf16[32,128]{1,0:T(8,128)(2,1)S(1)} %fusion.34), channel_id=1, source_target_pairs={{0,1016},{8,0},{16,8},{24,16},{32,24},{40,32},{48,40},{56,48},{64,... | collective-permute-start | bytes 24584 | tf_op jit(solution)/shard_map/ppermute | solution.py:12
  53.6 2.1 %collective-permute-start.4 = (f32[32,128]{1,0:T(8,128)S(1)}, f32[32,128]{1,0:T(8,128)S(1)}, u32[]{:S(2)}, u32[]{:S(2)}) collective-permute-start(f32[32,128]{1,0:T(8,128)S(1)} %slice_add_fusion.28), channel_id=1, source_target_pairs={{0,8},{8,16},{16,24},{24,32},{32,40},{40,48},{48,56},{56,64},{64,7... | collective-permute-start | bytes 49160 | tf_op jit(solution)/shard_map/ppermute | solution.py:12
  57.9 2.5 %fusion.57 = f32[96,1024]{1,0:T(8,128)S(1)} fusion(bf16[32,1458]{1,0:T(8,128)(2,1)S(1)} %get-tuple-element.31, bf16[32,1458]{1,0:T(8,128)(2,1)S(1)} %get-tuple-element.32, bf16[32,1458]{1,0:T(8,128)(2,1)S(1)} %get-tuple-element.30, pred[1458,1152]{1,0:T(8,128)(4,1)} %copy-done.1), kind=kOutput, calls=%fused_computation.80 | convolution fusion | flops 287494272 | bytes 2172288 | tf_op jit(solution)/shard_map/dot_general | solution.py:83
  63.2 5.7 %collective-permute-start.5 = (bf16[32,128]{1,0:T(8,128)(2,1)S(1)}, bf16[32,128]{1,0:T(8,128)(2,1)S(1)}, u32[]{:S(2)}, u32[]{:S(2)}) collective-permute-start(bf16[32,128]{1,0:T(8,128)(2,1)S(1)} %fusion.37), channel_id=1, source_target_pairs={{0,1016},{8,0},{16,8},{24,16},{32,24},{40,32},{48,40},{56,48},{64,... | collective-permute-start | bytes 24584 | tf_op jit(solution)/shard_map/ppermute | solution.py:12
  71.3 1.9 collective-permute-start.6
  75.5 2.5 %fusion.69 = f32[96,1024]{1,0:T(8,128)S(1)} fusion(bf16[32,1458]{1,0:T(8,128)(2,1)S(1)} %get-tuple-element.25, bf16[32,1458]{1,0:T(8,128)(2,1)S(1)} %get-tuple-element.26, bf16[32,1458]{1,0:T(8,128)(2,1)S(1)} %get-tuple-element.24, pred[1458,1152]{1,0:T(8,128)(4,1)} %copy-done.1), kind=kOutput, calls=%fused_computation.92 | convolution fusion | flops 287494272 | bytes 2172288 | tf_op jit(solution)/shard_map/dot_general | solution.py:83
  80.9 5.5 %collective-permute-start.7 = (bf16[32,128]{1,0:T(8,128)(2,1)S(1)}, bf16[32,128]{1,0:T(8,128)(2,1)S(1)}, u32[]{:S(2)}, u32[]{:S(2)}) collective-permute-start(bf16[32,128]{1,0:T(8,128)(2,1)S(1)} %fusion.40), channel_id=1, source_target_pairs={{0,1016},{8,0},{16,8},{24,16},{32,24},{40,32},{48,40},{56,48},{64,... | collective-permute-start | bytes 24584 | tf_op jit(solution)/shard_map/ppermute | solution.py:12
  88.8 1.9 collective-permute-start.8
  93.0 2.4 %fusion.81 = f32[96,1024]{1,0:T(8,128)S(1)} fusion(bf16[32,1458]{1,0:T(8,128)(2,1)S(1)} %get-tuple-element.19, bf16[32,1458]{1,0:T(8,128)(2,1)S(1)} %get-tuple-element.20, bf16[32,1458]{1,0:T(8,128)(2,1)S(1)} %get-tuple-element.18, pred[1458,1152]{1,0:T(8,128)(4,1)} %copy-done.1), kind=kOutput, calls=%fused_computation.104 | convolution fusion | flops 287494272 | bytes 2172288 | tf_op jit(solution)/shard_map/dot_general | solution.py:83
  95.4 1.3 collective-permute-done.8
  97.1 17.3 %all_gather.6 = bf16[256,1024]{1,0:T(8,128)(2,1)S(1)} all-gather(bf16[32,1024]{1,0:T(8,128)(2,1)S(1)} %fusion.139), channel_id=1, replica_groups=mesh['space'=128,'wave'=8] {'wave'}, dimensions={0}, use_global_device_ids=true | all-gather | bytes 589824 | tf_op jit(solution)/shard_map/all_gather | solution.py:138
  114.6 1.9 collective-permute-start.9
  116.6 2.7 %collective-permute-done.9 = f32[32,256]{1,0:T(8,128)S(1)} collective-permute-done((f32[32,256]{1,0:T(8,128)S(1)}, f32[32,256]{1,0:T(8,128)S(1)}, u32[]{:S(2)}, u32[]{:S(2)}) %collective-permute-start.9) | collective-permute-done | bytes 32800 | tf_op jit(solution)/shard_map/ppermute | solution.py:102
  119.3 1.9 collective-permute-start.10
  121.2 4.2 %collective-permute-done.10 = f32[32,256]{1,0:T(8,128)S(1)} collective-permute-done((f32[32,256]{1,0:T(8,128)S(1)}, f32[32,256]{1,0:T(8,128)S(1)}, u32[]{:S(2)}, u32[]{:S(2)}) %collective-permute-start.10) | collective-permute-done | bytes 32800 | tf_op jit(solution)/shard_map/ppermute | solution.py:102
  125.5 1.9 collective-permute-start.11
  127.4 2.7 %collective-permute-done.11 = f32[32,256]{1,0:T(8,128)S(1)} collective-permute-done((f32[32,256]{1,0:T(8,128)S(1)}, f32[32,256]{1,0:T(8,128)S(1)}, u32[]{:S(2)}, u32[]{:S(2)}) %collective-permute-start.11) | collective-permute-done | bytes 32800 | tf_op jit(solution)/shard_map/ppermute | solution.py:102
  130.1 1.9 collective-permute-start.12
  132.0 3.7 %collective-permute-done.12 = f32[32,256]{1,0:T(8,128)S(1)} collective-permute-done((f32[32,256]{1,0:T(8,128)S(1)}, f32[32,256]{1,0:T(8,128)S(1)}, u32[]{:S(2)}, u32[]{:S(2)}) %collective-permute-start.12) | collective-permute-done | bytes 32800 | tf_op jit(solution)/shard_map/ppermute | solution.py:102
  135.7 1.9 collective-permute-start.13
  137.7 7.1 %collective-permute-done.13 = f32[32,256]{1,0:T(8,128)S(1)} collective-permute-done((f32[32,256]{1,0:T(8,128)S(1)}, f32[32,256]{1,0:T(8,128)S(1)}, u32[]{:S(2)}, u32[]{:S(2)}) %collective-permute-start.13) | collective-permute-done | bytes 32800 | tf_op jit(solution)/shard_map/ppermute | solution.py:102
  144.7 3.8 %collective-permute-start.14 = (f32[32,256]{1,0:T(8,128)S(1)}, f32[32,256]{1,0:T(8,128)S(1)}, u32[]{:S(2)}, u32[]{:S(2)}) collective-permute-start(f32[32,256]{1,0:T(8,128)S(1)} %add.235), channel_id=1, source_target_pairs={{0,256},{8,264},{16,272},{24,280},{32,288},{40,296},{48,304},{56,3... | collective-permute-start | bytes 98312 | tf_op jit(solution)/shard_map/ppermute | solution.py:102
  148.6 10.9 %collective-permute-done.14 = f32[32,256]{1,0:T(8,128)S(1)} collective-permute-done((f32[32,256]{1,0:T(8,128)S(1)}, f32[32,256]{1,0:T(8,128)S(1)}, u32[]{:S(2)}, u32[]{:S(2)}) %collective-permute-start.14) | collective-permute-done | bytes 32800 | tf_op jit(solution)/shard_map/ppermute | solution.py:102
  159.5 13.7 %collective-permute-start.15 = (f32[32,256]{1,0:T(8,128)S(1)}, f32[32,256]{1,0:T(8,128)S(1)}, u32[]{:S(2)}, u32[]{:S(2)}) collective-permute-start(f32[32,256]{1,0:T(8,128)S(1)} %add.236), channel_id=1, source_target_pairs={{0,512},{8,520},{16,528},{24,536},{32,544},{40,552},{48,560},{56,5... | collective-permute-start | bytes 98312 | tf_op jit(solution)/shard_map/ppermute | solution.py:102
  173.2 9.5 %collective-permute-done.15 = f32[32,256]{1,0:T(8,128)S(1)} collective-permute-done((f32[32,256]{1,0:T(8,128)S(1)}, f32[32,256]{1,0:T(8,128)S(1)}, u32[]{:S(2)}, u32[]{:S(2)}) %collective-permute-start.15) | collective-permute-done | bytes 32800 | tf_op jit(solution)/shard_map/ppermute | solution.py:102
  182.8 20.6 %all_gather.7 = f32[256,256]{1,0:T(8,128)S(1)} all-gather(f32[32,256]{1,0:T(8,128)S(1)} %add.237), channel_id=1, replica_groups=mesh['space'=128,'wave'=8] {'wave'}, dimensions={0}, use_global_device_ids=true | all-gather | bytes 294912 | tf_op jit(solution)/shard_map/all_gather | solution.py:141
  (135 shorter events, 39.7 us)
Async XLA Ops:
  0.0 3.8 %copy-start = (bf16[2,729,729]{2,0,1:T(2,128)(2,1)S(1)}, bf16[2,729,729]{2,0,1:T(2,128)(2,1)}, u32[]{:S(2)}) copy-start(bf16[2,729,729]{2,0,1:T(2,128)(2,1)} %param.5) | copy-start | bytes 6377296
  2.4 1.2 copy-start.1
  6.9 1.4 copy-start.2
  8.3 4.6 %copy-start.6 = (bf16[32,1024]{1,0:T(8,128)(2,1)S(1)}, bf16[32,1024]{1,0:T(8,128)(2,1)}, u32[]{:S(2)}) copy-start(bf16[32,1024]{1,0:T(8,128)(2,1)} %param.4) | copy-start | bytes 196612
  8.3 4.6 %copy-start.7 = (s32[128]{0:T(128)S(1)}, s32[128]{0:T(128)}, u32[]{:S(2)}) copy-start(s32[128]{0:T(128)} %param.7) | copy-start | bytes 1540
  8.9 33.6 %collective-permute-start.2 = (bf16[384,128]{1,0:T(8,128)(2,1)S(1)}, bf16[384,128]{1,0:T(8,128)(2,1)S(1)}, u32[]{:S(2)}, u32[]{:S(2)}) collective-permute-start(bf16[384,128]{1,0:T(8,128)(2,1)S(1)} %pad_maximum_fusion), channel_id=1, source_target_pairs={{0,8},{8,16},{16,24},{24,32},{32,40},{40,48},{48,56},{56,64},{64,7... | collective-permute-start | bytes 294920 | tf_op jit(solution)/shard_map/ppermute | solution.py:12
  13.2 24.6 %collective-permute-start = (bf16[32,128]{1,0:T(8,128)(2,1)S(1)}, bf16[32,128]{1,0:T(8,128)(2,1)S(1)}, u32[]{:S(2)}, u32[]{:S(2)}) collective-permute-start(bf16[32,128]{1,0:T(8,128)(2,1)S(1)} %bitcast.102), channel_id=1, source_target_pairs={{0,1016},{8,0},{16,8},{24,16},{32,24},{40,32},{48,40},{56,48},{64,... | collective-permute-start | bytes 24584 | tf_op jit(solution)/shard_map/ppermute | solution.py:12
  35.9 7.8 %collective-permute-start.1 = (f32[32,128]{1,0:T(8,128)S(1)}, f32[32,128]{1,0:T(8,128)S(1)}, u32[]{:S(2)}, u32[]{:S(2)}) collective-permute-start(f32[32,128]{1,0:T(8,128)S(1)} %slice_add_fusion.32), channel_id=1, source_target_pairs={{0,8},{8,16},{16,24},{24,32},{32,40},{40,48},{48,56},{56,64},{64,7... | collective-permute-start | bytes 49160 | tf_op jit(solution)/shard_map/ppermute | solution.py:12
  40.0 4.1 %copy-start.3 = (pred[1458,1152]{1,0:T(8,128)(4,1)S(1)}, pred[1458,1152]{1,0:T(8,128)(4,1)}, u32[]{:S(2)}) copy-start(pred[1458,1152]{1,0:T(8,128)(4,1)} %copy-done.1) | copy-start | bytes 5038852
  45.5 10.2 %collective-permute-start.3 = (bf16[32,128]{1,0:T(8,128)(2,1)S(1)}, bf16[32,128]{1,0:T(8,128)(2,1)S(1)}, u32[]{:S(2)}, u32[]{:S(2)}) collective-permute-start(bf16[32,128]{1,0:T(8,128)(2,1)S(1)} %fusion.34), channel_id=1, source_target_pairs={{0,1016},{8,0},{16,8},{24,16},{32,24},{40,32},{48,40},{56,48},{64,... | collective-permute-start | bytes 24584 | tf_op jit(solution)/shard_map/ppermute | solution.py:12
  53.6 7.8 %collective-permute-start.4 = (f32[32,128]{1,0:T(8,128)S(1)}, f32[32,128]{1,0:T(8,128)S(1)}, u32[]{:S(2)}, u32[]{:S(2)}) collective-permute-start(f32[32,128]{1,0:T(8,128)S(1)} %slice_add_fusion.28), channel_id=1, source_target_pairs={{0,8},{8,16},{16,24},{24,32},{32,40},{40,48},{48,56},{56,64},{64,7... | collective-permute-start | bytes 49160 | tf_op jit(solution)/shard_map/ppermute | solution.py:12
  57.9 3.9 %copy-start.4 = (pred[1458,1152]{1,0:T(8,128)(4,1)S(1)}, pred[1458,1152]{1,0:T(8,128)(4,1)}, u32[]{:S(2)}) copy-start(pred[1458,1152]{1,0:T(8,128)(4,1)} %copy-done.1) | copy-start | bytes 5038852
  63.2 10.0 %collective-permute-start.5 = (bf16[32,128]{1,0:T(8,128)(2,1)S(1)}, bf16[32,128]{1,0:T(8,128)(2,1)S(1)}, u32[]{:S(2)}, u32[]{:S(2)}) collective-permute-start(bf16[32,128]{1,0:T(8,128)(2,1)S(1)} %fusion.37), channel_id=1, source_target_pairs={{0,1016},{8,0},{16,8},{24,16},{32,24},{40,32},{48,40},{56,48},{64,... | collective-permute-start | bytes 24584 | tf_op jit(solution)/shard_map/ppermute | solution.py:12
  71.3 7.8 %collective-permute-start.6 = (f32[32,128]{1,0:T(8,128)S(1)}, f32[32,128]{1,0:T(8,128)S(1)}, u32[]{:S(2)}, u32[]{:S(2)}) collective-permute-start(f32[32,128]{1,0:T(8,128)S(1)} %slice_add_fusion.24), channel_id=1, source_target_pairs={{0,8},{8,16},{16,24},{24,32},{32,40},{40,48},{48,56},{56,64},{64,7... | collective-permute-start | bytes 49160 | tf_op jit(solution)/shard_map/ppermute | solution.py:12
  75.5 4.1 %copy-start.5 = (pred[1458,1152]{1,0:T(8,128)(4,1)S(1)}, pred[1458,1152]{1,0:T(8,128)(4,1)}, u32[]{:S(2)}) copy-start(pred[1458,1152]{1,0:T(8,128)(4,1)} %copy-done.1) | copy-start | bytes 5038852
  80.9 9.9 %collective-permute-start.7 = (bf16[32,128]{1,0:T(8,128)(2,1)S(1)}, bf16[32,128]{1,0:T(8,128)(2,1)S(1)}, u32[]{:S(2)}, u32[]{:S(2)}) collective-permute-start(bf16[32,128]{1,0:T(8,128)(2,1)S(1)} %fusion.40), channel_id=1, source_target_pairs={{0,1016},{8,0},{16,8},{24,16},{32,24},{40,32},{48,40},{56,48},{64,... | collective-permute-start | bytes 24584 | tf_op jit(solution)/shard_map/ppermute | solution.py:12
  88.8 7.8 %collective-permute-start.8 = (f32[32,128]{1,0:T(8,128)S(1)}, f32[32,128]{1,0:T(8,128)S(1)}, u32[]{:S(2)}, u32[]{:S(2)}) collective-permute-start(f32[32,128]{1,0:T(8,128)S(1)} %slice_add_fusion.20), channel_id=1, source_target_pairs={{0,8},{8,16},{16,24},{24,32},{32,40},{40,48},{48,56},{56,64},{64,7... | collective-permute-start | bytes 49160 | tf_op jit(solution)/shard_map/ppermute | solution.py:12
  114.6 4.7 %collective-permute-start.9 = (f32[32,256]{1,0:T(8,128)S(1)}, f32[32,256]{1,0:T(8,128)S(1)}, u32[]{:S(2)}, u32[]{:S(2)}) collective-permute-start(f32[32,256]{1,0:T(8,128)S(1)} %fusion.242), channel_id=1, source_target_pairs={{0,8},{8,0},{16,24},{24,16},{32,40},{40,32},{48,56},{56,48},{64,72... | collective-permute-start | bytes 98312 | tf_op jit(solution)/shard_map/ppermute | solution.py:102
  119.3 6.2 %collective-permute-start.10 = (f32[32,256]{1,0:T(8,128)S(1)}, f32[32,256]{1,0:T(8,128)S(1)}, u32[]{:S(2)}, u32[]{:S(2)}) collective-permute-start(f32[32,256]{1,0:T(8,128)S(1)} %add.231), channel_id=1, source_target_pairs={{0,16},{8,24},{16,0},{24,8},{32,48},{40,56},{48,32},{56,40},{64,80... | collective-permute-start | bytes 98312 | tf_op jit(solution)/shard_map/ppermute | solution.py:102
  125.5 4.6 %collective-permute-start.11 = (f32[32,256]{1,0:T(8,128)S(1)}, f32[32,256]{1,0:T(8,128)S(1)}, u32[]{:S(2)}, u32[]{:S(2)}) collective-permute-start(f32[32,256]{1,0:T(8,128)S(1)} %add.232), channel_id=1, source_target_pairs={{0,32},{8,40},{16,48},{24,56},{32,0},{40,8},{48,16},{56,24},{64,96... | collective-permute-start | bytes 98312 | tf_op jit(solution)/shard_map/ppermute | solution.py:102
  130.1 5.6 %collective-permute-start.12 = (f32[32,256]{1,0:T(8,128)S(1)}, f32[32,256]{1,0:T(8,128)S(1)}, u32[]{:S(2)}, u32[]{:S(2)}) collective-permute-start(f32[32,256]{1,0:T(8,128)S(1)} %add.233), channel_id=1, source_target_pairs={{0,64},{8,72},{16,80},{24,88},{32,96},{40,104},{48,112},{56,120},{... | collective-permute-start | bytes 98312 | tf_op jit(solution)/shard_map/ppermute | solution.py:102
  135.7 9.0 %collective-permute-start.13 = (f32[32,256]{1,0:T(8,128)S(1)}, f32[32,256]{1,0:T(8,128)S(1)}, u32[]{:S(2)}, u32[]{:S(2)}) collective-permute-start(f32[32,256]{1,0:T(8,128)S(1)} %add.234), channel_id=1, source_target_pairs={{0,128},{8,136},{16,144},{24,152},{32,160},{40,168},{48,176},{56,1... | collective-permute-start | bytes 98312 | tf_op jit(solution)/shard_map/ppermute | solution.py:102
  144.7 14.8 %collective-permute-start.14 = (f32[32,256]{1,0:T(8,128)S(1)}, f32[32,256]{1,0:T(8,128)S(1)}, u32[]{:S(2)}, u32[]{:S(2)}) collective-permute-start(f32[32,256]{1,0:T(8,128)S(1)} %add.235), channel_id=1, source_target_pairs={{0,256},{8,264},{16,272},{24,280},{32,288},{40,296},{48,304},{56,3... | collective-permute-start | bytes 98312 | tf_op jit(solution)/shard_map/ppermute | solution.py:102
  159.5 23.2 %collective-permute-start.15 = (f32[32,256]{1,0:T(8,128)S(1)}, f32[32,256]{1,0:T(8,128)S(1)}, u32[]{:S(2)}, u32[]{:S(2)}) collective-permute-start(f32[32,256]{1,0:T(8,128)S(1)} %add.236), channel_id=1, source_target_pairs={{0,512},{8,520},{16,528},{24,536},{32,544},{40,552},{48,560},{56,5... | collective-permute-start | bytes 98312 | tf_op jit(solution)/shard_map/ppermute | solution.py:102

commit v5 on v2

--- a/solution.py
+++ b/solution.py
@@ -65,12 +65,34 @@
     return local_part + back
 
 
-def butterfly_sum(block, axis):
+def ring_partners(count):
+    steps = []
+    stride = 1
+    while stride * 2 < count:
+        steps.append([position ^ stride for position in range(count)])
+        stride *= 2
+    quarter = count // 4
+    if count >= 4:
+        steps.append(
+            [
+                (position + quarter) % count if (position // quarter) % 2 else (position - quarter) % count
+                for position in range(count)
+            ]
+        )
+    elif count == 2:
+        steps.append([1, 0])
+    return steps
+
+
+def butterfly_sum(block, axis, inner):
     peers = lax.axis_size(axis)
-    stride = 1
-    while stride < peers:
-        block = block + lax.ppermute(block, axis, [(i, i ^ stride) for i in range(peers)])
-        stride *= 2
+    outer = peers // inner
+    for step in ring_partners(inner):
+        pairs = [(i, (i // inner) * inner + step[i % inner]) for i in range(peers)]
+        block = block + lax.ppermute(block, axis, pairs)
+    for step in ring_partners(outer):
+        pairs = [(i, step[i // inner] * inner + i % inner) for i in range(peers)]
+        block = block + lax.ppermute(block, axis, pairs)
     return block
 
 
@@ -105,7 +127,7 @@
     column_count = filtered.shape[0]
     every_column = lax.all_gather(filtered, "wave", axis=0, tiled=True)
     own_rows = jnp.dot(filtered, every_column.T, preferred_element_type=jnp.float32)
-    own_rows = butterfly_sum(own_rows, "space")
+    own_rows = butterfly_sum(own_rows, "space", 4)
     margin = lax.all_gather(own_rows, "wave", axis=0, tiled=True) / node_total
     rotation = newton_schulz(margin)
     own_rotation = lax.dynamic_slice_in_dim(

time: 202 us -> 192 us (0.950)
  waiting for transfers between devices: 68.9 us -> 63.3 us
  starting transfers between devices: 57.8 us -> 53.5 us
    ppermute x7, waiting for transfers between devices: 44.7 us -> 39.1 us  [butterfly_sum(): block = block + lax.ppermute(block, axis, pairs)]
    ppermute x7, starting transfers between devices: 22.8 us -> 18.5 us  [butterfly_sum(): block = block + lax.ppermute(block, axis, pairs)]
where the time goes in v5:
time: 192 us; the launch traced here: 191 us
  waiting for transfers between devices  63.3 us (33%)
  starting transfers between devices  53.5 us (28%)
  blocking collectives  42.4 us (22%)
  matrix products  25 us (13%)
  local copies, waits for them, and re-layouts  2.99 us (2%)
  other arithmetic  2.65 us (1%)
    ppermute x7, waiting for transfers between devices, butterfly_sum(): block = block + lax.ppermute(block, axis, pairs)  39.1 us
    ppermute x8, starting transfers between devices, from_behind(): lax.ppermute(shard, axis, [(i, (i + by) % peers) for i in range(peers)])  35 us
    ppermute x8, waiting for transfers between devices, from_behind(): lax.ppermute(shard, axis, [(i, (i + by) % peers) for i in range(peers)])  24.2 us
    all_gather x1, blocking collectives, body(): every_column = lax.all_gather(filtered, 'wave', axis=0, tiled=True)  22.2 us
    all_gather x1, blocking collectives, body(): margin = lax.all_gather(own_rows, 'wave', axis=0, tiled=True) / node_total  20.2 us
    ppermute x7, starting transfers between devices, butterfly_sum(): block = block + lax.ppermute(block, axis, pairs)  18.5 us
    dot_general x4, matrix products, apply_filter(): jnp.dot(stacked, pick[:, node_count:], preferred_element_type=jnp.float32)  5.13 us
    dot_general x4, matrix products, apply_filter(): jnp.dot(stacked, pick[:, :node_count], preferred_element_type=jnp.float32)  3.89 us
  transfers between devices with their start and end apart: 15, of which 14 were waited for; matrix products, arithmetic and copies ran while one was open for 5% of the time, Pallas kernels for 0%

profile of v5, /device:TPU:1, one launch (start us, length us, event | category | flops | bytes accessed | tf_op | source)
XLA Modules:
  0.0 191.2 jit_solution(5308615425135200633)
XLA Ops:
  1.5 21.4 %collective-permute-start = (bf16[32,128]{0,1:T(8,128)(2,1)S(1)}, bf16[32,128]{0,1:T(8,128)(2,1)S(1)}, u32[]{:S(2)}, u32[]{:S(2)}) collective-permute-start(bf16[32,128]{0,1:T(8,128)(2,1)S(1)} %fusion.42), channel_id=1, source_target_pairs={{0,1016},{8,0},{16,8},{24,16},{32,24},{40,32},{48,40},{56,48},{64,... | collective-permute-start | bytes 24584 | tf_op jit(solution)/shard_map/ppermute | solution.py:12
  23.7 1.5 iota_compare_fusion
  29.0 1.9 %collective-permute-start.1 = (f32[32,128]{1,0:T(8,128)S(1)}, f32[32,128]{1,0:T(8,128)S(1)}, u32[]{:S(2)}, u32[]{:S(2)}) collective-permute-start(f32[32,128]{1,0:T(8,128)S(1)} %slice_add_fusion.22), channel_id=1, source_target_pairs={{0,8},{8,16},{16,24},{24,32},{32,40},{40,48},{48,56},{56,64},{64,7... | collective-permute-start | bytes 49160 | tf_op jit(solution)/shard_map/ppermute | solution.py:12
  31.9 4.9 %collective-permute-done.1 = f32[32,128]{1,0:T(8,128)S(1)} collective-permute-done((f32[32,128]{1,0:T(8,128)S(1)}, f32[32,128]{1,0:T(8,128)S(1)}, u32[]{:S(2)}, u32[]{:S(2)}) %collective-permute-start.1) | collective-permute-done | bytes 16416 | tf_op jit(solution)/shard_map/ppermute | solution.py:12
  37.6 1.9 %collective-permute-start.2 = (bf16[32,128]{1,0:T(8,128)(2,1)S(1)}, bf16[32,128]{1,0:T(8,128)(2,1)S(1)}, u32[]{:S(2)}, u32[]{:S(2)}) collective-permute-start(bf16[32,128]{1,0:T(8,128)(2,1)S(1)} %fusion.43), channel_id=1, source_target_pairs={{0,1016},{8,0},{16,8},{24,16},{32,24},{40,32},{48,40},{56,48},{64,... | collective-permute-start | bytes 24584 | tf_op jit(solution)/shard_map/ppermute | solution.py:12
  40.5 1.5 collective-permute-done.2
  44.6 1.9 %collective-permute-start.3 = (f32[32,128]{1,0:T(8,128)S(1)}, f32[32,128]{1,0:T(8,128)S(1)}, u32[]{:S(2)}, u32[]{:S(2)}) collective-permute-start(f32[32,128]{1,0:T(8,128)S(1)} %slice_add_fusion.20), channel_id=1, source_target_pairs={{0,8},{8,16},{16,24},{24,32},{32,40},{40,48},{48,56},{56,64},{64,7... | collective-permute-start | bytes 49160 | tf_op jit(solution)/shard_map/ppermute | solution.py:12
  47.5 4.9 %collective-permute-done.3 = f32[32,128]{1,0:T(8,128)S(1)} collective-permute-done((f32[32,128]{1,0:T(8,128)S(1)}, f32[32,128]{1,0:T(8,128)S(1)}, u32[]{:S(2)}, u32[]{:S(2)}) %collective-permute-start.3) | collective-permute-done | bytes 16416 | tf_op jit(solution)/shard_map/ppermute | solution.py:12
  53.2 1.9 %collective-permute-start.4 = (bf16[32,128]{1,0:T(8,128)(2,1)S(1)}, bf16[32,128]{1,0:T(8,128)(2,1)S(1)}, u32[]{:S(2)}, u32[]{:S(2)}) collective-permute-start(bf16[32,128]{1,0:T(8,128)(2,1)S(1)} %fusion.46), channel_id=1, source_target_pairs={{0,1016},{8,0},{16,8},{24,16},{32,24},{40,32},{48,40},{56,48},{64,... | collective-permute-start | bytes 24584 | tf_op jit(solution)/shard_map/ppermute | solution.py:12
  56.1 1.5 collective-permute-done.4
  60.2 1.9 %collective-permute-start.5 = (f32[32,128]{1,0:T(8,128)S(1)}, f32[32,128]{1,0:T(8,128)S(1)}, u32[]{:S(2)}, u32[]{:S(2)}) collective-permute-start(f32[32,128]{1,0:T(8,128)S(1)} %slice_add_fusion.18), channel_id=1, source_target_pairs={{0,8},{8,16},{16,24},{24,32},{32,40},{40,48},{48,56},{56,64},{64,7... | collective-permute-start | bytes 49160 | tf_op jit(solution)/shard_map/ppermute | solution.py:12
  63.1 4.9 %collective-permute-done.5 = f32[32,128]{1,0:T(8,128)S(1)} collective-permute-done((f32[32,128]{1,0:T(8,128)S(1)}, f32[32,128]{1,0:T(8,128)S(1)}, u32[]{:S(2)}, u32[]{:S(2)}) %collective-permute-start.5) | collective-permute-done | bytes 16416 | tf_op jit(solution)/shard_map/ppermute | solution.py:12
  68.8 2.1 %collective-permute-start.6 = (bf16[32,128]{1,0:T(8,128)(2,1)S(1)}, bf16[32,128]{1,0:T(8,128)(2,1)S(1)}, u32[]{:S(2)}, u32[]{:S(2)}) collective-permute-start(bf16[32,128]{1,0:T(8,128)(2,1)S(1)} %fusion.49), channel_id=1, source_target_pairs={{0,1016},{8,0},{16,8},{24,16},{32,24},{40,32},{48,40},{56,48},{64,... | collective-permute-start | bytes 24584 | tf_op jit(solution)/shard_map/ppermute | solution.py:12
  71.9 1.6 collective-permute-done.6
  76.1 1.9 %collective-permute-start.7 = (f32[32,128]{1,0:T(8,128)S(1)}, f32[32,128]{1,0:T(8,128)S(1)}, u32[]{:S(2)}, u32[]{:S(2)}) collective-permute-start(f32[32,128]{1,0:T(8,128)S(1)} %slice_add_fusion.16), channel_id=1, source_target_pairs={{0,8},{8,16},{16,24},{24,32},{32,40},{40,48},{48,56},{56,64},{64,7... | collective-permute-start | bytes 49160 | tf_op jit(solution)/shard_map/ppermute | solution.py:12
  79.0 4.9 %collective-permute-done.7 = f32[32,128]{1,0:T(8,128)S(1)} collective-permute-done((f32[32,128]{1,0:T(8,128)S(1)}, f32[32,128]{1,0:T(8,128)S(1)}, u32[]{:S(2)}, u32[]{:S(2)}) %collective-permute-start.7) | collective-permute-done | bytes 16416 | tf_op jit(solution)/shard_map/ppermute | solution.py:12
  84.4 22.2 %all_gather.6 = bf16[256,1024]{1,0:T(8,128)(2,1)S(1)} all-gather(bf16[32,1024]{1,0:T(8,128)(2,1)S(1)} %fusion.81), channel_id=1, replica_groups=mesh['space'=128,'wave'=8] {'wave'}, dimensions={0}, use_global_device_ids=true | all-gather | bytes 589824 | tf_op jit(solution)/shard_map/all_gather | solution.py:128
  106.8 1.9 %collective-permute-start.8 = (f32[32,256]{1,0:T(8,128)S(1)}, f32[32,256]{1,0:T(8,128)S(1)}, u32[]{:S(2)}, u32[]{:S(2)}) collective-permute-start(f32[32,256]{1,0:T(8,128)S(1)} %fusion.171), channel_id=1, source_target_pairs={{0,8},{8,0},{16,24},{24,16},{32,40},{40,32},{48,56},{56,48},{64,72... | collective-permute-start | bytes 98312 | tf_op jit(solution)/shard_map/ppermute | solution.py:92
  108.7 2.7 %collective-permute-done.8 = f32[32,256]{1,0:T(8,128)S(1)} collective-permute-done((f32[32,256]{1,0:T(8,128)S(1)}, f32[32,256]{1,0:T(8,128)S(1)}, u32[]{:S(2)}, u32[]{:S(2)}) %collective-permute-start.8) | collective-permute-done | bytes 32800 | tf_op jit(solution)/shard_map/ppermute | solution.py:92
  111.5 1.9 collective-permute-start.9
  113.4 3.9 %collective-permute-done.9 = f32[32,256]{1,0:T(8,128)S(1)} collective-permute-done((f32[32,256]{1,0:T(8,128)S(1)}, f32[32,256]{1,0:T(8,128)S(1)}, u32[]{:S(2)}, u32[]{:S(2)}) %collective-permute-start.9) | collective-permute-done | bytes 32800 | tf_op jit(solution)/shard_map/ppermute | solution.py:92
  117.3 1.9 collective-permute-start.10
  119.3 2.7 %collective-permute-done.10 = f32[32,256]{1,0:T(8,128)S(1)} collective-permute-done((f32[32,256]{1,0:T(8,128)S(1)}, f32[32,256]{1,0:T(8,128)S(1)}, u32[]{:S(2)}, u32[]{:S(2)}) %collective-permute-start.10) | collective-permute-done | bytes 32800 | tf_op jit(solution)/shard_map/ppermute | solution.py:95
  122.0 1.9 collective-permute-start.11
  123.9 3.7 %collective-permute-done.11 = f32[32,256]{1,0:T(8,128)S(1)} collective-permute-done((f32[32,256]{1,0:T(8,128)S(1)}, f32[32,256]{1,0:T(8,128)S(1)}, u32[]{:S(2)}, u32[]{:S(2)}) %collective-permute-start.11) | collective-permute-done | bytes 32800 | tf_op jit(solution)/shard_map/ppermute | solution.py:95
  127.6 1.9 collective-permute-start.12
  129.5 7.1 %collective-permute-done.12 = f32[32,256]{1,0:T(8,128)S(1)} collective-permute-done((f32[32,256]{1,0:T(8,128)S(1)}, f32[32,256]{1,0:T(8,128)S(1)}, u32[]{:S(2)}, u32[]{:S(2)}) %collective-permute-start.12) | collective-permute-done | bytes 32800 | tf_op jit(solution)/shard_map/ppermute | solution.py:95
  136.6 1.9 collective-permute-start.13
  138.5 12.6 %collective-permute-done.13 = f32[32,256]{1,0:T(8,128)S(1)} collective-permute-done((f32[32,256]{1,0:T(8,128)S(1)}, f32[32,256]{1,0:T(8,128)S(1)}, u32[]{:S(2)}, u32[]{:S(2)}) %collective-permute-start.13) | collective-permute-done | bytes 32800 | tf_op jit(solution)/shard_map/ppermute | solution.py:95
  151.1 7.0 %collective-permute-start.14 = (f32[32,256]{1,0:T(8,128)S(1)}, f32[32,256]{1,0:T(8,128)S(1)}, u32[]{:S(2)}, u32[]{:S(2)}) collective-permute-start(f32[32,256]{1,0:T(8,128)S(1)} %add.160), channel_id=1, source_target_pairs={{0,768},{8,776},{16,784},{24,792},{32,800},{40,808},{48,816},{56,8... | collective-permute-start | bytes 98312 | tf_op jit(solution)/shard_map/ppermute | solution.py:95
  158.2 6.3 %collective-permute-done.14 = f32[32,256]{1,0:T(8,128)S(1)} collective-permute-done((f32[32,256]{1,0:T(8,128)S(1)}, f32[32,256]{1,0:T(8,128)S(1)}, u32[]{:S(2)}, u32[]{:S(2)}) %collective-permute-start.14) | collective-permute-done | bytes 32800 | tf_op jit(solution)/shard_map/ppermute | solution.py:95
  164.5 20.2 %all_gather.7 = f32[256,256]{1,0:T(8,128)S(1)} all-gather(f32[32,256]{1,0:T(8,128)S(1)} %add.161), channel_id=1, replica_groups=mesh['space'=128,'wave'=8] {'wave'}, dimensions={0}, use_global_device_ids=true | all-gather | bytes 294912 | tf_op jit(solution)/shard_map/all_gather | solution.py:131
  (96 shorter events, 29.2 us)
Async XLA Ops:
  0.0 26.8 %copy-start = (bf16[2,729,729]{2,0,1:T(2,128)(2,1)S(1)}, bf16[2,729,729]{2,0,1:T(2,128)(2,1)}, u32[]{:S(2)}) copy-start(bf16[2,729,729]{2,0,1:T(2,128)(2,1)} %param.5) | copy-start | bytes 6377296
  0.0 25.1 %copy-start.6 = (bf16[32,1024]{1,0:T(8,128)(2,1)S(1)}, bf16[32,1024]{1,0:T(8,128)(2,1)}, u32[]{:S(2)}) copy-start(bf16[32,1024]{1,0:T(8,128)(2,1)} %param.4) | copy-start | bytes 196612
  1.5 24.7 %collective-permute-start = (bf16[32,128]{0,1:T(8,128)(2,1)S(1)}, bf16[32,128]{0,1:T(8,128)(2,1)S(1)}, u32[]{:S(2)}, u32[]{:S(2)}) collective-permute-start(bf16[32,128]{0,1:T(8,128)(2,1)S(1)} %fusion.42), channel_id=1, source_target_pairs={{0,1016},{8,0},{16,8},{24,16},{32,24},{40,32},{48,40},{56,48},{64,... | collective-permute-start | bytes 24584 | tf_op jit(solution)/shard_map/ppermute | solution.py:12
  25.1 1.2 copy-start.1
  27.6 3.3 %copy-start.2 = (pred[1458,1152]{1,0:T(8,128)(4,1)S(1)}, pred[1458,1152]{1,0:T(8,128)(4,1)}, u32[]{:S(2)}) copy-start(pred[1458,1152]{1,0:T(8,128)(4,1)} %copy-done.1) | copy-start | bytes 5038852
  29.0 7.8 %copy-start.7 = (s32[128]{0:T(128)S(1)}, s32[128]{0:T(128)}, u32[]{:S(2)}) copy-start(s32[128]{0:T(128)} %param.7) | copy-start | bytes 1540
  29.0 7.8 %collective-permute-start.1 = (f32[32,128]{1,0:T(8,128)S(1)}, f32[32,128]{1,0:T(8,128)S(1)}, u32[]{:S(2)}, u32[]{:S(2)}) collective-permute-start(f32[32,128]{1,0:T(8,128)S(1)} %slice_add_fusion.22), channel_id=1, source_target_pairs={{0,8},{8,16},{16,24},{24,32},{32,40},{40,48},{48,56},{56,64},{64,7... | collective-permute-start | bytes 49160 | tf_op jit(solution)/shard_map/ppermute | solution.py:12
  37.6 4.4 %collective-permute-start.2 = (bf16[32,128]{1,0:T(8,128)(2,1)S(1)}, bf16[32,128]{1,0:T(8,128)(2,1)S(1)}, u32[]{:S(2)}, u32[]{:S(2)}) collective-permute-start(bf16[32,128]{1,0:T(8,128)(2,1)S(1)} %fusion.43), channel_id=1, source_target_pairs={{0,1016},{8,0},{16,8},{24,16},{32,24},{40,32},{48,40},{56,48},{64,... | collective-permute-start | bytes 24584 | tf_op jit(solution)/shard_map/ppermute | solution.py:12
  43.3 3.3 %copy-start.3 = (pred[1458,1152]{1,0:T(8,128)(4,1)S(1)}, pred[1458,1152]{1,0:T(8,128)(4,1)}, u32[]{:S(2)}) copy-start(pred[1458,1152]{1,0:T(8,128)(4,1)} %copy-done.1) | copy-start | bytes 5038852
  44.6 7.8 %collective-permute-start.3 = (f32[32,128]{1,0:T(8,128)S(1)}, f32[32,128]{1,0:T(8,128)S(1)}, u32[]{:S(2)}, u32[]{:S(2)}) collective-permute-start(f32[32,128]{1,0:T(8,128)S(1)} %slice_add_fusion.20), channel_id=1, source_target_pairs={{0,8},{8,16},{16,24},{24,32},{32,40},{40,48},{48,56},{56,64},{64,7... | collective-permute-start | bytes 49160 | tf_op jit(solution)/shard_map/ppermute | solution.py:12
  53.2 4.4 %collective-permute-start.4 = (bf16[32,128]{1,0:T(8,128)(2,1)S(1)}, bf16[32,128]{1,0:T(8,128)(2,1)S(1)}, u32[]{:S(2)}, u32[]{:S(2)}) collective-permute-start(bf16[32,128]{1,0:T(8,128)(2,1)S(1)} %fusion.46), channel_id=1, source_target_pairs={{0,1016},{8,0},{16,8},{24,16},{32,24},{40,32},{48,40},{56,48},{64,... | collective-permute-start | bytes 24584 | tf_op jit(solution)/shard_map/ppermute | solution.py:12
  58.9 3.3 %copy-start.4 = (pred[1458,1152]{1,0:T(8,128)(4,1)S(1)}, pred[1458,1152]{1,0:T(8,128)(4,1)}, u32[]{:S(2)}) copy-start(pred[1458,1152]{1,0:T(8,128)(4,1)} %copy-done.1) | copy-start | bytes 5038852
  60.2 7.8 %collective-permute-start.5 = (f32[32,128]{1,0:T(8,128)S(1)}, f32[32,128]{1,0:T(8,128)S(1)}, u32[]{:S(2)}, u32[]{:S(2)}) collective-permute-start(f32[32,128]{1,0:T(8,128)S(1)} %slice_add_fusion.18), channel_id=1, source_target_pairs={{0,8},{8,16},{16,24},{24,32},{32,40},{40,48},{48,56},{56,64},{64,7... | collective-permute-start | bytes 49160 | tf_op jit(solution)/shard_map/ppermute | solution.py:12
  68.8 4.7 %collective-permute-start.6 = (bf16[32,128]{1,0:T(8,128)(2,1)S(1)}, bf16[32,128]{1,0:T(8,128)(2,1)S(1)}, u32[]{:S(2)}, u32[]{:S(2)}) collective-permute-start(bf16[32,128]{1,0:T(8,128)(2,1)S(1)} %fusion.49), channel_id=1, source_target_pairs={{0,1016},{8,0},{16,8},{24,16},{32,24},{40,32},{48,40},{56,48},{64,... | collective-permute-start | bytes 24584 | tf_op jit(solution)/shard_map/ppermute | solution.py:12
  74.8 3.3 %copy-start.5 = (pred[1458,1152]{1,0:T(8,128)(4,1)S(1)}, pred[1458,1152]{1,0:T(8,128)(4,1)}, u32[]{:S(2)}) copy-start(pred[1458,1152]{1,0:T(8,128)(4,1)} %copy-done.1) | copy-start | bytes 5038852
  76.1 7.8 %collective-permute-start.7 = (f32[32,128]{1,0:T(8,128)S(1)}, f32[32,128]{1,0:T(8,128)S(1)}, u32[]{:S(2)}, u32[]{:S(2)}) collective-permute-start(f32[32,128]{1,0:T(8,128)S(1)} %slice_add_fusion.16), channel_id=1, source_target_pairs={{0,8},{8,16},{16,24},{24,32},{32,40},{40,48},{48,56},{56,64},{64,7... | collective-permute-start | bytes 49160 | tf_op jit(solution)/shard_map/ppermute | solution.py:12
  106.8 4.7 %collective-permute-start.8 = (f32[32,256]{1,0:T(8,128)S(1)}, f32[32,256]{1,0:T(8,128)S(1)}, u32[]{:S(2)}, u32[]{:S(2)}) collective-permute-start(f32[32,256]{1,0:T(8,128)S(1)} %fusion.171), channel_id=1, source_target_pairs={{0,8},{8,0},{16,24},{24,16},{32,40},{40,32},{48,56},{56,48},{64,72... | collective-permute-start | bytes 98312 | tf_op jit(solution)/shard_map/ppermute | solution.py:92
  111.5 5.9 %collective-permute-start.9 = (f32[32,256]{1,0:T(8,128)S(1)}, f32[32,256]{1,0:T(8,128)S(1)}, u32[]{:S(2)}, u32[]{:S(2)}) collective-permute-start(f32[32,256]{1,0:T(8,128)S(1)} %add.155), channel_id=1, source_target_pairs={{0,24},{8,16},{16,8},{24,0},{32,56},{40,48},{48,40},{56,32},{64,88... | collective-permute-start | bytes 98312 | tf_op jit(solution)/shard_map/ppermute | solution.py:92
  117.3 4.6 %collective-permute-start.10 = (f32[32,256]{1,0:T(8,128)S(1)}, f32[32,256]{1,0:T(8,128)S(1)}, u32[]{:S(2)}, u32[]{:S(2)}) collective-permute-start(f32[32,256]{1,0:T(8,128)S(1)} %add.156), channel_id=1, source_target_pairs={{0,32},{8,40},{16,48},{24,56},{32,0},{40,8},{48,16},{56,24},{64,96... | collective-permute-start | bytes 98312 | tf_op jit(solution)/shard_map/ppermute | solution.py:95
  122.0 5.6 %collective-permute-start.11 = (f32[32,256]{1,0:T(8,128)S(1)}, f32[32,256]{1,0:T(8,128)S(1)}, u32[]{:S(2)}, u32[]{:S(2)}) collective-permute-start(f32[32,256]{1,0:T(8,128)S(1)} %add.157), channel_id=1, source_target_pairs={{0,64},{8,72},{16,80},{24,88},{32,96},{40,104},{48,112},{56,120},{... | collective-permute-start | bytes 98312 | tf_op jit(solution)/shard_map/ppermute | solution.py:95
  127.6 9.0 %collective-permute-start.12 = (f32[32,256]{1,0:T(8,128)S(1)}, f32[32,256]{1,0:T(8,128)S(1)}, u32[]{:S(2)}, u32[]{:S(2)}) collective-permute-start(f32[32,256]{1,0:T(8,128)S(1)} %add.158), channel_id=1, source_target_pairs={{0,128},{8,136},{16,144},{24,152},{32,160},{40,168},{48,176},{56,1... | collective-permute-start | bytes 98312 | tf_op jit(solution)/shard_map/ppermute | solution.py:95
  136.6 14.5 %collective-permute-start.13 = (f32[32,256]{1,0:T(8,128)S(1)}, f32[32,256]{1,0:T(8,128)S(1)}, u32[]{:S(2)}, u32[]{:S(2)}) collective-permute-start(f32[32,256]{1,0:T(8,128)S(1)} %add.159), channel_id=1, source_target_pairs={{0,256},{8,264},{16,272},{24,280},{32,288},{40,296},{48,304},{56,3... | collective-permute-start | bytes 98312 | tf_op jit(solution)/shard_map/ppermute | solution.py:95
  151.1 13.4 %collective-permute-start.14 = (f32[32,256]{1,0:T(8,128)S(1)}, f32[32,256]{1,0:T(8,128)S(1)}, u32[]{:S(2)}, u32[]{:S(2)}) collective-permute-start(f32[32,256]{1,0:T(8,128)S(1)} %add.160), channel_id=1, source_target_pairs={{0,768},{8,776},{16,784},{24,792},{32,800},{40,808},{48,816},{56,8... | collective-permute-start | bytes 98312 | tf_op jit(solution)/shard_map/ppermute | solution.py:95

commit v6 on v5

--- a/solution.py
+++ b/solution.py
@@ -35,11 +35,10 @@
     return pick, owner
 
 
-def apply_filter(wave_block, cell_matrices, pick, owner):
+def apply_filter(wave_block, own_plane, cell_matrices, pick, owner):
     column_count = wave_block.shape[0]
     node_count = wave_block.shape[1]
     cell_count, cell_nodes, _ = cell_matrices.shape
-    own_plane = jnp.dot(wave_block, owner, preferred_element_type=jnp.float32).astype(jnp.bfloat16)
     upper_plane = from_behind(own_plane, "space", -1)
     contract_nodes = (((1,), (1,)), ((), ()))
     gathered = lax.dot_general(
@@ -59,10 +58,13 @@
     local_part = sum_three(
         jnp.dot(stacked, pick[:, :node_count], preferred_element_type=jnp.float32)
     )
+    local_plane = sum_three(
+        jnp.dot(split_three(local_part), owner, preferred_element_type=jnp.float32)
+    )
     back = sum_three(
         lax.dot_general(split_three(returned), owner, contract_nodes, preferred_element_type=jnp.float32)
     )
-    return local_part + back
+    return local_part + back, local_plane + returned
 
 
 def ring_partners(count):
@@ -114,14 +116,18 @@
 
 def body(wavefunctions, filter_cells, connectivity, owner_list):
     pick, owner = selectors(connectivity, owner_list, wavefunctions.shape[1])
+    start_plane = jnp.dot(wavefunctions, owner, preferred_element_type=jnp.float32).astype(jnp.bfloat16)
     previous = wavefunctions.astype(jnp.float32)
-    current = apply_filter(wavefunctions, filter_cells, pick, owner)
+    previous_plane = start_plane.astype(jnp.float32)
+    current, current_plane = apply_filter(wavefunctions, start_plane, filter_cells, pick, owner)
     for degree_step in range(DEGREE - 1):
-        following = (
-            2.0 * apply_filter(current.astype(jnp.bfloat16), filter_cells, pick, owner)
-            - previous
+        applied, applied_plane = apply_filter(
+            current.astype(jnp.bfloat16), current_plane.astype(jnp.bfloat16), filter_cells, pick, owner
         )
+        following = 2.0 * applied - previous
+        following_plane = 2.0 * applied_plane - previous_plane
         previous, current = (current, following)
+        previous_plane, current_plane = (current_plane, following_plane)
     filtered = current.astype(jnp.bfloat16)
     node_total = filtered.shape[1] * lax.axis_size("space")
     column_count = filtered.shape[0]

time: 192 us -> 195 us (1.016)
  transfers between devices with their start and end apart: 15 -> 15, of which waited for: 14 -> 14; matrix products, arithmetic and copies ran while one was open for 5% -> 4% of each run, Pallas kernels for 0% -> 0%
where the time goes in v6:
time: 195 us; the launch traced here: 194 us
  waiting for transfers between devices  65.1 us (33%)
  starting transfers between devices  53.8 us (28%)
  blocking collectives  42.4 us (22%)
  matrix products  24.9 us (13%)
  local copies, waits for them, and re-layouts  3.6 us (2%)
  other arithmetic  2.68 us (1%)
    ppermute x7, waiting for transfers between devices, butterfly_sum(): block = block + lax.ppermute(block, axis, pairs)  39.1 us
    ppermute x8, starting transfers between devices, from_behind(): lax.ppermute(shard, axis, [(i, (i + by) % peers) for i in range(peers)])  35.3 us
    ppermute x8, waiting for transfers between devices, from_behind(): lax.ppermute(shard, axis, [(i, (i + by) % peers) for i in range(peers)])  26 us
    all_gather x1, blocking collectives, body(): every_column = lax.all_gather(filtered, 'wave', axis=0, tiled=True)  22.2 us
    all_gather x1, blocking collectives, body(): margin = lax.all_gather(own_rows, 'wave', axis=0, tiled=True) / node_total  20.2 us
    ppermute x7, starting transfers between devices, butterfly_sum(): block = block + lax.ppermute(block, axis, pairs)  18.5 us
    dot_general x4, matrix products, apply_filter(): jnp.dot(stacked, pick[:, node_count:], preferred_element_type=jnp.float32)  5.13 us
  transfers between devices with their start and end apart: 15, of which 14 were waited for; matrix products, arithmetic and copies ran while one was open for 4% of the time, Pallas kernels for 0%

profile of v6, /device:TPU:1, one launch (start us, length us, event | category | flops | bytes accessed | tf_op | source)
XLA Modules:
  0.0 193.8 jit_solution(4553886710292856762)
XLA Ops:
  0.0 1.4 fusion.47
  1.4 21.4 %collective-permute-start = (bf16[32,128]{1,0:T(8,128)(2,1)S(1)}, bf16[32,128]{1,0:T(8,128)(2,1)S(1)}, u32[]{:S(2)}, u32[]{:S(2)}) collective-permute-start(bf16[32,128]{1,0:T(8,128)(2,1)S(1)} %fusion.47), channel_id=1, source_target_pairs={{0,1016},{8,0},{16,8},{24,16},{32,24},{40,32},{48,40},{56,48},{64,... | collective-permute-start | bytes 24584 | tf_op jit(solution)/shard_map/ppermute | solution.py:12
  23.6 1.5 iota_compare_fusion
  30.1 1.9 collective-permute-start.1
  32.0 5.8 %collective-permute-done.1 = f32[32,128]{1,0:T(8,128)S(1)} collective-permute-done((f32[32,128]{1,0:T(8,128)S(1)}, f32[32,128]{1,0:T(8,128)S(1)}, u32[]{:S(2)}, u32[]{:S(2)}) %collective-permute-start.1) | collective-permute-done | bytes 16416 | tf_op jit(solution)/shard_map/ppermute | solution.py:12
  38.7 1.9 collective-permute-start.2
  41.6 1.5 collective-permute-done.2
  46.9 1.9 collective-permute-start.3
  48.8 5.8 %collective-permute-done.3 = f32[32,128]{1,0:T(8,128)S(1)} collective-permute-done((f32[32,128]{1,0:T(8,128)S(1)}, f32[32,128]{1,0:T(8,128)S(1)}, u32[]{:S(2)}, u32[]{:S(2)}) %collective-permute-start.3) | collective-permute-done | bytes 16416 | tf_op jit(solution)/shard_map/ppermute | solution.py:12
  55.5 1.9 collective-permute-start.4
  58.4 1.5 collective-permute-done.4
  63.7 1.9 collective-permute-start.5
  66.0 5.4 %collective-permute-done.5 = f32[32,128]{1,0:T(8,128)S(1)} collective-permute-done((f32[32,128]{1,0:T(8,128)S(1)}, f32[32,128]{1,0:T(8,128)S(1)}, u32[]{:S(2)}, u32[]{:S(2)}) %collective-permute-start.5) | collective-permute-done | bytes 16416 | tf_op jit(solution)/shard_map/ppermute | solution.py:12
  71.5 2.1 %collective-permute-start.6 = (bf16[32,128]{1,0:T(8,128)(2,1)S(1)}, bf16[32,128]{1,0:T(8,128)(2,1)S(1)}, u32[]{:S(2)}, u32[]{:S(2)}) collective-permute-start(bf16[32,128]{1,0:T(8,128)(2,1)S(1)} %get-tuple-element.36), channel_id=1, source_target_pairs={{0,1016},{8,0},{16,8},{24,16},{32,24},{40,32},{48,40},{56,48},{64,... | collective-permute-start | bytes 24584 | tf_op jit(solution)/shard_map/ppermute | solution.py:12
  78.8 2.2 %collective-permute-start.7 = (f32[32,128]{1,0:T(8,128)S(1)}, f32[32,128]{1,0:T(8,128)S(1)}, u32[]{:S(2)}, u32[]{:S(2)}) collective-permute-start(f32[32,128]{1,0:T(8,128)S(1)} %slice_add_fusion.16), channel_id=1, source_target_pairs={{0,8},{8,16},{16,24},{24,32},{32,40},{40,48},{48,56},{56,64},{64,7... | collective-permute-start | bytes 49160 | tf_op jit(solution)/shard_map/ppermute | solution.py:12
  81.9 4.7 %collective-permute-done.7 = f32[32,128]{1,0:T(8,128)S(1)} collective-permute-done((f32[32,128]{1,0:T(8,128)S(1)}, f32[32,128]{1,0:T(8,128)S(1)}, u32[]{:S(2)}, u32[]{:S(2)}) %collective-permute-start.7) | collective-permute-done | bytes 16416 | tf_op jit(solution)/shard_map/ppermute | solution.py:12
  87.0 22.2 %all_gather.6 = bf16[256,1024]{1,0:T(8,128)(2,1)S(1)} all-gather(bf16[32,1024]{1,0:T(8,128)(2,1)S(1)} %fusion.100), channel_id=1, replica_groups=mesh['space'=128,'wave'=8] {'wave'}, dimensions={0}, use_global_device_ids=true | all-gather | bytes 589824 | tf_op jit(solution)/shard_map/all_gather | solution.py:134
  109.5 1.9 collective-permute-start.8
  111.4 2.7 %collective-permute-done.8 = f32[32,256]{1,0:T(8,128)S(1)} collective-permute-done((f32[32,256]{1,0:T(8,128)S(1)}, f32[32,256]{1,0:T(8,128)S(1)}, u32[]{:S(2)}, u32[]{:S(2)}) %collective-permute-start.8) | collective-permute-done | bytes 32800 | tf_op jit(solution)/shard_map/ppermute | solution.py:94
  114.2 1.9 collective-permute-start.9
  116.1 3.9 %collective-permute-done.9 = f32[32,256]{1,0:T(8,128)S(1)} collective-permute-done((f32[32,256]{1,0:T(8,128)S(1)}, f32[32,256]{1,0:T(8,128)S(1)}, u32[]{:S(2)}, u32[]{:S(2)}) %collective-permute-start.9) | collective-permute-done | bytes 32800 | tf_op jit(solution)/shard_map/ppermute | solution.py:94
  120.0 1.9 collective-permute-start.10
  121.9 2.7 %collective-permute-done.10 = f32[32,256]{1,0:T(8,128)S(1)} collective-permute-done((f32[32,256]{1,0:T(8,128)S(1)}, f32[32,256]{1,0:T(8,128)S(1)}, u32[]{:S(2)}, u32[]{:S(2)}) %collective-permute-start.10) | collective-permute-done | bytes 32800 | tf_op jit(solution)/shard_map/ppermute | solution.py:97
  124.7 1.9 collective-permute-start.11
  126.6 3.7 %collective-permute-done.11 = f32[32,256]{1,0:T(8,128)S(1)} collective-permute-done((f32[32,256]{1,0:T(8,128)S(1)}, f32[32,256]{1,0:T(8,128)S(1)}, u32[]{:S(2)}, u32[]{:S(2)}) %collective-permute-start.11) | collective-permute-done | bytes 32800 | tf_op jit(solution)/shard_map/ppermute | solution.py:97
  130.3 1.9 collective-permute-start.12
  132.2 7.1 %collective-permute-done.12 = f32[32,256]{1,0:T(8,128)S(1)} collective-permute-done((f32[32,256]{1,0:T(8,128)S(1)}, f32[32,256]{1,0:T(8,128)S(1)}, u32[]{:S(2)}, u32[]{:S(2)}) %collective-permute-start.12) | collective-permute-done | bytes 32800 | tf_op jit(solution)/shard_map/ppermute | solution.py:97
  139.3 1.9 collective-permute-start.13
  141.2 12.6 %collective-permute-done.13 = f32[32,256]{1,0:T(8,128)S(1)} collective-permute-done((f32[32,256]{1,0:T(8,128)S(1)}, f32[32,256]{1,0:T(8,128)S(1)}, u32[]{:S(2)}, u32[]{:S(2)}) %collective-permute-start.13) | collective-permute-done | bytes 32800 | tf_op jit(solution)/shard_map/ppermute | solution.py:97
  153.8 7.0 %collective-permute-start.14 = (f32[32,256]{1,0:T(8,128)S(1)}, f32[32,256]{1,0:T(8,128)S(1)}, u32[]{:S(2)}, u32[]{:S(2)}) collective-permute-start(f32[32,256]{1,0:T(8,128)S(1)} %add.196), channel_id=1, source_target_pairs={{0,768},{8,776},{16,784},{24,792},{32,800},{40,808},{48,816},{56,8... | collective-permute-start | bytes 98312 | tf_op jit(solution)/shard_map/ppermute | solution.py:97
  160.8 6.3 %collective-permute-done.14 = f32[32,256]{1,0:T(8,128)S(1)} collective-permute-done((f32[32,256]{1,0:T(8,128)S(1)}, f32[32,256]{1,0:T(8,128)S(1)}, u32[]{:S(2)}, u32[]{:S(2)}) %collective-permute-start.14) | collective-permute-done | bytes 32800 | tf_op jit(solution)/shard_map/ppermute | solution.py:97
  167.2 20.2 %all_gather.7 = f32[256,256]{1,0:T(8,128)S(1)} all-gather(f32[32,256]{1,0:T(8,128)S(1)} %add.197), channel_id=1, replica_groups=mesh['space'=128,'wave'=8] {'wave'}, dimensions={0}, use_global_device_ids=true | all-gather | bytes 294912 | tf_op jit(solution)/shard_map/all_gather | solution.py:137
  (101 shorter events, 29.6 us)
Async XLA Ops:
  0.0 26.7 %copy-start = (bf16[2,729,729]{2,0,1:T(2,128)(2,1)S(1)}, bf16[2,729,729]{2,0,1:T(2,128)(2,1)}, u32[]{:S(2)}) copy-start(bf16[2,729,729]{2,0,1:T(2,128)(2,1)} %param.5) | copy-start | bytes 6377296
  0.0 25.0 %copy-start.6 = (bf16[32,1024]{1,0:T(8,128)(2,1)S(1)}, bf16[32,1024]{1,0:T(8,128)(2,1)}, u32[]{:S(2)}) copy-start(bf16[32,1024]{1,0:T(8,128)(2,1)} %param.4) | copy-start | bytes 196612
  1.4 24.7 %collective-permute-start = (bf16[32,128]{1,0:T(8,128)(2,1)S(1)}, bf16[32,128]{1,0:T(8,128)(2,1)S(1)}, u32[]{:S(2)}, u32[]{:S(2)}) collective-permute-start(bf16[32,128]{1,0:T(8,128)(2,1)S(1)} %fusion.47), channel_id=1, source_target_pairs={{0,1016},{8,0},{16,8},{24,16},{32,24},{40,32},{48,40},{56,48},{64,... | collective-permute-start | bytes 24584 | tf_op jit(solution)/shard_map/ppermute | solution.py:12
  25.0 1.2 copy-start.1
  27.5 1.6 copy-start.2
  29.1 8.8 %copy-start.7 = (s32[128]{0:T(128)S(1)}, s32[128]{0:T(128)}, u32[]{:S(2)}) copy-start(s32[128]{0:T(128)} %param.7) | copy-start | bytes 1540
  30.1 7.8 %collective-permute-start.1 = (f32[32,128]{1,0:T(8,128)S(1)}, f32[32,128]{1,0:T(8,128)S(1)}, u32[]{:S(2)}, u32[]{:S(2)}) collective-permute-start(f32[32,128]{1,0:T(8,128)S(1)} %slice_add_fusion.28), channel_id=1, source_target_pairs={{0,8},{8,16},{16,24},{24,32},{32,40},{40,48},{48,56},{56,64},{64,7... | collective-permute-start | bytes 49160 | tf_op jit(solution)/shard_map/ppermute | solution.py:12
  38.7 4.4 %collective-permute-start.2 = (bf16[32,128]{1,0:T(8,128)(2,1)S(1)}, bf16[32,128]{1,0:T(8,128)(2,1)S(1)}, u32[]{:S(2)}, u32[]{:S(2)}) collective-permute-start(bf16[32,128]{1,0:T(8,128)(2,1)S(1)} %get-tuple-element.9), channel_id=1, source_target_pairs={{0,1016},{8,0},{16,8},{24,16},{32,24},{40,32},{48,40},{56,48},{64,... | collective-permute-start | bytes 24584 | tf_op jit(solution)/shard_map/ppermute | solution.py:12
  44.3 1.6 copy-start.3
  46.9 7.8 %collective-permute-start.3 = (f32[32,128]{1,0:T(8,128)S(1)}, f32[32,128]{1,0:T(8,128)S(1)}, u32[]{:S(2)}, u32[]{:S(2)}) collective-permute-start(f32[32,128]{1,0:T(8,128)S(1)} %slice_add_fusion.24), channel_id=1, source_target_pairs={{0,8},{8,16},{16,24},{24,32},{32,40},{40,48},{48,56},{56,64},{64,7... | collective-permute-start | bytes 49160 | tf_op jit(solution)/shard_map/ppermute | solution.py:12
  55.5 4.4 %collective-permute-start.4 = (bf16[32,128]{1,0:T(8,128)(2,1)S(1)}, bf16[32,128]{1,0:T(8,128)(2,1)S(1)}, u32[]{:S(2)}, u32[]{:S(2)}) collective-permute-start(bf16[32,128]{1,0:T(8,128)(2,1)S(1)} %fusion.166), channel_id=1, source_target_pairs={{0,1016},{8,0},{16,8},{24,16},{32,24},{40,32},{48,40},{56,48},{64,... | collective-permute-start | bytes 24584 | tf_op jit(solution)/shard_map/ppermute | solution.py:12
  61.1 1.6 copy-start.4
  63.7 7.8 %collective-permute-start.5 = (f32[32,128]{1,0:T(8,128)S(1)}, f32[32,128]{1,0:T(8,128)S(1)}, u32[]{:S(2)}, u32[]{:S(2)}) collective-permute-start(f32[32,128]{1,0:T(8,128)S(1)} %slice_add_fusion.20), channel_id=1, source_target_pairs={{0,8},{8,16},{16,24},{24,32},{32,40},{40,48},{48,56},{56,64},{64,7... | collective-permute-start | bytes 49160 | tf_op jit(solution)/shard_map/ppermute | solution.py:12
  71.5 4.7 %collective-permute-start.6 = (bf16[32,128]{1,0:T(8,128)(2,1)S(1)}, bf16[32,128]{1,0:T(8,128)(2,1)S(1)}, u32[]{:S(2)}, u32[]{:S(2)}) collective-permute-start(bf16[32,128]{1,0:T(8,128)(2,1)S(1)} %get-tuple-element.36), channel_id=1, source_target_pairs={{0,1016},{8,0},{16,8},{24,16},{32,24},{40,32},{48,40},{56,48},{64,... | collective-permute-start | bytes 24584 | tf_op jit(solution)/shard_map/ppermute | solution.py:12
  77.4 3.5 %copy-start.5 = (pred[1458,1152]{1,0:T(8,128)(4,1)S(1)}, pred[1458,1152]{1,0:T(8,128)(4,1)}, u32[]{:S(2)}) copy-start(pred[1458,1152]{1,0:T(8,128)(4,1)} %copy-done.1) | copy-start | bytes 5038852
  78.8 7.8 %collective-permute-start.7 = (f32[32,128]{1,0:T(8,128)S(1)}, f32[32,128]{1,0:T(8,128)S(1)}, u32[]{:S(2)}, u32[]{:S(2)}) collective-permute-start(f32[32,128]{1,0:T(8,128)S(1)} %slice_add_fusion.16), channel_id=1, source_target_pairs={{0,8},{8,16},{16,24},{24,32},{32,40},{40,48},{48,56},{56,64},{64,7... | collective-permute-start | bytes 49160 | tf_op jit(solution)/shard_map/ppermute | solution.py:12
  109.5 4.7 %collective-permute-start.8 = (f32[32,256]{1,0:T(8,128)S(1)}, f32[32,256]{1,0:T(8,128)S(1)}, u32[]{:S(2)}, u32[]{:S(2)}) collective-permute-start(f32[32,256]{1,0:T(8,128)S(1)} %fusion.205), channel_id=1, source_target_pairs={{0,8},{8,0},{16,24},{24,16},{32,40},{40,32},{48,56},{56,48},{64,72... | collective-permute-start | bytes 98312 | tf_op jit(solution)/shard_map/ppermute | solution.py:94
  114.2 5.9 %collective-permute-start.9 = (f32[32,256]{1,0:T(8,128)S(1)}, f32[32,256]{1,0:T(8,128)S(1)}, u32[]{:S(2)}, u32[]{:S(2)}) collective-permute-start(f32[32,256]{1,0:T(8,128)S(1)} %add.191), channel_id=1, source_target_pairs={{0,24},{8,16},{16,8},{24,0},{32,56},{40,48},{48,40},{56,32},{64,88... | collective-permute-start | bytes 98312 | tf_op jit(solution)/shard_map/ppermute | solution.py:94
  120.0 4.6 %collective-permute-start.10 = (f32[32,256]{1,0:T(8,128)S(1)}, f32[32,256]{1,0:T(8,128)S(1)}, u32[]{:S(2)}, u32[]{:S(2)}) collective-permute-start(f32[32,256]{1,0:T(8,128)S(1)} %add.192), channel_id=1, source_target_pairs={{0,32},{8,40},{16,48},{24,56},{32,0},{40,8},{48,16},{56,24},{64,96... | collective-permute-start | bytes 98312 | tf_op jit(solution)/shard_map/ppermute | solution.py:97
  124.7 5.6 %collective-permute-start.11 = (f32[32,256]{1,0:T(8,128)S(1)}, f32[32,256]{1,0:T(8,128)S(1)}, u32[]{:S(2)}, u32[]{:S(2)}) collective-permute-start(f32[32,256]{1,0:T(8,128)S(1)} %add.193), channel_id=1, source_target_pairs={{0,64},{8,72},{16,80},{24,88},{32,96},{40,104},{48,112},{56,120},{... | collective-permute-start | bytes 98312 | tf_op jit(solution)/shard_map/ppermute | solution.py:97
  130.3 9.0 %collective-permute-start.12 = (f32[32,256]{1,0:T(8,128)S(1)}, f32[32,256]{1,0:T(8,128)S(1)}, u32[]{:S(2)}, u32[]{:S(2)}) collective-permute-start(f32[32,256]{1,0:T(8,128)S(1)} %add.194), channel_id=1, source_target_pairs={{0,128},{8,136},{16,144},{24,152},{32,160},{40,168},{48,176},{56,1... | collective-permute-start | bytes 98312 | tf_op jit(solution)/shard_map/ppermute | solution.py:97
  139.3 14.5 %collective-permute-start.13 = (f32[32,256]{1,0:T(8,128)S(1)}, f32[32,256]{1,0:T(8,128)S(1)}, u32[]{:S(2)}, u32[]{:S(2)}) collective-permute-start(f32[32,256]{1,0:T(8,128)S(1)} %add.195), channel_id=1, source_target_pairs={{0,256},{8,264},{16,272},{24,280},{32,288},{40,296},{48,304},{56,3... | collective-permute-start | bytes 98312 | tf_op jit(solution)/shard_map/ppermute | solution.py:97
  153.8 13.4 %collective-permute-start.14 = (f32[32,256]{1,0:T(8,128)S(1)}, f32[32,256]{1,0:T(8,128)S(1)}, u32[]{:S(2)}, u32[]{:S(2)}) collective-permute-start(f32[32,256]{1,0:T(8,128)S(1)} %add.196), channel_id=1, source_target_pairs={{0,768},{8,776},{16,784},{24,792},{32,800},{40,808},{48,816},{56,8... | collective-permute-start | bytes 98312 | tf_op jit(solution)/shard_map/ppermute | solution.py:97

commit v7 on v5

--- a/solution.py
+++ b/solution.py
@@ -35,29 +35,58 @@
     return pick, owner
 
 
-def apply_filter(wave_block, cell_matrices, pick, owner):
+def plane_coupling(cell_matrices, pick, node_count):
+    cell_count, cell_nodes, _ = cell_matrices.shape
+    plane_pick = pick[:, node_count:]
+    plane_count = plane_pick.shape[1]
+    per_cell = plane_pick.reshape(cell_count, cell_nodes, plane_count)
+    halfway = jnp.einsum("clq,clm->qcm", per_cell, cell_matrices, preferred_element_type=jnp.float32)
+    halfway = halfway.reshape(plane_count, cell_count * cell_nodes)
+    coupling = sum_three(jnp.dot(split_three(halfway), plane_pick, preferred_element_type=jnp.float32))
+    return split_three(coupling).reshape(3, plane_count, plane_count)
+
+
+def apply_filter(wave_block, cell_matrices, pick, owner, coupling):
     column_count = wave_block.shape[0]
     node_count = wave_block.shape[1]
     cell_count, cell_nodes, _ = cell_matrices.shape
+    contract_nodes = (((1,), (1,)), ((), ()))
     own_plane = jnp.dot(wave_block, owner, preferred_element_type=jnp.float32).astype(jnp.bfloat16)
     upper_plane = from_behind(own_plane, "space", -1)
-    contract_nodes = (((1,), (1,)), ((), ()))
-    gathered = lax.dot_general(
+    from_own = lax.dot_general(
         wave_block, pick[:, :node_count], contract_nodes, preferred_element_type=jnp.float32
-    ) + lax.dot_general(
+    ).astype(jnp.bfloat16)
+    own_products = jnp.einsum(
+        "bcn,cnm->bcm",
+        from_own.reshape(column_count, cell_count, cell_nodes),
+        cell_matrices,
+        preferred_element_type=jnp.float32,
+    )
+    from_own_nodes = sum_three(
+        jnp.dot(
+            split_three(own_products.reshape(column_count, cell_count * cell_nodes)),
+            pick[:, node_count:],
+            preferred_element_type=jnp.float32,
+        )
+    )
+    coupled = jnp.einsum("bq,kqp->kbp", upper_plane, coupling, preferred_element_type=jnp.float32)
+    plane_part = from_own_nodes + ((coupled[0] + coupled[1]) + coupled[2])
+    returned = from_behind(plane_part, "space", 1)
+    from_upper = lax.dot_general(
         upper_plane, pick[:, node_count:], contract_nodes, preferred_element_type=jnp.float32
+    ).astype(jnp.bfloat16)
+    products = jnp.einsum(
+        "bcn,cnm->bcm",
+        (from_own + from_upper).reshape(column_count, cell_count, cell_nodes),
+        cell_matrices,
+        preferred_element_type=jnp.float32,
     )
-    gathered = gathered.astype(jnp.bfloat16).reshape(column_count, cell_count, cell_nodes)
-    products = jnp.einsum(
-        "bcn,cnm->bcm", gathered, cell_matrices, preferred_element_type=jnp.float32
-    )
-    stacked = split_three(products.reshape(column_count, cell_count * cell_nodes))
-    plane_part = sum_three(
-        jnp.dot(stacked, pick[:, node_count:], preferred_element_type=jnp.float32)
-    )
-    returned = from_behind(plane_part, "space", 1)
     local_part = sum_three(
-        jnp.dot(stacked, pick[:, :node_count], preferred_element_type=jnp.float32)
+        jnp.dot(
+            split_three(products.reshape(column_count, cell_count * cell_nodes)),
+            pick[:, :node_count],
+            preferred_element_type=jnp.float32,
+        )
     )
     back = sum_three(
         lax.dot_general(split_three(returned), owner, contract_nodes, preferred_element_type=jnp.float32)
@@ -114,11 +143,12 @@
 
 def body(wavefunctions, filter_cells, connectivity, owner_list):
     pick, owner = selectors(connectivity, owner_list, wavefunctions.shape[1])
+    coupling = plane_coupling(filter_cells, pick, wavefunctions.shape[1])
     previous = wavefunctions.astype(jnp.float32)
-    current = apply_filter(wavefunctions, filter_cells, pick, owner)
+    current = apply_filter(wavefunctions, filter_cells, pick, owner, coupling)
     for degree_step in range(DEGREE - 1):
         following = (
-            2.0 * apply_filter(current.astype(jnp.bfloat16), filter_cells, pick, owner)
+            2.0 * apply_filter(current.astype(jnp.bfloat16), filter_cells, pick, owner, coupling)
             - previous
         )
         previous, current = (current, following)

time: 192 us -> 202 us (1.052)
  matrix products: 25 us -> 40 us
  waiting for transfers between devices: 63.3 us -> 50.3 us
  starting transfers between devices: 53.5 us -> 60.2 us
  local copies, waits for them, and re-layouts: 2.99 us -> 7.26 us
  blocking collectives: 42.4 us -> 38.7 us
    ppermute x8, waiting for transfers between devices: 24.2 us -> 11.2 us  [from_behind(): lax.ppermute(shard, axis, [(i, (i + by) % peers) for i in range(peers)])]
    dot_general x12 -> x22, matrix products: 11 us -> 22.3 us  [the longest x4 9.83 us: apply_filter(): jnp.dot(split_three(products.reshape(column_count, cell_count * cell_node...]
    ppermute x8, starting transfers between devices: 35 us -> 41.7 us  [from_behind(): lax.ppermute(shard, axis, [(i, (i + by) % peers) for i in range(peers)])]
    all_gather x1, blocking collectives: 22.2 us -> 18.2 us  [body(): every_column = lax.all_gather(filtered, 'wave', axis=0, tiled=True)]
    dot_general x4, matrix products: 1.01 us -> 4.69 us  [apply_filter(): lax.dot_general(upper_plane, pick[:, node_count:], contract_nodes, prefer...]
    reshape x4 -> x14, local copies, waits for them, and re-layouts: 0.61 us -> 3.21 us  [the longest x1 1.17 us: plane_coupling(): halfway = halfway.reshape(plane_count, cell_count * cell_nodes)]
  transfers between devices with their start and end apart: 15 -> 15, of which waited for: 14 -> 11; matrix products, arithmetic and copies ran while one was open for 5% -> 14% of each run, Pallas kernels for 0% -> 0%
where the time goes in v7:
time: 202 us; the launch traced here: 201 us
  starting transfers between devices  60.2 us (30%)
  waiting for transfers between devices  50.3 us (25%)
  matrix products  40 us (20%)
  blocking collectives  38.7 us (19%)
  local copies, waits for them, and re-layouts  7.26 us (4%)
  other arithmetic  3.07 us (2%)
    ppermute x8, starting transfers between devices, from_behind(): lax.ppermute(shard, axis, [(i, (i + by) % peers) for i in range(peers)])  41.7 us
    ppermute x7, waiting for transfers between devices, butterfly_sum(): block = block + lax.ppermute(block, axis, pairs)  39.1 us
    all_gather x1, blocking collectives, body(): margin = lax.all_gather(own_rows, 'wave', axis=0, tiled=True) / node_total  20.4 us
    ppermute x7, starting transfers between devices, butterfly_sum(): block = block + lax.ppermute(block, axis, pairs)  18.5 us
    all_gather x1, blocking collectives, body(): every_column = lax.all_gather(filtered, 'wave', axis=0, tiled=True)  18.2 us
    ppermute x8, waiting for transfers between devices, from_behind(): lax.ppermute(shard, axis, [(i, (i + by) % peers) for i in range(peers)])  11.2 us
    dot_general x4, matrix products, apply_filter(): jnp.dot(split_three(products.reshape(column_count, cell_count * cell_node...  9.83 us
    dot_general x4, matrix products, apply_filter(): lax.dot_general(upper_plane, pick[:, node_count:], contract_nodes, prefer...  4.69 us
  transfers between devices with their start and end apart: 15, of which 11 were waited for; matrix products, arithmetic and copies ran while one was open for 14% of the time, Pallas kernels for 0%

profile of v7, /device:TPU:1, one launch (start us, length us, event | category | flops | bytes accessed | tf_op | source)
XLA Modules:
  0.0 200.9 jit_solution(14358737275239827542)
XLA Ops:
  1.4 21.4 %collective-permute-start = (bf16[32,128]{1,0:T(8,128)(2,1)S(1)}, bf16[32,128]{1,0:T(8,128)(2,1)S(1)}, u32[]{:S(2)}, u32[]{:S(2)}) collective-permute-start(bf16[32,128]{1,0:T(8,128)(2,1)S(1)} %fusion.43), channel_id=1, source_target_pairs={{0,1016},{8,0},{16,8},{24,16},{32,24},{40,32},{48,40},{56,48},{64,... | collective-permute-start | bytes 24584 | tf_op jit(solution)/shard_map/ppermute | solution.py:12
  27.4 1.9 convolution_bitcast_fusion
  34.5 1.9 collective-permute-start.1
  38.7 2.5 %fusion.48 = f32[96,1024]{1,0:T(8,128)S(1)} fusion(bf16[32,1458]{1,0:T(8,128)(2,1)S(1)} %get-tuple-element.29, bf16[32,1458]{1,0:T(8,128)(2,1)S(1)} %get-tuple-element.30, bf16[32,1458]{1,0:T(8,128)(2,1)S(1)} %get-tuple-element.28, pred[1458,1152]{1,0:T(8,128)(4,1)} %copy-done.1), kind=kOutput, calls=%fused_computation.69 | convolution fusion | flops 287494272 | bytes 2172288 | tf_op jit(solution)/shard_map/dot_general | solution.py:85
  44.1 5.6 %collective-permute-start.2 = (bf16[32,128]{1,0:T(8,128)(2,1)S(1)}, bf16[32,128]{1,0:T(8,128)(2,1)S(1)}, u32[]{:S(2)}, u32[]{:S(2)}) collective-permute-start(bf16[32,128]{1,0:T(8,128)(2,1)S(1)} %fusion.34), channel_id=1, source_target_pairs={{0,1016},{8,0},{16,8},{24,16},{32,24},{40,32},{48,40},{56,48},{64,... | collective-permute-start | bytes 24584 | tf_op jit(solution)/shard_map/ppermute | solution.py:12
  54.3 2.1 %collective-permute-start.3 = (f32[32,128]{1,0:T(8,128)S(1)}, f32[32,128]{1,0:T(8,128)S(1)}, u32[]{:S(2)}, u32[]{:S(2)}) collective-permute-start(f32[32,128]{1,0:T(8,128)S(1)} %fusion.201), channel_id=1, source_target_pairs={{0,8},{8,16},{16,24},{24,32},{32,40},{40,48},{48,56},{56,64},{64,7... | collective-permute-start | bytes 49160 | tf_op jit(solution)/shard_map/ppermute | solution.py:12
  56.4 2.5 %fusion.60 = f32[96,1024]{1,0:T(8,128)S(1)} fusion(bf16[32,1458]{1,0:T(8,128)(2,1)S(1)} %get-tuple-element.23, bf16[32,1458]{1,0:T(8,128)(2,1)S(1)} %get-tuple-element.24, bf16[32,1458]{1,0:T(8,128)(2,1)S(1)} %get-tuple-element.22, pred[1458,1152]{1,0:T(8,128)(4,1)} %copy-done.1), kind=kOutput, calls=%fused_computation.81 | convolution fusion | flops 287494272 | bytes 2172288 | tf_op jit(solution)/shard_map/dot_general | solution.py:85
  58.9 3.2 %collective-permute-done.3 = f32[32,128]{1,0:T(8,128)S(1)} collective-permute-done((f32[32,128]{1,0:T(8,128)S(1)}, f32[32,128]{1,0:T(8,128)S(1)}, u32[]{:S(2)}, u32[]{:S(2)}) %collective-permute-start.3) | collective-permute-done | bytes 16416 | tf_op jit(solution)/shard_map/ppermute | solution.py:12
  63.9 3.5 %collective-permute-start.4 = (bf16[32,128]{1,0:T(8,128)(2,1)S(1)}, bf16[32,128]{1,0:T(8,128)(2,1)S(1)}, u32[]{:S(2)}, u32[]{:S(2)}) collective-permute-start(bf16[32,128]{1,0:T(8,128)(2,1)S(1)} %fusion.37), channel_id=1, source_target_pairs={{0,1016},{8,0},{16,8},{24,16},{32,24},{40,32},{48,40},{56,48},{64,... | collective-permute-start | bytes 24584 | tf_op jit(solution)/shard_map/ppermute | solution.py:12
  72.0 1.9 collective-permute-start.5
  74.0 2.5 %fusion.72 = f32[96,1024]{1,0:T(8,128)S(1)} fusion(bf16[32,1458]{1,0:T(8,128)(2,1)S(1)} %get-tuple-element.17, bf16[32,1458]{1,0:T(8,128)(2,1)S(1)} %get-tuple-element.18, bf16[32,1458]{1,0:T(8,128)(2,1)S(1)} %get-tuple-element.16, pred[1458,1152]{1,0:T(8,128)(4,1)} %copy-done.1), kind=kOutput, calls=%fused_computation.93 | convolution fusion | flops 287494272 | bytes 2172288 | tf_op jit(solution)/shard_map/dot_general | solution.py:85
  76.5 3.4 %collective-permute-done.5 = f32[32,128]{1,0:T(8,128)S(1)} collective-permute-done((f32[32,128]{1,0:T(8,128)S(1)}, f32[32,128]{1,0:T(8,128)S(1)}, u32[]{:S(2)}, u32[]{:S(2)}) %collective-permute-start.5) | collective-permute-done | bytes 16416 | tf_op jit(solution)/shard_map/ppermute | solution.py:12
  81.7 3.3 %collective-permute-start.6 = (bf16[32,128]{1,0:T(8,128)(2,1)S(1)}, bf16[32,128]{1,0:T(8,128)(2,1)S(1)}, u32[]{:S(2)}, u32[]{:S(2)}) collective-permute-start(bf16[32,128]{1,0:T(8,128)(2,1)S(1)} %fusion.40), channel_id=1, source_target_pairs={{0,1016},{8,0},{16,8},{24,16},{32,24},{40,32},{48,40},{56,48},{64,... | collective-permute-start | bytes 24584 | tf_op jit(solution)/shard_map/ppermute | solution.py:12
  89.6 2.0 collective-permute-start.7
  91.6 2.4 %fusion.84 = f32[96,1024]{1,0:T(8,128)S(1)} fusion(bf16[32,1458]{1,0:T(8,128)(2,1)S(1)} %get-tuple-element.11, bf16[32,1458]{1,0:T(8,128)(2,1)S(1)} %get-tuple-element.12, bf16[32,1458]{1,0:T(8,128)(2,1)S(1)} %get-tuple-element.10, pred[1458,1152]{1,0:T(8,128)(4,1)} %copy-done.1), kind=kOutput, calls=%fused_computation.105 | convolution fusion | flops 287494272 | bytes 2172288 | tf_op jit(solution)/shard_map/dot_general | solution.py:85
  93.9 3.4 %collective-permute-done.7 = f32[32,128]{1,0:T(8,128)S(1)} collective-permute-done((f32[32,128]{1,0:T(8,128)S(1)}, f32[32,128]{1,0:T(8,128)S(1)}, u32[]{:S(2)}, u32[]{:S(2)}) %collective-permute-start.7) | collective-permute-done | bytes 16416 | tf_op jit(solution)/shard_map/ppermute | solution.py:12
  97.8 18.2 %all_gather.6 = bf16[256,1024]{1,0:T(8,128)(2,1)S(1)} all-gather(bf16[32,1024]{1,0:T(8,128)(2,1)S(1)} %fusion.142), channel_id=1, replica_groups=mesh['space'=128,'wave'=8] {'wave'}, dimensions={0}, use_global_device_ids=true | all-gather | bytes 589824 | tf_op jit(solution)/shard_map/all_gather | solution.py:158
  116.3 1.9 collective-permute-start.8
  118.2 2.7 %collective-permute-done.8 = f32[32,256]{1,0:T(8,128)S(1)} collective-permute-done((f32[32,256]{1,0:T(8,128)S(1)}, f32[32,256]{1,0:T(8,128)S(1)}, u32[]{:S(2)}, u32[]{:S(2)}) %collective-permute-start.8) | collective-permute-done | bytes 32800 | tf_op jit(solution)/shard_map/ppermute | solution.py:121
  121.0 1.9 collective-permute-start.9
  122.9 3.9 %collective-permute-done.9 = f32[32,256]{1,0:T(8,128)S(1)} collective-permute-done((f32[32,256]{1,0:T(8,128)S(1)}, f32[32,256]{1,0:T(8,128)S(1)}, u32[]{:S(2)}, u32[]{:S(2)}) %collective-permute-start.9) | collective-permute-done | bytes 32800 | tf_op jit(solution)/shard_map/ppermute | solution.py:121
  126.8 1.9 collective-permute-start.10
  128.8 2.7 %collective-permute-done.10 = f32[32,256]{1,0:T(8,128)S(1)} collective-permute-done((f32[32,256]{1,0:T(8,128)S(1)}, f32[32,256]{1,0:T(8,128)S(1)}, u32[]{:S(2)}, u32[]{:S(2)}) %collective-permute-start.10) | collective-permute-done | bytes 32800 | tf_op jit(solution)/shard_map/ppermute | solution.py:124
  131.5 1.9 collective-permute-start.11
  133.4 3.7 %collective-permute-done.11 = f32[32,256]{1,0:T(8,128)S(1)} collective-permute-done((f32[32,256]{1,0:T(8,128)S(1)}, f32[32,256]{1,0:T(8,128)S(1)}, u32[]{:S(2)}, u32[]{:S(2)}) %collective-permute-start.11) | collective-permute-done | bytes 32800 | tf_op jit(solution)/shard_map/ppermute | solution.py:124
  137.1 1.9 collective-permute-start.12
  139.0 7.1 %collective-permute-done.12 = f32[32,256]{1,0:T(8,128)S(1)} collective-permute-done((f32[32,256]{1,0:T(8,128)S(1)}, f32[32,256]{1,0:T(8,128)S(1)}, u32[]{:S(2)}, u32[]{:S(2)}) %collective-permute-start.12) | collective-permute-done | bytes 32800 | tf_op jit(solution)/shard_map/ppermute | solution.py:124
  146.1 1.9 collective-permute-start.13
  148.0 12.6 %collective-permute-done.13 = f32[32,256]{1,0:T(8,128)S(1)} collective-permute-done((f32[32,256]{1,0:T(8,128)S(1)}, f32[32,256]{1,0:T(8,128)S(1)}, u32[]{:S(2)}, u32[]{:S(2)}) %collective-permute-start.13) | collective-permute-done | bytes 32800 | tf_op jit(solution)/shard_map/ppermute | solution.py:124
  160.6 7.0 %collective-permute-start.14 = (f32[32,256]{1,0:T(8,128)S(1)}, f32[32,256]{1,0:T(8,128)S(1)}, u32[]{:S(2)}, u32[]{:S(2)}) collective-permute-start(f32[32,256]{1,0:T(8,128)S(1)} %add.236), channel_id=1, source_target_pairs={{0,768},{8,776},{16,784},{24,792},{32,800},{40,808},{48,816},{56,8... | collective-permute-start | bytes 98312 | tf_op jit(solution)/shard_map/ppermute | solution.py:124
  167.7 6.3 %collective-permute-done.14 = f32[32,256]{1,0:T(8,128)S(1)} collective-permute-done((f32[32,256]{1,0:T(8,128)S(1)}, f32[32,256]{1,0:T(8,128)S(1)}, u32[]{:S(2)}, u32[]{:S(2)}) %collective-permute-start.14) | collective-permute-done | bytes 32800 | tf_op jit(solution)/shard_map/ppermute | solution.py:124
  174.0 20.4 %all_gather.7 = f32[256,256]{1,0:T(8,128)S(1)} all-gather(f32[32,256]{1,0:T(8,128)S(1)} %add.237), channel_id=1, replica_groups=mesh['space'=128,'wave'=8] {'wave'}, dimensions={0}, use_global_device_ids=true | all-gather | bytes 294912 | tf_op jit(solution)/shard_map/all_gather | solution.py:161
  (127 shorter events, 39.7 us)
Async XLA Ops:
  0.0 27.3 %copy-start = (bf16[2,729,729]{2,0,1:T(2,128)(2,1)S(1)}, bf16[2,729,729]{2,0,1:T(2,128)(2,1)}, u32[]{:S(2)}) copy-start(bf16[2,729,729]{2,0,1:T(2,128)(2,1)} %param.5) | copy-start | bytes 6377296
  0.0 26.3 %copy-start.5 = (bf16[32,1024]{1,0:T(8,128)(2,1)S(1)}, bf16[32,1024]{1,0:T(8,128)(2,1)}, u32[]{:S(2)}) copy-start(bf16[32,1024]{1,0:T(8,128)(2,1)} %param.4) | copy-start | bytes 196612
  1.4 33.0 %collective-permute-start = (bf16[32,128]{1,0:T(8,128)(2,1)S(1)}, bf16[32,128]{1,0:T(8,128)(2,1)S(1)}, u32[]{:S(2)}, u32[]{:S(2)}) collective-permute-start(bf16[32,128]{1,0:T(8,128)(2,1)S(1)} %fusion.43), channel_id=1, source_target_pairs={{0,1016},{8,0},{16,8},{24,16},{32,24},{40,32},{48,40},{56,48},{64,... | collective-permute-start | bytes 24584 | tf_op jit(solution)/shard_map/ppermute | solution.py:12
  25.0 1.2 copy-start.1
  34.5 7.8 %collective-permute-start.1 = (f32[32,128]{1,0:T(8,128)S(1)}, f32[32,128]{1,0:T(8,128)S(1)}, u32[]{:S(2)}, u32[]{:S(2)}) collective-permute-start(f32[32,128]{1,0:T(8,128)S(1)} %fusion.203), channel_id=1, source_target_pairs={{0,8},{8,16},{16,24},{24,32},{32,40},{40,48},{48,56},{56,64},{64,7... | collective-permute-start | bytes 49160 | tf_op jit(solution)/shard_map/ppermute | solution.py:12
  38.7 3.7 %copy-start.6 = (s32[128]{0:T(128)S(1)}, s32[128]{0:T(128)}, u32[]{:S(2)}) copy-start(s32[128]{0:T(128)} %param.7) | copy-start | bytes 1540
  38.7 4.1 %copy-start.2 = (pred[1458,1152]{1,0:T(8,128)(4,1)S(1)}, pred[1458,1152]{1,0:T(8,128)(4,1)}, u32[]{:S(2)}) copy-start(pred[1458,1152]{1,0:T(8,128)(4,1)} %copy-done.1) | copy-start | bytes 5038852
  44.1 7.8 %collective-permute-start.2 = (bf16[32,128]{1,0:T(8,128)(2,1)S(1)}, bf16[32,128]{1,0:T(8,128)(2,1)S(1)}, u32[]{:S(2)}, u32[]{:S(2)}) collective-permute-start(bf16[32,128]{1,0:T(8,128)(2,1)S(1)} %fusion.34), channel_id=1, source_target_pairs={{0,1016},{8,0},{16,8},{24,16},{32,24},{40,32},{48,40},{56,48},{64,... | collective-permute-start | bytes 24584 | tf_op jit(solution)/shard_map/ppermute | solution.py:12
  54.3 7.8 %collective-permute-start.3 = (f32[32,128]{1,0:T(8,128)S(1)}, f32[32,128]{1,0:T(8,128)S(1)}, u32[]{:S(2)}, u32[]{:S(2)}) collective-permute-start(f32[32,128]{1,0:T(8,128)S(1)} %fusion.201), channel_id=1, source_target_pairs={{0,8},{8,16},{16,24},{24,32},{32,40},{40,48},{48,56},{56,64},{64,7... | collective-permute-start | bytes 49160 | tf_op jit(solution)/shard_map/ppermute | solution.py:12
  56.4 6.2 %copy-start.3 = (pred[1458,1152]{1,0:T(8,128)(4,1)S(1)}, pred[1458,1152]{1,0:T(8,128)(4,1)}, u32[]{:S(2)}) copy-start(pred[1458,1152]{1,0:T(8,128)(4,1)} %copy-done.1) | copy-start | bytes 5038852
  63.9 5.7 %collective-permute-start.4 = (bf16[32,128]{1,0:T(8,128)(2,1)S(1)}, bf16[32,128]{1,0:T(8,128)(2,1)S(1)}, u32[]{:S(2)}, u32[]{:S(2)}) collective-permute-start(bf16[32,128]{1,0:T(8,128)(2,1)S(1)} %fusion.37), channel_id=1, source_target_pairs={{0,1016},{8,0},{16,8},{24,16},{32,24},{40,32},{48,40},{56,48},{64,... | collective-permute-start | bytes 24584 | tf_op jit(solution)/shard_map/ppermute | solution.py:12
  72.0 7.8 %collective-permute-start.5 = (f32[32,128]{1,0:T(8,128)S(1)}, f32[32,128]{1,0:T(8,128)S(1)}, u32[]{:S(2)}, u32[]{:S(2)}) collective-permute-start(f32[32,128]{1,0:T(8,128)S(1)} %fusion.199), channel_id=1, source_target_pairs={{0,8},{8,16},{16,24},{24,32},{32,40},{40,48},{48,56},{56,64},{64,7... | collective-permute-start | bytes 49160 | tf_op jit(solution)/shard_map/ppermute | solution.py:12
  74.0 6.3 %copy-start.4 = (pred[1458,1152]{1,0:T(8,128)(4,1)S(1)}, pred[1458,1152]{1,0:T(8,128)(4,1)}, u32[]{:S(2)}) copy-start(pred[1458,1152]{1,0:T(8,128)(4,1)} %copy-done.1) | copy-start | bytes 5038852
  81.7 5.5 %collective-permute-start.6 = (bf16[32,128]{1,0:T(8,128)(2,1)S(1)}, bf16[32,128]{1,0:T(8,128)(2,1)S(1)}, u32[]{:S(2)}, u32[]{:S(2)}) collective-permute-start(bf16[32,128]{1,0:T(8,128)(2,1)S(1)} %fusion.40), channel_id=1, source_target_pairs={{0,1016},{8,0},{16,8},{24,16},{32,24},{40,32},{48,40},{56,48},{64,... | collective-permute-start | bytes 24584 | tf_op jit(solution)/shard_map/ppermute | solution.py:12
  89.6 7.8 %collective-permute-start.7 = (f32[32,128]{1,0:T(8,128)S(1)}, f32[32,128]{1,0:T(8,128)S(1)}, u32[]{:S(2)}, u32[]{:S(2)}) collective-permute-start(f32[32,128]{1,0:T(8,128)S(1)} %fusion.197), channel_id=1, source_target_pairs={{0,8},{8,16},{16,24},{24,32},{32,40},{40,48},{48,56},{56,64},{64,7... | collective-permute-start | bytes 49160 | tf_op jit(solution)/shard_map/ppermute | solution.py:12
  116.3 4.7 %collective-permute-start.8 = (f32[32,256]{1,0:T(8,128)S(1)}, f32[32,256]{1,0:T(8,128)S(1)}, u32[]{:S(2)}, u32[]{:S(2)}) collective-permute-start(f32[32,256]{1,0:T(8,128)S(1)} %fusion.241), channel_id=1, source_target_pairs={{0,8},{8,0},{16,24},{24,16},{32,40},{40,32},{48,56},{56,48},{64,72... | collective-permute-start | bytes 98312 | tf_op jit(solution)/shard_map/ppermute | solution.py:121
  121.0 5.9 %collective-permute-start.9 = (f32[32,256]{1,0:T(8,128)S(1)}, f32[32,256]{1,0:T(8,128)S(1)}, u32[]{:S(2)}, u32[]{:S(2)}) collective-permute-start(f32[32,256]{1,0:T(8,128)S(1)} %add.231), channel_id=1, source_target_pairs={{0,24},{8,16},{16,8},{24,0},{32,56},{40,48},{48,40},{56,32},{64,88... | collective-permute-start | bytes 98312 | tf_op jit(solution)/shard_map/ppermute | solution.py:121
  126.8 4.6 %collective-permute-start.10 = (f32[32,256]{1,0:T(8,128)S(1)}, f32[32,256]{1,0:T(8,128)S(1)}, u32[]{:S(2)}, u32[]{:S(2)}) collective-permute-start(f32[32,256]{1,0:T(8,128)S(1)} %add.232), channel_id=1, source_target_pairs={{0,32},{8,40},{16,48},{24,56},{32,0},{40,8},{48,16},{56,24},{64,96... | collective-permute-start | bytes 98312 | tf_op jit(solution)/shard_map/ppermute | solution.py:124
  131.5 5.6 %collective-permute-start.11 = (f32[32,256]{1,0:T(8,128)S(1)}, f32[32,256]{1,0:T(8,128)S(1)}, u32[]{:S(2)}, u32[]{:S(2)}) collective-permute-start(f32[32,256]{1,0:T(8,128)S(1)} %add.233), channel_id=1, source_target_pairs={{0,64},{8,72},{16,80},{24,88},{32,96},{40,104},{48,112},{56,120},{... | collective-permute-start | bytes 98312 | tf_op jit(solution)/shard_map/ppermute | solution.py:124
  137.1 9.0 %collective-permute-start.12 = (f32[32,256]{1,0:T(8,128)S(1)}, f32[32,256]{1,0:T(8,128)S(1)}, u32[]{:S(2)}, u32[]{:S(2)}) collective-permute-start(f32[32,256]{1,0:T(8,128)S(1)} %add.234), channel_id=1, source_target_pairs={{0,128},{8,136},{16,144},{24,152},{32,160},{40,168},{48,176},{56,1... | collective-permute-start | bytes 98312 | tf_op jit(solution)/shard_map/ppermute | solution.py:124
  146.1 14.5 %collective-permute-start.13 = (f32[32,256]{1,0:T(8,128)S(1)}, f32[32,256]{1,0:T(8,128)S(1)}, u32[]{:S(2)}, u32[]{:S(2)}) collective-permute-start(f32[32,256]{1,0:T(8,128)S(1)} %add.235), channel_id=1, source_target_pairs={{0,256},{8,264},{16,272},{24,280},{32,288},{40,296},{48,304},{56,3... | collective-permute-start | bytes 98312 | tf_op jit(solution)/shard_map/ppermute | solution.py:124
  160.6 13.4 %collective-permute-start.14 = (f32[32,256]{1,0:T(8,128)S(1)}, f32[32,256]{1,0:T(8,128)S(1)}, u32[]{:S(2)}, u32[]{:S(2)}) collective-permute-start(f32[32,256]{1,0:T(8,128)S(1)} %add.236), channel_id=1, source_target_pairs={{0,768},{8,776},{16,784},{24,792},{32,800},{40,808},{48,816},{56,8... | collective-permute-start | bytes 98312 | tf_op jit(solution)/shard_map/ppermute | solution.py:124

commit v8 on v5

--- a/solution.py
+++ b/solution.py
@@ -102,8 +102,10 @@
     scale = jnp.sqrt(jnp.sum(margin * margin) + 1e-06)
     approx = margin / scale
     identity = jnp.eye(size_cols, dtype=jnp.float32)
-    inverse = identity
-    for iteration in range(NS_ITERS):
+    middle = 1.5 * identity - 0.5 * approx
+    approx = jnp.dot(approx, middle, precision=highest, preferred_element_type=jnp.float32)
+    inverse = middle
+    for iteration in range(NS_ITERS - 1):
         middle = 1.5 * identity - 0.5 * jnp.dot(
             inverse, approx, precision=highest, preferred_element_type=jnp.float32
         )

time: 192 us -> 191 us (level)
  no operation moved by 1% of the time
where the time goes in v8:
time: 191 us
  waiting for transfers between devices  63.3 us (33%)
  starting transfers between devices  53.5 us (28%)
  blocking collectives  42.4 us (22%)
  matrix products  24.5 us (13%)
  local copies, waits for them, and re-layouts  2.99 us (2%)
  other arithmetic  2.65 us (1%)
    ppermute x7, waiting for transfers between devices, butterfly_sum(): block = block + lax.ppermute(block, axis, pairs)  39.1 us
    ppermute x8, starting transfers between devices, from_behind(): lax.ppermute(shard, axis, [(i, (i + by) % peers) for i in range(peers)])  35 us
    ppermute x8, waiting for transfers between devices, from_behind(): lax.ppermute(shard, axis, [(i, (i + by) % peers) for i in range(peers)])  24.2 us
    all_gather x1, blocking collectives, body(): every_column = lax.all_gather(filtered, 'wave', axis=0, tiled=True)  22.2 us
    all_gather x1, blocking collectives, body(): margin = lax.all_gather(own_rows, 'wave', axis=0, tiled=True) / node_total  20.2 us
    ppermute x7, starting transfers between devices, butterfly_sum(): block = block + lax.ppermute(block, axis, pairs)  18.5 us
    dot_general x4, matrix products, apply_filter(): jnp.dot(stacked, pick[:, node_count:], preferred_element_type=jnp.float32)  5.13 us
    dot_general x4, matrix products, apply_filter(): jnp.dot(stacked, pick[:, :node_count], preferred_element_type=jnp.float32)  3.89 us
  transfers between devices with their start and end apart: 15, of which 14 were waited for; matrix products, arithmetic and copies ran while one was open for 5% of the time, Pallas kernels for 0%

profile of v8, /device:TPU:1, one launch (start us, length us, event | category | flops | bytes accessed | tf_op | source)
XLA Modules:
  0.0 190.7 jit_solution(12936526677705835796)
XLA Ops:
  1.5 21.4 %collective-permute-start = (bf16[32,128]{0,1:T(8,128)(2,1)S(1)}, bf16[32,128]{0,1:T(8,128)(2,1)S(1)}, u32[]{:S(2)}, u32[]{:S(2)}) collective-permute-start(bf16[32,128]{0,1:T(8,128)(2,1)S(1)} %fusion.41), channel_id=1, source_target_pairs={{0,1016},{8,0},{16,8},{24,16},{32,24},{40,32},{48,40},{56,48},{64,... | collective-permute-start | bytes 24584 | tf_op jit(solution)/shard_map/ppermute | solution.py:12
  23.7 1.5 iota_compare_fusion
  29.0 1.9 %collective-permute-start.1 = (f32[32,128]{1,0:T(8,128)S(1)}, f32[32,128]{1,0:T(8,128)S(1)}, u32[]{:S(2)}, u32[]{:S(2)}) collective-permute-start(f32[32,128]{1,0:T(8,128)S(1)} %slice_add_fusion.22), channel_id=1, source_target_pairs={{0,8},{8,16},{16,24},{24,32},{32,40},{40,48},{48,56},{56,64},{64,7... | collective-permute-start | bytes 49160 | tf_op jit(solution)/shard_map/ppermute | solution.py:12
  31.9 4.9 %collective-permute-done.1 = f32[32,128]{1,0:T(8,128)S(1)} collective-permute-done((f32[32,128]{1,0:T(8,128)S(1)}, f32[32,128]{1,0:T(8,128)S(1)}, u32[]{:S(2)}, u32[]{:S(2)}) %collective-permute-start.1) | collective-permute-done | bytes 16416 | tf_op jit(solution)/shard_map/ppermute | solution.py:12
  37.6 1.9 %collective-permute-start.2 = (bf16[32,128]{1,0:T(8,128)(2,1)S(1)}, bf16[32,128]{1,0:T(8,128)(2,1)S(1)}, u32[]{:S(2)}, u32[]{:S(2)}) collective-permute-start(bf16[32,128]{1,0:T(8,128)(2,1)S(1)} %fusion.42), channel_id=1, source_target_pairs={{0,1016},{8,0},{16,8},{24,16},{32,24},{40,32},{48,40},{56,48},{64,... | collective-permute-start | bytes 24584 | tf_op jit(solution)/shard_map/ppermute | solution.py:12
  40.5 1.5 collective-permute-done.2
  44.6 1.9 %collective-permute-start.3 = (f32[32,128]{1,0:T(8,128)S(1)}, f32[32,128]{1,0:T(8,128)S(1)}, u32[]{:S(2)}, u32[]{:S(2)}) collective-permute-start(f32[32,128]{1,0:T(8,128)S(1)} %slice_add_fusion.20), channel_id=1, source_target_pairs={{0,8},{8,16},{16,24},{24,32},{32,40},{40,48},{48,56},{56,64},{64,7... | collective-permute-start | bytes 49160 | tf_op jit(solution)/shard_map/ppermute | solution.py:12
  47.5 4.9 %collective-permute-done.3 = f32[32,128]{1,0:T(8,128)S(1)} collective-permute-done((f32[32,128]{1,0:T(8,128)S(1)}, f32[32,128]{1,0:T(8,128)S(1)}, u32[]{:S(2)}, u32[]{:S(2)}) %collective-permute-start.3) | collective-permute-done | bytes 16416 | tf_op jit(solution)/shard_map/ppermute | solution.py:12
  53.2 1.9 %collective-permute-start.4 = (bf16[32,128]{1,0:T(8,128)(2,1)S(1)}, bf16[32,128]{1,0:T(8,128)(2,1)S(1)}, u32[]{:S(2)}, u32[]{:S(2)}) collective-permute-start(bf16[32,128]{1,0:T(8,128)(2,1)S(1)} %fusion.45), channel_id=1, source_target_pairs={{0,1016},{8,0},{16,8},{24,16},{32,24},{40,32},{48,40},{56,48},{64,... | collective-permute-start | bytes 24584 | tf_op jit(solution)/shard_map/ppermute | solution.py:12
  56.1 1.5 collective-permute-done.4
  60.2 1.9 %collective-permute-start.5 = (f32[32,128]{1,0:T(8,128)S(1)}, f32[32,128]{1,0:T(8,128)S(1)}, u32[]{:S(2)}, u32[]{:S(2)}) collective-permute-start(f32[32,128]{1,0:T(8,128)S(1)} %slice_add_fusion.18), channel_id=1, source_target_pairs={{0,8},{8,16},{16,24},{24,32},{32,40},{40,48},{48,56},{56,64},{64,7... | collective-permute-start | bytes 49160 | tf_op jit(solution)/shard_map/ppermute | solution.py:12
  63.1 4.9 %collective-permute-done.5 = f32[32,128]{1,0:T(8,128)S(1)} collective-permute-done((f32[32,128]{1,0:T(8,128)S(1)}, f32[32,128]{1,0:T(8,128)S(1)}, u32[]{:S(2)}, u32[]{:S(2)}) %collective-permute-start.5) | collective-permute-done | bytes 16416 | tf_op jit(solution)/shard_map/ppermute | solution.py:12
  68.8 2.1 %collective-permute-start.6 = (bf16[32,128]{1,0:T(8,128)(2,1)S(1)}, bf16[32,128]{1,0:T(8,128)(2,1)S(1)}, u32[]{:S(2)}, u32[]{:S(2)}) collective-permute-start(bf16[32,128]{1,0:T(8,128)(2,1)S(1)} %fusion.48), channel_id=1, source_target_pairs={{0,1016},{8,0},{16,8},{24,16},{32,24},{40,32},{48,40},{56,48},{64,... | collective-permute-start | bytes 24584 | tf_op jit(solution)/shard_map/ppermute | solution.py:12
  71.9 1.6 collective-permute-done.6
  76.1 1.9 %collective-permute-start.7 = (f32[32,128]{1,0:T(8,128)S(1)}, f32[32,128]{1,0:T(8,128)S(1)}, u32[]{:S(2)}, u32[]{:S(2)}) collective-permute-start(f32[32,128]{1,0:T(8,128)S(1)} %slice_add_fusion.16), channel_id=1, source_target_pairs={{0,8},{8,16},{16,24},{24,32},{32,40},{40,48},{48,56},{56,64},{64,7... | collective-permute-start | bytes 49160 | tf_op jit(solution)/shard_map/ppermute | solution.py:12
  79.0 4.9 %collective-permute-done.7 = f32[32,128]{1,0:T(8,128)S(1)} collective-permute-done((f32[32,128]{1,0:T(8,128)S(1)}, f32[32,128]{1,0:T(8,128)S(1)}, u32[]{:S(2)}, u32[]{:S(2)}) %collective-permute-start.7) | collective-permute-done | bytes 16416 | tf_op jit(solution)/shard_map/ppermute | solution.py:12
  84.4 22.2 %all_gather.6 = bf16[256,1024]{1,0:T(8,128)(2,1)S(1)} all-gather(bf16[32,1024]{1,0:T(8,128)(2,1)S(1)} %fusion.81), channel_id=1, replica_groups=mesh['space'=128,'wave'=8] {'wave'}, dimensions={0}, use_global_device_ids=true | all-gather | bytes 589824 | tf_op jit(solution)/shard_map/all_gather | solution.py:130
  106.8 1.9 %collective-permute-start.8 = (f32[32,256]{1,0:T(8,128)S(1)}, f32[32,256]{1,0:T(8,128)S(1)}, u32[]{:S(2)}, u32[]{:S(2)}) collective-permute-start(f32[32,256]{1,0:T(8,128)S(1)} %fusion.186), channel_id=1, source_target_pairs={{0,8},{8,0},{16,24},{24,16},{32,40},{40,32},{48,56},{56,48},{64,72... | collective-permute-start | bytes 98312 | tf_op jit(solution)/shard_map/ppermute | solution.py:92
  108.7 2.7 %collective-permute-done.8 = f32[32,256]{1,0:T(8,128)S(1)} collective-permute-done((f32[32,256]{1,0:T(8,128)S(1)}, f32[32,256]{1,0:T(8,128)S(1)}, u32[]{:S(2)}, u32[]{:S(2)}) %collective-permute-start.8) | collective-permute-done | bytes 32800 | tf_op jit(solution)/shard_map/ppermute | solution.py:92
  111.5 1.9 %collective-permute-start.9 = (f32[32,256]{1,0:T(8,128)S(1)}, f32[32,256]{1,0:T(8,128)S(1)}, u32[]{:S(2)}, u32[]{:S(2)}) collective-permute-start(f32[32,256]{1,0:T(8,128)S(1)} %add.155), channel_id=1, source_target_pairs={{0,24},{8,16},{16,8},{24,0},{32,56},{40,48},{48,40},{56,32},{64,88... | collective-permute-start | bytes 98312 | tf_op jit(solution)/shard_map/ppermute | solution.py:92
  113.4 3.9 %collective-permute-done.9 = f32[32,256]{1,0:T(8,128)S(1)} collective-permute-done((f32[32,256]{1,0:T(8,128)S(1)}, f32[32,256]{1,0:T(8,128)S(1)}, u32[]{:S(2)}, u32[]{:S(2)}) %collective-permute-start.9) | collective-permute-done | bytes 32800 | tf_op jit(solution)/shard_map/ppermute | solution.py:92
  117.3 1.9 %collective-permute-start.10 = (f32[32,256]{1,0:T(8,128)S(1)}, f32[32,256]{1,0:T(8,128)S(1)}, u32[]{:S(2)}, u32[]{:S(2)}) collective-permute-start(f32[32,256]{1,0:T(8,128)S(1)} %add.156), channel_id=1, source_target_pairs={{0,32},{8,40},{16,48},{24,56},{32,0},{40,8},{48,16},{56,24},{64,96... | collective-permute-start | bytes 98312 | tf_op jit(solution)/shard_map/ppermute | solution.py:95
  119.3 2.7 %collective-permute-done.10 = f32[32,256]{1,0:T(8,128)S(1)} collective-permute-done((f32[32,256]{1,0:T(8,128)S(1)}, f32[32,256]{1,0:T(8,128)S(1)}, u32[]{:S(2)}, u32[]{:S(2)}) %collective-permute-start.10) | collective-permute-done | bytes 32800 | tf_op jit(solution)/shard_map/ppermute | solution.py:95
  122.0 1.9 %collective-permute-start.11 = (f32[32,256]{1,0:T(8,128)S(1)}, f32[32,256]{1,0:T(8,128)S(1)}, u32[]{:S(2)}, u32[]{:S(2)}) collective-permute-start(f32[32,256]{1,0:T(8,128)S(1)} %add.157), channel_id=1, source_target_pairs={{0,64},{8,72},{16,80},{24,88},{32,96},{40,104},{48,112},{56,120},{... | collective-permute-start | bytes 98312 | tf_op jit(solution)/shard_map/ppermute | solution.py:95
  123.9 3.7 %collective-permute-done.11 = f32[32,256]{1,0:T(8,128)S(1)} collective-permute-done((f32[32,256]{1,0:T(8,128)S(1)}, f32[32,256]{1,0:T(8,128)S(1)}, u32[]{:S(2)}, u32[]{:S(2)}) %collective-permute-start.11) | collective-permute-done | bytes 32800 | tf_op jit(solution)/shard_map/ppermute | solution.py:95
  127.6 1.9 %collective-permute-start.12 = (f32[32,256]{1,0:T(8,128)S(1)}, f32[32,256]{1,0:T(8,128)S(1)}, u32[]{:S(2)}, u32[]{:S(2)}) collective-permute-start(f32[32,256]{1,0:T(8,128)S(1)} %add.158), channel_id=1, source_target_pairs={{0,128},{8,136},{16,144},{24,152},{32,160},{40,168},{48,176},{56,1... | collective-permute-start | bytes 98312 | tf_op jit(solution)/shard_map/ppermute | solution.py:95
  129.5 7.1 %collective-permute-done.12 = f32[32,256]{1,0:T(8,128)S(1)} collective-permute-done((f32[32,256]{1,0:T(8,128)S(1)}, f32[32,256]{1,0:T(8,128)S(1)}, u32[]{:S(2)}, u32[]{:S(2)}) %collective-permute-start.12) | collective-permute-done | bytes 32800 | tf_op jit(solution)/shard_map/ppermute | solution.py:95
  136.6 1.9 %collective-permute-start.13 = (f32[32,256]{1,0:T(8,128)S(1)}, f32[32,256]{1,0:T(8,128)S(1)}, u32[]{:S(2)}, u32[]{:S(2)}) collective-permute-start(f32[32,256]{1,0:T(8,128)S(1)} %add.159), channel_id=1, source_target_pairs={{0,256},{8,264},{16,272},{24,280},{32,288},{40,296},{48,304},{56,3... | collective-permute-start | bytes 98312 | tf_op jit(solution)/shard_map/ppermute | solution.py:95
  138.5 12.6 %collective-permute-done.13 = f32[32,256]{1,0:T(8,128)S(1)} collective-permute-done((f32[32,256]{1,0:T(8,128)S(1)}, f32[32,256]{1,0:T(8,128)S(1)}, u32[]{:S(2)}, u32[]{:S(2)}) %collective-permute-start.13) | collective-permute-done | bytes 32800 | tf_op jit(solution)/shard_map/ppermute | solution.py:95
  151.1 7.0 %collective-permute-start.14 = (f32[32,256]{1,0:T(8,128)S(1)}, f32[32,256]{1,0:T(8,128)S(1)}, u32[]{:S(2)}, u32[]{:S(2)}) collective-permute-start(f32[32,256]{1,0:T(8,128)S(1)} %add.160), channel_id=1, source_target_pairs={{0,768},{8,776},{16,784},{24,792},{32,800},{40,808},{48,816},{56,8... | collective-permute-start | bytes 98312 | tf_op jit(solution)/shard_map/ppermute | solution.py:95
  158.2 6.3 %collective-permute-done.14 = f32[32,256]{1,0:T(8,128)S(1)} collective-permute-done((f32[32,256]{1,0:T(8,128)S(1)}, f32[32,256]{1,0:T(8,128)S(1)}, u32[]{:S(2)}, u32[]{:S(2)}) %collective-permute-start.14) | collective-permute-done | bytes 32800 | tf_op jit(solution)/shard_map/ppermute | solution.py:95
  164.5 20.2 %all_gather.7 = f32[256,256]{1,0:T(8,128)S(1)} all-gather(f32[32,256]{1,0:T(8,128)S(1)} %add.161), channel_id=1, replica_groups=mesh['space'=128,'wave'=8] {'wave'}, dimensions={0}, use_global_device_ids=true | all-gather | bytes 294912 | tf_op jit(solution)/shard_map/all_gather | solution.py:133
  (94 shorter events, 28.7 us)
Async XLA Ops:
  0.0 26.8 %copy-start = (bf16[2,729,729]{2,0,1:T(2,128)(2,1)S(1)}, bf16[2,729,729]{2,0,1:T(2,128)(2,1)}, u32[]{:S(2)}) copy-start(bf16[2,729,729]{2,0,1:T(2,128)(2,1)} %param.5) | copy-start | bytes 6377296
  0.0 25.1 %copy-start.6 = (bf16[32,1024]{1,0:T(8,128)(2,1)S(1)}, bf16[32,1024]{1,0:T(8,128)(2,1)}, u32[]{:S(2)}) copy-start(bf16[32,1024]{1,0:T(8,128)(2,1)} %param.4) | copy-start | bytes 196612
  1.5 24.7 %collective-permute-start = (bf16[32,128]{0,1:T(8,128)(2,1)S(1)}, bf16[32,128]{0,1:T(8,128)(2,1)S(1)}, u32[]{:S(2)}, u32[]{:S(2)}) collective-permute-start(bf16[32,128]{0,1:T(8,128)(2,1)S(1)} %fusion.41), channel_id=1, source_target_pairs={{0,1016},{8,0},{16,8},{24,16},{32,24},{40,32},{48,40},{56,48},{64,... | collective-permute-start | bytes 24584 | tf_op jit(solution)/shard_map/ppermute | solution.py:12
  25.1 1.2 copy-start.1
  27.6 3.3 %copy-start.2 = (pred[1458,1152]{1,0:T(8,128)(4,1)S(1)}, pred[1458,1152]{1,0:T(8,128)(4,1)}, u32[]{:S(2)}) copy-start(pred[1458,1152]{1,0:T(8,128)(4,1)} %copy-done.1) | copy-start | bytes 5038852
  29.0 7.8 %copy-start.7 = (s32[128]{0:T(128)S(1)}, s32[128]{0:T(128)}, u32[]{:S(2)}) copy-start(s32[128]{0:T(128)} %param.7) | copy-start | bytes 1540
  29.0 7.8 %collective-permute-start.1 = (f32[32,128]{1,0:T(8,128)S(1)}, f32[32,128]{1,0:T(8,128)S(1)}, u32[]{:S(2)}, u32[]{:S(2)}) collective-permute-start(f32[32,128]{1,0:T(8,128)S(1)} %slice_add_fusion.22), channel_id=1, source_target_pairs={{0,8},{8,16},{16,24},{24,32},{32,40},{40,48},{48,56},{56,64},{64,7... | collective-permute-start | bytes 49160 | tf_op jit(solution)/shard_map/ppermute | solution.py:12
  37.6 4.4 %collective-permute-start.2 = (bf16[32,128]{1,0:T(8,128)(2,1)S(1)}, bf16[32,128]{1,0:T(8,128)(2,1)S(1)}, u32[]{:S(2)}, u32[]{:S(2)}) collective-permute-start(bf16[32,128]{1,0:T(8,128)(2,1)S(1)} %fusion.42), channel_id=1, source_target_pairs={{0,1016},{8,0},{16,8},{24,16},{32,24},{40,32},{48,40},{56,48},{64,... | collective-permute-start | bytes 24584 | tf_op jit(solution)/shard_map/ppermute | solution.py:12
  43.3 3.3 %copy-start.3 = (pred[1458,1152]{1,0:T(8,128)(4,1)S(1)}, pred[1458,1152]{1,0:T(8,128)(4,1)}, u32[]{:S(2)}) copy-start(pred[1458,1152]{1,0:T(8,128)(4,1)} %copy-done.1) | copy-start | bytes 5038852
  44.6 7.8 %collective-permute-start.3 = (f32[32,128]{1,0:T(8,128)S(1)}, f32[32,128]{1,0:T(8,128)S(1)}, u32[]{:S(2)}, u32[]{:S(2)}) collective-permute-start(f32[32,128]{1,0:T(8,128)S(1)} %slice_add_fusion.20), channel_id=1, source_target_pairs={{0,8},{8,16},{16,24},{24,32},{32,40},{40,48},{48,56},{56,64},{64,7... | collective-permute-start | bytes 49160 | tf_op jit(solution)/shard_map/ppermute | solution.py:12
  53.2 4.4 %collective-permute-start.4 = (bf16[32,128]{1,0:T(8,128)(2,1)S(1)}, bf16[32,128]{1,0:T(8,128)(2,1)S(1)}, u32[]{:S(2)}, u32[]{:S(2)}) collective-permute-start(bf16[32,128]{1,0:T(8,128)(2,1)S(1)} %fusion.45), channel_id=1, source_target_pairs={{0,1016},{8,0},{16,8},{24,16},{32,24},{40,32},{48,40},{56,48},{64,... | collective-permute-start | bytes 24584 | tf_op jit(solution)/shard_map/ppermute | solution.py:12
  58.9 3.3 %copy-start.4 = (pred[1458,1152]{1,0:T(8,128)(4,1)S(1)}, pred[1458,1152]{1,0:T(8,128)(4,1)}, u32[]{:S(2)}) copy-start(pred[1458,1152]{1,0:T(8,128)(4,1)} %copy-done.1) | copy-start | bytes 5038852
  60.2 7.8 %collective-permute-start.5 = (f32[32,128]{1,0:T(8,128)S(1)}, f32[32,128]{1,0:T(8,128)S(1)}, u32[]{:S(2)}, u32[]{:S(2)}) collective-permute-start(f32[32,128]{1,0:T(8,128)S(1)} %slice_add_fusion.18), channel_id=1, source_target_pairs={{0,8},{8,16},{16,24},{24,32},{32,40},{40,48},{48,56},{56,64},{64,7... | collective-permute-start | bytes 49160 | tf_op jit(solution)/shard_map/ppermute | solution.py:12
  68.8 4.7 %collective-permute-start.6 = (bf16[32,128]{1,0:T(8,128)(2,1)S(1)}, bf16[32,128]{1,0:T(8,128)(2,1)S(1)}, u32[]{:S(2)}, u32[]{:S(2)}) collective-permute-start(bf16[32,128]{1,0:T(8,128)(2,1)S(1)} %fusion.48), channel_id=1, source_target_pairs={{0,1016},{8,0},{16,8},{24,16},{32,24},{40,32},{48,40},{56,48},{64,... | collective-permute-start | bytes 24584 | tf_op jit(solution)/shard_map/ppermute | solution.py:12
  74.8 3.3 %copy-start.5 = (pred[1458,1152]{1,0:T(8,128)(4,1)S(1)}, pred[1458,1152]{1,0:T(8,128)(4,1)}, u32[]{:S(2)}) copy-start(pred[1458,1152]{1,0:T(8,128)(4,1)} %copy-done.1) | copy-start | bytes 5038852
  76.1 7.8 %collective-permute-start.7 = (f32[32,128]{1,0:T(8,128)S(1)}, f32[32,128]{1,0:T(8,128)S(1)}, u32[]{:S(2)}, u32[]{:S(2)}) collective-permute-start(f32[32,128]{1,0:T(8,128)S(1)} %slice_add_fusion.16), channel_id=1, source_target_pairs={{0,8},{8,16},{16,24},{24,32},{32,40},{40,48},{48,56},{56,64},{64,7... | collective-permute-start | bytes 49160 | tf_op jit(solution)/shard_map/ppermute | solution.py:12
  106.8 4.7 %collective-permute-start.8 = (f32[32,256]{1,0:T(8,128)S(1)}, f32[32,256]{1,0:T(8,128)S(1)}, u32[]{:S(2)}, u32[]{:S(2)}) collective-permute-start(f32[32,256]{1,0:T(8,128)S(1)} %fusion.186), channel_id=1, source_target_pairs={{0,8},{8,0},{16,24},{24,16},{32,40},{40,32},{48,56},{56,48},{64,72... | collective-permute-start | bytes 98312 | tf_op jit(solution)/shard_map/ppermute | solution.py:92
  111.5 5.9 %collective-permute-start.9 = (f32[32,256]{1,0:T(8,128)S(1)}, f32[32,256]{1,0:T(8,128)S(1)}, u32[]{:S(2)}, u32[]{:S(2)}) collective-permute-start(f32[32,256]{1,0:T(8,128)S(1)} %add.155), channel_id=1, source_target_pairs={{0,24},{8,16},{16,8},{24,0},{32,56},{40,48},{48,40},{56,32},{64,88... | collective-permute-start | bytes 98312 | tf_op jit(solution)/shard_map/ppermute | solution.py:92
  117.3 4.6 %collective-permute-start.10 = (f32[32,256]{1,0:T(8,128)S(1)}, f32[32,256]{1,0:T(8,128)S(1)}, u32[]{:S(2)}, u32[]{:S(2)}) collective-permute-start(f32[32,256]{1,0:T(8,128)S(1)} %add.156), channel_id=1, source_target_pairs={{0,32},{8,40},{16,48},{24,56},{32,0},{40,8},{48,16},{56,24},{64,96... | collective-permute-start | bytes 98312 | tf_op jit(solution)/shard_map/ppermute | solution.py:95
  122.0 5.6 %collective-permute-start.11 = (f32[32,256]{1,0:T(8,128)S(1)}, f32[32,256]{1,0:T(8,128)S(1)}, u32[]{:S(2)}, u32[]{:S(2)}) collective-permute-start(f32[32,256]{1,0:T(8,128)S(1)} %add.157), channel_id=1, source_target_pairs={{0,64},{8,72},{16,80},{24,88},{32,96},{40,104},{48,112},{56,120},{... | collective-permute-start | bytes 98312 | tf_op jit(solution)/shard_map/ppermute | solution.py:95
  127.6 9.0 %collective-permute-start.12 = (f32[32,256]{1,0:T(8,128)S(1)}, f32[32,256]{1,0:T(8,128)S(1)}, u32[]{:S(2)}, u32[]{:S(2)}) collective-permute-start(f32[32,256]{1,0:T(8,128)S(1)} %add.158), channel_id=1, source_target_pairs={{0,128},{8,136},{16,144},{24,152},{32,160},{40,168},{48,176},{56,1... | collective-permute-start | bytes 98312 | tf_op jit(solution)/shard_map/ppermute | solution.py:95
  136.6 14.5 %collective-permute-start.13 = (f32[32,256]{1,0:T(8,128)S(1)}, f32[32,256]{1,0:T(8,128)S(1)}, u32[]{:S(2)}, u32[]{:S(2)}) collective-permute-start(f32[32,256]{1,0:T(8,128)S(1)} %add.159), channel_id=1, source_target_pairs={{0,256},{8,264},{16,272},{24,280},{32,288},{40,296},{48,304},{56,3... | collective-permute-start | bytes 98312 | tf_op jit(solution)/shard_map/ppermute | solution.py:95
  151.1 13.4 %collective-permute-start.14 = (f32[32,256]{1,0:T(8,128)S(1)}, f32[32,256]{1,0:T(8,128)S(1)}, u32[]{:S(2)}, u32[]{:S(2)}) collective-permute-start(f32[32,256]{1,0:T(8,128)S(1)} %add.160), channel_id=1, source_target_pairs={{0,768},{8,776},{16,784},{24,792},{32,800},{40,808},{48,816},{56,8... | collective-permute-start | bytes 98312 | tf_op jit(solution)/shard_map/ppermute | solution.py:95

commit v9 on v8

--- a/solution.py
+++ b/solution.py
@@ -96,7 +96,7 @@
     return block
 
 
-def newton_schulz(margin):
+def newton_schulz(margin, first_column, width):
     highest = lax.Precision.HIGHEST
     size_cols = margin.shape[0]
     scale = jnp.sqrt(jnp.sum(margin * margin) + 1e-06)
@@ -109,6 +109,8 @@
         middle = 1.5 * identity - 0.5 * jnp.dot(
             inverse, approx, precision=highest, preferred_element_type=jnp.float32
         )
+        if iteration == NS_ITERS - 2:
+            inverse = lax.dynamic_slice_in_dim(inverse, first_column, width, 1)
         approx = jnp.dot(approx, middle, precision=highest, preferred_element_type=jnp.float32)
         inverse = jnp.dot(middle, inverse, precision=highest, preferred_element_type=jnp.float32)
     return (inverse / jnp.sqrt(scale)).astype(jnp.bfloat16)
@@ -131,10 +133,7 @@
     own_rows = jnp.dot(filtered, every_column.T, preferred_element_type=jnp.float32)
     own_rows = butterfly_sum(own_rows, "space", 4)
     margin = lax.all_gather(own_rows, "wave", axis=0, tiled=True) / node_total
-    rotation = newton_schulz(margin)
-    own_rotation = lax.dynamic_slice_in_dim(
-        rotation, lax.axis_index("wave") * column_count, column_count, 1
-    )
+    own_rotation = newton_schulz(margin, lax.axis_index("wave") * column_count, column_count)
     return jnp.dot(own_rotation.T, every_column, preferred_element_type=jnp.float32).astype(
         jnp.bfloat16
     )

time: 191 us -> 192 us (level)
  no operation moved by 1% of the time
where the time goes in v9:
time: 192 us; the launch traced here: 191 us
  waiting for transfers between devices  63.3 us (33%)
  starting transfers between devices  53.5 us (28%)
  blocking collectives  42.4 us (22%)
  matrix products  24.8 us (13%)
  local copies, waits for them, and re-layouts  2.99 us (2%)
  other arithmetic  2.65 us (1%)
    ppermute x7, waiting for transfers between devices, butterfly_sum(): block = block + lax.ppermute(block, axis, pairs)  39.1 us
    ppermute x8, starting transfers between devices, from_behind(): lax.ppermute(shard, axis, [(i, (i + by) % peers) for i in range(peers)])  35 us
    ppermute x8, waiting for transfers between devices, from_behind(): lax.ppermute(shard, axis, [(i, (i + by) % peers) for i in range(peers)])  24.2 us
    all_gather x1, blocking collectives, body(): every_column = lax.all_gather(filtered, 'wave', axis=0, tiled=True)  22.2 us
    all_gather x1, blocking collectives, body(): margin = lax.all_gather(own_rows, 'wave', axis=0, tiled=True) / node_total  20.2 us
    ppermute x7, starting transfers between devices, butterfly_sum(): block = block + lax.ppermute(block, axis, pairs)  18.5 us
    dot_general x4, matrix products, apply_filter(): jnp.dot(stacked, pick[:, node_count:], preferred_element_type=jnp.float32)  5.13 us
    dot_general x4, matrix products, apply_filter(): jnp.dot(stacked, pick[:, :node_count], preferred_element_type=jnp.float32)  3.89 us
  transfers between devices with their start and end apart: 15, of which 14 were waited for; matrix products, arithmetic and copies ran while one was open for 5% of the time, Pallas kernels for 0%

profile of v9, /device:TPU:1, one launch (start us, length us, event | category | flops | bytes accessed | tf_op | source)
XLA Modules:
  0.0 191.0 jit_solution(3640199416372961906)
XLA Ops:
  1.5 21.4 %collective-permute-start = (bf16[32,128]{0,1:T(8,128)(2,1)S(1)}, bf16[32,128]{0,1:T(8,128)(2,1)S(1)}, u32[]{:S(2)}, u32[]{:S(2)}) collective-permute-start(bf16[32,128]{0,1:T(8,128)(2,1)S(1)} %fusion.42), channel_id=1, source_target_pairs={{0,1016},{8,0},{16,8},{24,16},{32,24},{40,32},{48,40},{56,48},{64,... | collective-permute-start | bytes 24584 | tf_op jit(solution)/shard_map/ppermute | solution.py:12
  23.7 1.5 iota_compare_fusion
  29.0 1.9 %collective-permute-start.1 = (f32[32,128]{1,0:T(8,128)S(1)}, f32[32,128]{1,0:T(8,128)S(1)}, u32[]{:S(2)}, u32[]{:S(2)}) collective-permute-start(f32[32,128]{1,0:T(8,128)S(1)} %slice_add_fusion.22), channel_id=1, source_target_pairs={{0,8},{8,16},{16,24},{24,32},{32,40},{40,48},{48,56},{56,64},{64,7... | collective-permute-start | bytes 49160 | tf_op jit(solution)/shard_map/ppermute | solution.py:12
  31.9 4.9 %collective-permute-done.1 = f32[32,128]{1,0:T(8,128)S(1)} collective-permute-done((f32[32,128]{1,0:T(8,128)S(1)}, f32[32,128]{1,0:T(8,128)S(1)}, u32[]{:S(2)}, u32[]{:S(2)}) %collective-permute-start.1) | collective-permute-done | bytes 16416 | tf_op jit(solution)/shard_map/ppermute | solution.py:12
  37.6 1.9 %collective-permute-start.2 = (bf16[32,128]{1,0:T(8,128)(2,1)S(1)}, bf16[32,128]{1,0:T(8,128)(2,1)S(1)}, u32[]{:S(2)}, u32[]{:S(2)}) collective-permute-start(bf16[32,128]{1,0:T(8,128)(2,1)S(1)} %fusion.43), channel_id=1, source_target_pairs={{0,1016},{8,0},{16,8},{24,16},{32,24},{40,32},{48,40},{56,48},{64,... | collective-permute-start | bytes 24584 | tf_op jit(solution)/shard_map/ppermute | solution.py:12
  40.5 1.5 collective-permute-done.2
  44.6 1.9 %collective-permute-start.3 = (f32[32,128]{1,0:T(8,128)S(1)}, f32[32,128]{1,0:T(8,128)S(1)}, u32[]{:S(2)}, u32[]{:S(2)}) collective-permute-start(f32[32,128]{1,0:T(8,128)S(1)} %slice_add_fusion.20), channel_id=1, source_target_pairs={{0,8},{8,16},{16,24},{24,32},{32,40},{40,48},{48,56},{56,64},{64,7... | collective-permute-start | bytes 49160 | tf_op jit(solution)/shard_map/ppermute | solution.py:12
  47.5 4.9 %collective-permute-done.3 = f32[32,128]{1,0:T(8,128)S(1)} collective-permute-done((f32[32,128]{1,0:T(8,128)S(1)}, f32[32,128]{1,0:T(8,128)S(1)}, u32[]{:S(2)}, u32[]{:S(2)}) %collective-permute-start.3) | collective-permute-done | bytes 16416 | tf_op jit(solution)/shard_map/ppermute | solution.py:12
  53.2 1.9 %collective-permute-start.4 = (bf16[32,128]{1,0:T(8,128)(2,1)S(1)}, bf16[32,128]{1,0:T(8,128)(2,1)S(1)}, u32[]{:S(2)}, u32[]{:S(2)}) collective-permute-start(bf16[32,128]{1,0:T(8,128)(2,1)S(1)} %fusion.46), channel_id=1, source_target_pairs={{0,1016},{8,0},{16,8},{24,16},{32,24},{40,32},{48,40},{56,48},{64,... | collective-permute-start | bytes 24584 | tf_op jit(solution)/shard_map/ppermute | solution.py:12
  56.1 1.5 collective-permute-done.4
  60.2 1.9 %collective-permute-start.5 = (f32[32,128]{1,0:T(8,128)S(1)}, f32[32,128]{1,0:T(8,128)S(1)}, u32[]{:S(2)}, u32[]{:S(2)}) collective-permute-start(f32[32,128]{1,0:T(8,128)S(1)} %slice_add_fusion.18), channel_id=1, source_target_pairs={{0,8},{8,16},{16,24},{24,32},{32,40},{40,48},{48,56},{56,64},{64,7... | collective-permute-start | bytes 49160 | tf_op jit(solution)/shard_map/ppermute | solution.py:12
  63.1 4.9 %collective-permute-done.5 = f32[32,128]{1,0:T(8,128)S(1)} collective-permute-done((f32[32,128]{1,0:T(8,128)S(1)}, f32[32,128]{1,0:T(8,128)S(1)}, u32[]{:S(2)}, u32[]{:S(2)}) %collective-permute-start.5) | collective-permute-done | bytes 16416 | tf_op jit(solution)/shard_map/ppermute | solution.py:12
  68.8 2.1 %collective-permute-start.6 = (bf16[32,128]{1,0:T(8,128)(2,1)S(1)}, bf16[32,128]{1,0:T(8,128)(2,1)S(1)}, u32[]{:S(2)}, u32[]{:S(2)}) collective-permute-start(bf16[32,128]{1,0:T(8,128)(2,1)S(1)} %fusion.49), channel_id=1, source_target_pairs={{0,1016},{8,0},{16,8},{24,16},{32,24},{40,32},{48,40},{56,48},{64,... | collective-permute-start | bytes 24584 | tf_op jit(solution)/shard_map/ppermute | solution.py:12
  71.9 1.6 collective-permute-done.6
  76.1 1.9 %collective-permute-start.7 = (f32[32,128]{1,0:T(8,128)S(1)}, f32[32,128]{1,0:T(8,128)S(1)}, u32[]{:S(2)}, u32[]{:S(2)}) collective-permute-start(f32[32,128]{1,0:T(8,128)S(1)} %slice_add_fusion.16), channel_id=1, source_target_pairs={{0,8},{8,16},{16,24},{24,32},{32,40},{40,48},{48,56},{56,64},{64,7... | collective-permute-start | bytes 49160 | tf_op jit(solution)/shard_map/ppermute | solution.py:12
  79.0 4.9 %collective-permute-done.7 = f32[32,128]{1,0:T(8,128)S(1)} collective-permute-done((f32[32,128]{1,0:T(8,128)S(1)}, f32[32,128]{1,0:T(8,128)S(1)}, u32[]{:S(2)}, u32[]{:S(2)}) %collective-permute-start.7) | collective-permute-done | bytes 16416 | tf_op jit(solution)/shard_map/ppermute | solution.py:12
  84.4 22.2 %all_gather.6 = bf16[256,1024]{1,0:T(8,128)(2,1)S(1)} all-gather(bf16[32,1024]{1,0:T(8,128)(2,1)S(1)} %fusion.81), channel_id=1, replica_groups=mesh['space'=128,'wave'=8] {'wave'}, dimensions={0}, use_global_device_ids=true | all-gather | bytes 589824 | tf_op jit(solution)/shard_map/all_gather | solution.py:132
  106.8 1.9 %collective-permute-start.8 = (f32[32,256]{1,0:T(8,128)S(1)}, f32[32,256]{1,0:T(8,128)S(1)}, u32[]{:S(2)}, u32[]{:S(2)}) collective-permute-start(f32[32,256]{1,0:T(8,128)S(1)} %fusion.185), channel_id=1, source_target_pairs={{0,8},{8,0},{16,24},{24,16},{32,40},{40,32},{48,56},{56,48},{64,72... | collective-permute-start | bytes 98312 | tf_op jit(solution)/shard_map/ppermute | solution.py:92
  108.7 2.7 %collective-permute-done.8 = f32[32,256]{1,0:T(8,128)S(1)} collective-permute-done((f32[32,256]{1,0:T(8,128)S(1)}, f32[32,256]{1,0:T(8,128)S(1)}, u32[]{:S(2)}, u32[]{:S(2)}) %collective-permute-start.8) | collective-permute-done | bytes 32800 | tf_op jit(solution)/shard_map/ppermute | solution.py:92
  111.5 1.9 collective-permute-start.9
  113.4 3.9 %collective-permute-done.9 = f32[32,256]{1,0:T(8,128)S(1)} collective-permute-done((f32[32,256]{1,0:T(8,128)S(1)}, f32[32,256]{1,0:T(8,128)S(1)}, u32[]{:S(2)}, u32[]{:S(2)}) %collective-permute-start.9) | collective-permute-done | bytes 32800 | tf_op jit(solution)/shard_map/ppermute | solution.py:92
  117.3 1.9 collective-permute-start.10
  119.3 2.7 %collective-permute-done.10 = f32[32,256]{1,0:T(8,128)S(1)} collective-permute-done((f32[32,256]{1,0:T(8,128)S(1)}, f32[32,256]{1,0:T(8,128)S(1)}, u32[]{:S(2)}, u32[]{:S(2)}) %collective-permute-start.10) | collective-permute-done | bytes 32800 | tf_op jit(solution)/shard_map/ppermute | solution.py:95
  122.0 1.9 collective-permute-start.11
  123.9 3.7 %collective-permute-done.11 = f32[32,256]{1,0:T(8,128)S(1)} collective-permute-done((f32[32,256]{1,0:T(8,128)S(1)}, f32[32,256]{1,0:T(8,128)S(1)}, u32[]{:S(2)}, u32[]{:S(2)}) %collective-permute-start.11) | collective-permute-done | bytes 32800 | tf_op jit(solution)/shard_map/ppermute | solution.py:95
  127.6 1.9 collective-permute-start.12
  129.5 7.1 %collective-permute-done.12 = f32[32,256]{1,0:T(8,128)S(1)} collective-permute-done((f32[32,256]{1,0:T(8,128)S(1)}, f32[32,256]{1,0:T(8,128)S(1)}, u32[]{:S(2)}, u32[]{:S(2)}) %collective-permute-start.12) | collective-permute-done | bytes 32800 | tf_op jit(solution)/shard_map/ppermute | solution.py:95
  136.6 1.9 collective-permute-start.13
  138.5 12.6 %collective-permute-done.13 = f32[32,256]{1,0:T(8,128)S(1)} collective-permute-done((f32[32,256]{1,0:T(8,128)S(1)}, f32[32,256]{1,0:T(8,128)S(1)}, u32[]{:S(2)}, u32[]{:S(2)}) %collective-permute-start.13) | collective-permute-done | bytes 32800 | tf_op jit(solution)/shard_map/ppermute | solution.py:95
  151.1 7.0 %collective-permute-start.14 = (f32[32,256]{1,0:T(8,128)S(1)}, f32[32,256]{1,0:T(8,128)S(1)}, u32[]{:S(2)}, u32[]{:S(2)}) collective-permute-start(f32[32,256]{1,0:T(8,128)S(1)} %add.160), channel_id=1, source_target_pairs={{0,768},{8,776},{16,784},{24,792},{32,800},{40,808},{48,816},{56,8... | collective-permute-start | bytes 98312 | tf_op jit(solution)/shard_map/ppermute | solution.py:95
  158.2 6.3 %collective-permute-done.14 = f32[32,256]{1,0:T(8,128)S(1)} collective-permute-done((f32[32,256]{1,0:T(8,128)S(1)}, f32[32,256]{1,0:T(8,128)S(1)}, u32[]{:S(2)}, u32[]{:S(2)}) %collective-permute-start.14) | collective-permute-done | bytes 32800 | tf_op jit(solution)/shard_map/ppermute | solution.py:95
  164.5 20.2 %all_gather.7 = f32[256,256]{1,0:T(8,128)S(1)} all-gather(f32[32,256]{1,0:T(8,128)S(1)} %add.161), channel_id=1, replica_groups=mesh['space'=128,'wave'=8] {'wave'}, dimensions={0}, use_global_device_ids=true | all-gather | bytes 294912 | tf_op jit(solution)/shard_map/all_gather | solution.py:135
  (94 shorter events, 29.0 us)
Async XLA Ops:
  0.0 26.8 %copy-start = (bf16[2,729,729]{2,0,1:T(2,128)(2,1)S(1)}, bf16[2,729,729]{2,0,1:T(2,128)(2,1)}, u32[]{:S(2)}) copy-start(bf16[2,729,729]{2,0,1:T(2,128)(2,1)} %param.5) | copy-start | bytes 6377296
  0.0 25.1 %copy-start.6 = (bf16[32,1024]{1,0:T(8,128)(2,1)S(1)}, bf16[32,1024]{1,0:T(8,128)(2,1)}, u32[]{:S(2)}) copy-start(bf16[32,1024]{1,0:T(8,128)(2,1)} %param.4) | copy-start | bytes 196612
  1.5 24.7 %collective-permute-start = (bf16[32,128]{0,1:T(8,128)(2,1)S(1)}, bf16[32,128]{0,1:T(8,128)(2,1)S(1)}, u32[]{:S(2)}, u32[]{:S(2)}) collective-permute-start(bf16[32,128]{0,1:T(8,128)(2,1)S(1)} %fusion.42), channel_id=1, source_target_pairs={{0,1016},{8,0},{16,8},{24,16},{32,24},{40,32},{48,40},{56,48},{64,... | collective-permute-start | bytes 24584 | tf_op jit(solution)/shard_map/ppermute | solution.py:12
  25.1 1.2 copy-start.1
  27.6 3.3 %copy-start.2 = (pred[1458,1152]{1,0:T(8,128)(4,1)S(1)}, pred[1458,1152]{1,0:T(8,128)(4,1)}, u32[]{:S(2)}) copy-start(pred[1458,1152]{1,0:T(8,128)(4,1)} %copy-done.1) | copy-start | bytes 5038852
  29.0 7.8 %copy-start.7 = (s32[128]{0:T(128)S(1)}, s32[128]{0:T(128)}, u32[]{:S(2)}) copy-start(s32[128]{0:T(128)} %param.7) | copy-start | bytes 1540
  29.0 7.8 %collective-permute-start.1 = (f32[32,128]{1,0:T(8,128)S(1)}, f32[32,128]{1,0:T(8,128)S(1)}, u32[]{:S(2)}, u32[]{:S(2)}) collective-permute-start(f32[32,128]{1,0:T(8,128)S(1)} %slice_add_fusion.22), channel_id=1, source_target_pairs={{0,8},{8,16},{16,24},{24,32},{32,40},{40,48},{48,56},{56,64},{64,7... | collective-permute-start | bytes 49160 | tf_op jit(solution)/shard_map/ppermute | solution.py:12
  37.6 4.4 %collective-permute-start.2 = (bf16[32,128]{1,0:T(8,128)(2,1)S(1)}, bf16[32,128]{1,0:T(8,128)(2,1)S(1)}, u32[]{:S(2)}, u32[]{:S(2)}) collective-permute-start(bf16[32,128]{1,0:T(8,128)(2,1)S(1)} %fusion.43), channel_id=1, source_target_pairs={{0,1016},{8,0},{16,8},{24,16},{32,24},{40,32},{48,40},{56,48},{64,... | collective-permute-start | bytes 24584 | tf_op jit(solution)/shard_map/ppermute | solution.py:12
  43.3 3.3 %copy-start.3 = (pred[1458,1152]{1,0:T(8,128)(4,1)S(1)}, pred[1458,1152]{1,0:T(8,128)(4,1)}, u32[]{:S(2)}) copy-start(pred[1458,1152]{1,0:T(8,128)(4,1)} %copy-done.1) | copy-start | bytes 5038852
  44.6 7.8 %collective-permute-start.3 = (f32[32,128]{1,0:T(8,128)S(1)}, f32[32,128]{1,0:T(8,128)S(1)}, u32[]{:S(2)}, u32[]{:S(2)}) collective-permute-start(f32[32,128]{1,0:T(8,128)S(1)} %slice_add_fusion.20), channel_id=1, source_target_pairs={{0,8},{8,16},{16,24},{24,32},{32,40},{40,48},{48,56},{56,64},{64,7... | collective-permute-start | bytes 49160 | tf_op jit(solution)/shard_map/ppermute | solution.py:12
  53.2 4.4 %collective-permute-start.4 = (bf16[32,128]{1,0:T(8,128)(2,1)S(1)}, bf16[32,128]{1,0:T(8,128)(2,1)S(1)}, u32[]{:S(2)}, u32[]{:S(2)}) collective-permute-start(bf16[32,128]{1,0:T(8,128)(2,1)S(1)} %fusion.46), channel_id=1, source_target_pairs={{0,1016},{8,0},{16,8},{24,16},{32,24},{40,32},{48,40},{56,48},{64,... | collective-permute-start | bytes 24584 | tf_op jit(solution)/shard_map/ppermute | solution.py:12
  58.9 3.3 %copy-start.4 = (pred[1458,1152]{1,0:T(8,128)(4,1)S(1)}, pred[1458,1152]{1,0:T(8,128)(4,1)}, u32[]{:S(2)}) copy-start(pred[1458,1152]{1,0:T(8,128)(4,1)} %copy-done.1) | copy-start | bytes 5038852
  60.2 7.8 %collective-permute-start.5 = (f32[32,128]{1,0:T(8,128)S(1)}, f32[32,128]{1,0:T(8,128)S(1)}, u32[]{:S(2)}, u32[]{:S(2)}) collective-permute-start(f32[32,128]{1,0:T(8,128)S(1)} %slice_add_fusion.18), channel_id=1, source_target_pairs={{0,8},{8,16},{16,24},{24,32},{32,40},{40,48},{48,56},{56,64},{64,7... | collective-permute-start | bytes 49160 | tf_op jit(solution)/shard_map/ppermute | solution.py:12
  68.8 4.7 %collective-permute-start.6 = (bf16[32,128]{1,0:T(8,128)(2,1)S(1)}, bf16[32,128]{1,0:T(8,128)(2,1)S(1)}, u32[]{:S(2)}, u32[]{:S(2)}) collective-permute-start(bf16[32,128]{1,0:T(8,128)(2,1)S(1)} %fusion.49), channel_id=1, source_target_pairs={{0,1016},{8,0},{16,8},{24,16},{32,24},{40,32},{48,40},{56,48},{64,... | collective-permute-start | bytes 24584 | tf_op jit(solution)/shard_map/ppermute | solution.py:12
  74.8 3.3 %copy-start.5 = (pred[1458,1152]{1,0:T(8,128)(4,1)S(1)}, pred[1458,1152]{1,0:T(8,128)(4,1)}, u32[]{:S(2)}) copy-start(pred[1458,1152]{1,0:T(8,128)(4,1)} %copy-done.1) | copy-start | bytes 5038852
  76.1 7.8 %collective-permute-start.7 = (f32[32,128]{1,0:T(8,128)S(1)}, f32[32,128]{1,0:T(8,128)S(1)}, u32[]{:S(2)}, u32[]{:S(2)}) collective-permute-start(f32[32,128]{1,0:T(8,128)S(1)} %slice_add_fusion.16), channel_id=1, source_target_pairs={{0,8},{8,16},{16,24},{24,32},{32,40},{40,48},{48,56},{56,64},{64,7... | collective-permute-start | bytes 49160 | tf_op jit(solution)/shard_map/ppermute | solution.py:12
  106.8 4.7 %collective-permute-start.8 = (f32[32,256]{1,0:T(8,128)S(1)}, f32[32,256]{1,0:T(8,128)S(1)}, u32[]{:S(2)}, u32[]{:S(2)}) collective-permute-start(f32[32,256]{1,0:T(8,128)S(1)} %fusion.185), channel_id=1, source_target_pairs={{0,8},{8,0},{16,24},{24,16},{32,40},{40,32},{48,56},{56,48},{64,72... | collective-permute-start | bytes 98312 | tf_op jit(solution)/shard_map/ppermute | solution.py:92
  111.5 5.9 %collective-permute-start.9 = (f32[32,256]{1,0:T(8,128)S(1)}, f32[32,256]{1,0:T(8,128)S(1)}, u32[]{:S(2)}, u32[]{:S(2)}) collective-permute-start(f32[32,256]{1,0:T(8,128)S(1)} %add.155), channel_id=1, source_target_pairs={{0,24},{8,16},{16,8},{24,0},{32,56},{40,48},{48,40},{56,32},{64,88... | collective-permute-start | bytes 98312 | tf_op jit(solution)/shard_map/ppermute | solution.py:92
  117.3 4.6 %collective-permute-start.10 = (f32[32,256]{1,0:T(8,128)S(1)}, f32[32,256]{1,0:T(8,128)S(1)}, u32[]{:S(2)}, u32[]{:S(2)}) collective-permute-start(f32[32,256]{1,0:T(8,128)S(1)} %add.156), channel_id=1, source_target_pairs={{0,32},{8,40},{16,48},{24,56},{32,0},{40,8},{48,16},{56,24},{64,96... | collective-permute-start | bytes 98312 | tf_op jit(solution)/shard_map/ppermute | solution.py:95
  122.0 5.6 %collective-permute-start.11 = (f32[32,256]{1,0:T(8,128)S(1)}, f32[32,256]{1,0:T(8,128)S(1)}, u32[]{:S(2)}, u32[]{:S(2)}) collective-permute-start(f32[32,256]{1,0:T(8,128)S(1)} %add.157), channel_id=1, source_target_pairs={{0,64},{8,72},{16,80},{24,88},{32,96},{40,104},{48,112},{56,120},{... | collective-permute-start | bytes 98312 | tf_op jit(solution)/shard_map/ppermute | solution.py:95
  127.6 9.0 %collective-permute-start.12 = (f32[32,256]{1,0:T(8,128)S(1)}, f32[32,256]{1,0:T(8,128)S(1)}, u32[]{:S(2)}, u32[]{:S(2)}) collective-permute-start(f32[32,256]{1,0:T(8,128)S(1)} %add.158), channel_id=1, source_target_pairs={{0,128},{8,136},{16,144},{24,152},{32,160},{40,168},{48,176},{56,1... | collective-permute-start | bytes 98312 | tf_op jit(solution)/shard_map/ppermute | solution.py:95
  136.6 14.5 %collective-permute-start.13 = (f32[32,256]{1,0:T(8,128)S(1)}, f32[32,256]{1,0:T(8,128)S(1)}, u32[]{:S(2)}, u32[]{:S(2)}) collective-permute-start(f32[32,256]{1,0:T(8,128)S(1)} %add.159), channel_id=1, source_target_pairs={{0,256},{8,264},{16,272},{24,280},{32,288},{40,296},{48,304},{56,3... | collective-permute-start | bytes 98312 | tf_op jit(solution)/shard_map/ppermute | solution.py:95
  151.1 13.4 %collective-permute-start.14 = (f32[32,256]{1,0:T(8,128)S(1)}, f32[32,256]{1,0:T(8,128)S(1)}, u32[]{:S(2)}, u32[]{:S(2)}) collective-permute-start(f32[32,256]{1,0:T(8,128)S(1)} %add.160), channel_id=1, source_target_pairs={{0,768},{8,776},{16,784},{24,792},{32,800},{40,808},{48,816},{56,8... | collective-permute-start | bytes 98312 | tf_op jit(solution)/shard_map/ppermute | solution.py:95

commit v10 on v9

--- a/solution.py
+++ b/solution.py
@@ -35,11 +35,12 @@
     return pick, owner
 
 
-def apply_filter(wave_block, cell_matrices, pick, owner):
+def apply_filter(wave_block, cell_matrices, pick, owner, own_plane=None):
     column_count = wave_block.shape[0]
     node_count = wave_block.shape[1]
     cell_count, cell_nodes, _ = cell_matrices.shape
-    own_plane = jnp.dot(wave_block, owner, preferred_element_type=jnp.float32).astype(jnp.bfloat16)
+    if own_plane is None:
+        own_plane = jnp.dot(wave_block, owner, preferred_element_type=jnp.float32).astype(jnp.bfloat16)
     upper_plane = from_behind(own_plane, "space", -1)
     contract_nodes = (((1,), (1,)), ((), ()))
     gathered = lax.dot_general(
@@ -119,7 +120,9 @@
 def body(wavefunctions, filter_cells, connectivity, owner_list):
     pick, owner = selectors(connectivity, owner_list, wavefunctions.shape[1])
     previous = wavefunctions.astype(jnp.float32)
-    current = apply_filter(wavefunctions, filter_cells, pick, owner)
+    current = apply_filter(
+        wavefunctions, filter_cells, pick, owner, jnp.take(wavefunctions, owner_list, axis=1)
+    )
     for degree_step in range(DEGREE - 1):
         following = (
             2.0 * apply_filter(current.astype(jnp.bfloat16), filter_cells, pick, owner)

time: 192 us -> 194 us (1.010)
  no operation moved by 1% of the time
where the time goes in v10:
time: 194 us; the launch traced here: 193 us
  waiting for transfers between devices  63.3 us (33%)
  starting transfers between devices  53.5 us (28%)
  blocking collectives  42.4 us (22%)
  matrix products  23.4 us (12%)
  local copies, waits for them, and re-layouts  4.71 us (2%)
  other arithmetic  4.22 us (2%)
    ppermute x7, waiting for transfers between devices, butterfly_sum(): block = block + lax.ppermute(block, axis, pairs)  39.1 us
    ppermute x8, starting transfers between devices, from_behind(): lax.ppermute(shard, axis, [(i, (i + by) % peers) for i in range(peers)])  35 us
    ppermute x8, waiting for transfers between devices, from_behind(): lax.ppermute(shard, axis, [(i, (i + by) % peers) for i in range(peers)])  24.2 us
    all_gather x1, blocking collectives, body(): every_column = lax.all_gather(filtered, 'wave', axis=0, tiled=True)  22.2 us
    all_gather x1, blocking collectives, body(): margin = lax.all_gather(own_rows, 'wave', axis=0, tiled=True) / node_total  20.2 us
    ppermute x7, starting transfers between devices, butterfly_sum(): block = block + lax.ppermute(block, axis, pairs)  18.5 us
    dot_general x4, matrix products, apply_filter(): jnp.dot(stacked, pick[:, node_count:], preferred_element_type=jnp.float32)  5.14 us
    dot_general x4, matrix products, apply_filter(): jnp.dot(stacked, pick[:, :node_count], preferred_element_type=jnp.float32)  3.89 us
  transfers between devices with their start and end apart: 15, of which 14 were waited for; matrix products, arithmetic and copies ran while one was open for 5% of the time, Pallas kernels for 0%

profile of v10, /device:TPU:1, one launch (start us, length us, event | category | flops | bytes accessed | tf_op | source)
XLA Modules:
  0.0 192.9 jit_solution(15802484138209928705)
XLA Ops:
  3.3 21.4 %collective-permute-start = (bf16[32,128]{0,1:T(8,128)(2,1)S(1)}, bf16[32,128]{0,1:T(8,128)(2,1)S(1)}, u32[]{:S(2)}, u32[]{:S(2)}) collective-permute-start(bf16[32,128]{0,1:T(8,128)(2,1)S(1)} %select_bitcast_fusion), channel_id=1, source_target_pairs={{0,1016},{8,0},{16,8},{24,16},{32,24},{40,32},{48,40},{56,48},{64,... | collective-permute-start | bytes 24584 | tf_op jit(solution)/shard_map/ppermute | solution.py:12
  25.5 1.5 iota_compare_fusion
  30.9 1.9 collective-permute-start.1
  33.8 4.9 %collective-permute-done.1 = f32[32,128]{1,0:T(8,128)S(1)} collective-permute-done((f32[32,128]{1,0:T(8,128)S(1)}, f32[32,128]{1,0:T(8,128)S(1)}, u32[]{:S(2)}, u32[]{:S(2)}) %collective-permute-start.1) | collective-permute-done | bytes 16416 | tf_op jit(solution)/shard_map/ppermute | solution.py:12
  39.5 1.9 collective-permute-start.2
  42.4 1.5 collective-permute-done.2
  46.5 1.9 collective-permute-start.3
  49.4 4.9 %collective-permute-done.3 = f32[32,128]{1,0:T(8,128)S(1)} collective-permute-done((f32[32,128]{1,0:T(8,128)S(1)}, f32[32,128]{1,0:T(8,128)S(1)}, u32[]{:S(2)}, u32[]{:S(2)}) %collective-permute-start.3) | collective-permute-done | bytes 16416 | tf_op jit(solution)/shard_map/ppermute | solution.py:12
  55.1 1.9 collective-permute-start.4
  58.0 1.5 collective-permute-done.4
  62.1 1.9 collective-permute-start.5
  65.0 4.9 %collective-permute-done.5 = f32[32,128]{1,0:T(8,128)S(1)} collective-permute-done((f32[32,128]{1,0:T(8,128)S(1)}, f32[32,128]{1,0:T(8,128)S(1)}, u32[]{:S(2)}, u32[]{:S(2)}) %collective-permute-start.5) | collective-permute-done | bytes 16416 | tf_op jit(solution)/shard_map/ppermute | solution.py:12
  70.7 2.1 %collective-permute-start.6 = (bf16[32,128]{1,0:T(8,128)(2,1)S(1)}, bf16[32,128]{1,0:T(8,128)(2,1)S(1)}, u32[]{:S(2)}, u32[]{:S(2)}) collective-permute-start(bf16[32,128]{1,0:T(8,128)(2,1)S(1)} %fusion.48), channel_id=1, source_target_pairs={{0,1016},{8,0},{16,8},{24,16},{32,24},{40,32},{48,40},{56,48},{64,... | collective-permute-start | bytes 24584 | tf_op jit(solution)/shard_map/ppermute | solution.py:12
  73.8 1.6 collective-permute-done.6
  78.0 1.9 collective-permute-start.7
  80.9 4.9 %collective-permute-done.7 = f32[32,128]{1,0:T(8,128)S(1)} collective-permute-done((f32[32,128]{1,0:T(8,128)S(1)}, f32[32,128]{1,0:T(8,128)S(1)}, u32[]{:S(2)}, u32[]{:S(2)}) %collective-permute-start.7) | collective-permute-done | bytes 16416 | tf_op jit(solution)/shard_map/ppermute | solution.py:12
  86.2 22.2 %all_gather.6 = bf16[256,1024]{1,0:T(8,128)(2,1)S(1)} all-gather(bf16[32,1024]{1,0:T(8,128)(2,1)S(1)} %fusion.78), channel_id=1, replica_groups=mesh['space'=128,'wave'=8] {'wave'}, dimensions={0}, use_global_device_ids=true | all-gather | bytes 589824 | tf_op jit(solution)/shard_map/all_gather | solution.py:135
  108.7 1.9 %collective-permute-start.8 = (f32[32,256]{1,0:T(8,128)S(1)}, f32[32,256]{1,0:T(8,128)S(1)}, u32[]{:S(2)}, u32[]{:S(2)}) collective-permute-start(f32[32,256]{1,0:T(8,128)S(1)} %fusion.182), channel_id=1, source_target_pairs={{0,8},{8,0},{16,24},{24,16},{32,40},{40,32},{48,56},{56,48},{64,72... | collective-permute-start | bytes 98312 | tf_op jit(solution)/shard_map/ppermute | solution.py:93
  110.6 2.7 %collective-permute-done.8 = f32[32,256]{1,0:T(8,128)S(1)} collective-permute-done((f32[32,256]{1,0:T(8,128)S(1)}, f32[32,256]{1,0:T(8,128)S(1)}, u32[]{:S(2)}, u32[]{:S(2)}) %collective-permute-start.8) | collective-permute-done | bytes 32800 | tf_op jit(solution)/shard_map/ppermute | solution.py:93
  113.3 1.9 collective-permute-start.9
  115.3 3.9 %collective-permute-done.9 = f32[32,256]{1,0:T(8,128)S(1)} collective-permute-done((f32[32,256]{1,0:T(8,128)S(1)}, f32[32,256]{1,0:T(8,128)S(1)}, u32[]{:S(2)}, u32[]{:S(2)}) %collective-permute-start.9) | collective-permute-done | bytes 32800 | tf_op jit(solution)/shard_map/ppermute | solution.py:93
  119.2 1.9 collective-permute-start.10
  121.1 2.7 %collective-permute-done.10 = f32[32,256]{1,0:T(8,128)S(1)} collective-permute-done((f32[32,256]{1,0:T(8,128)S(1)}, f32[32,256]{1,0:T(8,128)S(1)}, u32[]{:S(2)}, u32[]{:S(2)}) %collective-permute-start.10) | collective-permute-done | bytes 32800 | tf_op jit(solution)/shard_map/ppermute | solution.py:96
  123.9 1.9 collective-permute-start.11
  125.8 3.7 %collective-permute-done.11 = f32[32,256]{1,0:T(8,128)S(1)} collective-permute-done((f32[32,256]{1,0:T(8,128)S(1)}, f32[32,256]{1,0:T(8,128)S(1)}, u32[]{:S(2)}, u32[]{:S(2)}) %collective-permute-start.11) | collective-permute-done | bytes 32800 | tf_op jit(solution)/shard_map/ppermute | solution.py:96
  129.5 1.9 collective-permute-start.12
  131.4 7.1 %collective-permute-done.12 = f32[32,256]{1,0:T(8,128)S(1)} collective-permute-done((f32[32,256]{1,0:T(8,128)S(1)}, f32[32,256]{1,0:T(8,128)S(1)}, u32[]{:S(2)}, u32[]{:S(2)}) %collective-permute-start.12) | collective-permute-done | bytes 32800 | tf_op jit(solution)/shard_map/ppermute | solution.py:96
  138.5 1.9 collective-permute-start.13
  140.4 12.6 %collective-permute-done.13 = f32[32,256]{1,0:T(8,128)S(1)} collective-permute-done((f32[32,256]{1,0:T(8,128)S(1)}, f32[32,256]{1,0:T(8,128)S(1)}, u32[]{:S(2)}, u32[]{:S(2)}) %collective-permute-start.13) | collective-permute-done | bytes 32800 | tf_op jit(solution)/shard_map/ppermute | solution.py:96
  153.0 7.0 %collective-permute-start.14 = (f32[32,256]{1,0:T(8,128)S(1)}, f32[32,256]{1,0:T(8,128)S(1)}, u32[]{:S(2)}, u32[]{:S(2)}) collective-permute-start(f32[32,256]{1,0:T(8,128)S(1)} %add.170), channel_id=1, source_target_pairs={{0,768},{8,776},{16,784},{24,792},{32,800},{40,808},{48,816},{56,8... | collective-permute-start | bytes 98312 | tf_op jit(solution)/shard_map/ppermute | solution.py:96
  160.0 6.3 %collective-permute-done.14 = f32[32,256]{1,0:T(8,128)S(1)} collective-permute-done((f32[32,256]{1,0:T(8,128)S(1)}, f32[32,256]{1,0:T(8,128)S(1)}, u32[]{:S(2)}, u32[]{:S(2)}) %collective-permute-start.14) | collective-permute-done | bytes 32800 | tf_op jit(solution)/shard_map/ppermute | solution.py:96
  166.4 20.2 %all_gather.7 = f32[256,256]{1,0:T(8,128)S(1)} all-gather(f32[32,256]{1,0:T(8,128)S(1)} %add.171), channel_id=1, replica_groups=mesh['space'=128,'wave'=8] {'wave'}, dimensions={0}, use_global_device_ids=true | all-gather | bytes 294912 | tf_op jit(solution)/shard_map/all_gather | solution.py:138
  (99 shorter events, 30.9 us)
Async XLA Ops:
  0.0 28.6 %copy-start = (bf16[2,729,729]{2,0,1:T(2,128)(2,1)S(1)}, bf16[2,729,729]{2,0,1:T(2,128)(2,1)}, u32[]{:S(2)}) copy-start(bf16[2,729,729]{2,0,1:T(2,128)(2,1)} %param.5) | copy-start | bytes 6377296
  0.0 27.0 %copy-start.6 = (bf16[32,1024]{1,0:T(8,128)(2,1)S(1)}, bf16[32,1024]{1,0:T(8,128)(2,1)}, u32[]{:S(2)}) copy-start(bf16[32,1024]{1,0:T(8,128)(2,1)} %param.4) | copy-start | bytes 196612
  3.3 24.7 %collective-permute-start = (bf16[32,128]{0,1:T(8,128)(2,1)S(1)}, bf16[32,128]{0,1:T(8,128)(2,1)S(1)}, u32[]{:S(2)}, u32[]{:S(2)}) collective-permute-start(bf16[32,128]{0,1:T(8,128)(2,1)S(1)} %select_bitcast_fusion), channel_id=1, source_target_pairs={{0,1016},{8,0},{16,8},{24,16},{32,24},{40,32},{48,40},{56,48},{64,... | collective-permute-start | bytes 24584 | tf_op jit(solution)/shard_map/ppermute | solution.py:12
  27.0 1.2 copy-start.1
  29.5 3.3 %copy-start.2 = (pred[1458,1152]{1,0:T(8,128)(4,1)S(1)}, pred[1458,1152]{1,0:T(8,128)(4,1)}, u32[]{:S(2)}) copy-start(pred[1458,1152]{1,0:T(8,128)(4,1)} %copy-done.1) | copy-start | bytes 5038852
  30.9 7.8 %copy-start.7 = (s32[128]{0:T(128)S(1)}, s32[128]{0:T(128)}, u32[]{:S(2)}) copy-start(s32[128]{0:T(128)} %param.7) | copy-start | bytes 1540
  30.9 7.8 %collective-permute-start.1 = (f32[32,128]{1,0:T(8,128)S(1)}, f32[32,128]{1,0:T(8,128)S(1)}, u32[]{:S(2)}, u32[]{:S(2)}) collective-permute-start(f32[32,128]{1,0:T(8,128)S(1)} %slice_add_fusion.22), channel_id=1, source_target_pairs={{0,8},{8,16},{16,24},{24,32},{32,40},{40,48},{48,56},{56,64},{64,7... | collective-permute-start | bytes 49160 | tf_op jit(solution)/shard_map/ppermute | solution.py:12
  39.5 4.4 %collective-permute-start.2 = (bf16[32,128]{1,0:T(8,128)(2,1)S(1)}, bf16[32,128]{1,0:T(8,128)(2,1)S(1)}, u32[]{:S(2)}, u32[]{:S(2)}) collective-permute-start(bf16[32,128]{1,0:T(8,128)(2,1)S(1)} %fusion.42), channel_id=1, source_target_pairs={{0,1016},{8,0},{16,8},{24,16},{32,24},{40,32},{48,40},{56,48},{64,... | collective-permute-start | bytes 24584 | tf_op jit(solution)/shard_map/ppermute | solution.py:12
  45.1 3.3 %copy-start.3 = (pred[1458,1152]{1,0:T(8,128)(4,1)S(1)}, pred[1458,1152]{1,0:T(8,128)(4,1)}, u32[]{:S(2)}) copy-start(pred[1458,1152]{1,0:T(8,128)(4,1)} %copy-done.1) | copy-start | bytes 5038852
  46.5 7.8 %collective-permute-start.3 = (f32[32,128]{1,0:T(8,128)S(1)}, f32[32,128]{1,0:T(8,128)S(1)}, u32[]{:S(2)}, u32[]{:S(2)}) collective-permute-start(f32[32,128]{1,0:T(8,128)S(1)} %slice_add_fusion.20), channel_id=1, source_target_pairs={{0,8},{8,16},{16,24},{24,32},{32,40},{40,48},{48,56},{56,64},{64,7... | collective-permute-start | bytes 49160 | tf_op jit(solution)/shard_map/ppermute | solution.py:12
  55.1 4.4 %collective-permute-start.4 = (bf16[32,128]{1,0:T(8,128)(2,1)S(1)}, bf16[32,128]{1,0:T(8,128)(2,1)S(1)}, u32[]{:S(2)}, u32[]{:S(2)}) collective-permute-start(bf16[32,128]{1,0:T(8,128)(2,1)S(1)} %fusion.45), channel_id=1, source_target_pairs={{0,1016},{8,0},{16,8},{24,16},{32,24},{40,32},{48,40},{56,48},{64,... | collective-permute-start | bytes 24584 | tf_op jit(solution)/shard_map/ppermute | solution.py:12
  60.7 3.3 %copy-start.4 = (pred[1458,1152]{1,0:T(8,128)(4,1)S(1)}, pred[1458,1152]{1,0:T(8,128)(4,1)}, u32[]{:S(2)}) copy-start(pred[1458,1152]{1,0:T(8,128)(4,1)} %copy-done.1) | copy-start | bytes 5038852
  62.1 7.8 %collective-permute-start.5 = (f32[32,128]{1,0:T(8,128)S(1)}, f32[32,128]{1,0:T(8,128)S(1)}, u32[]{:S(2)}, u32[]{:S(2)}) collective-permute-start(f32[32,128]{1,0:T(8,128)S(1)} %slice_add_fusion.18), channel_id=1, source_target_pairs={{0,8},{8,16},{16,24},{24,32},{32,40},{40,48},{48,56},{56,64},{64,7... | collective-permute-start | bytes 49160 | tf_op jit(solution)/shard_map/ppermute | solution.py:12
  70.7 4.7 %collective-permute-start.6 = (bf16[32,128]{1,0:T(8,128)(2,1)S(1)}, bf16[32,128]{1,0:T(8,128)(2,1)S(1)}, u32[]{:S(2)}, u32[]{:S(2)}) collective-permute-start(bf16[32,128]{1,0:T(8,128)(2,1)S(1)} %fusion.48), channel_id=1, source_target_pairs={{0,1016},{8,0},{16,8},{24,16},{32,24},{40,32},{48,40},{56,48},{64,... | collective-permute-start | bytes 24584 | tf_op jit(solution)/shard_map/ppermute | solution.py:12
  76.6 3.3 %copy-start.5 = (pred[1458,1152]{1,0:T(8,128)(4,1)S(1)}, pred[1458,1152]{1,0:T(8,128)(4,1)}, u32[]{:S(2)}) copy-start(pred[1458,1152]{1,0:T(8,128)(4,1)} %copy-done.1) | copy-start | bytes 5038852
  78.0 7.8 %collective-permute-start.7 = (f32[32,128]{1,0:T(8,128)S(1)}, f32[32,128]{1,0:T(8,128)S(1)}, u32[]{:S(2)}, u32[]{:S(2)}) collective-permute-start(f32[32,128]{1,0:T(8,128)S(1)} %slice_add_fusion.16), channel_id=1, source_target_pairs={{0,8},{8,16},{16,24},{24,32},{32,40},{40,48},{48,56},{56,64},{64,7... | collective-permute-start | bytes 49160 | tf_op jit(solution)/shard_map/ppermute | solution.py:12
  108.7 4.7 %collective-permute-start.8 = (f32[32,256]{1,0:T(8,128)S(1)}, f32[32,256]{1,0:T(8,128)S(1)}, u32[]{:S(2)}, u32[]{:S(2)}) collective-permute-start(f32[32,256]{1,0:T(8,128)S(1)} %fusion.182), channel_id=1, source_target_pairs={{0,8},{8,0},{16,24},{24,16},{32,40},{40,32},{48,56},{56,48},{64,72... | collective-permute-start | bytes 98312 | tf_op jit(solution)/shard_map/ppermute | solution.py:93
  113.3 5.9 %collective-permute-start.9 = (f32[32,256]{1,0:T(8,128)S(1)}, f32[32,256]{1,0:T(8,128)S(1)}, u32[]{:S(2)}, u32[]{:S(2)}) collective-permute-start(f32[32,256]{1,0:T(8,128)S(1)} %add.165), channel_id=1, source_target_pairs={{0,24},{8,16},{16,8},{24,0},{32,56},{40,48},{48,40},{56,32},{64,88... | collective-permute-start | bytes 98312 | tf_op jit(solution)/shard_map/ppermute | solution.py:93
  119.2 4.6 %collective-permute-start.10 = (f32[32,256]{1,0:T(8,128)S(1)}, f32[32,256]{1,0:T(8,128)S(1)}, u32[]{:S(2)}, u32[]{:S(2)}) collective-permute-start(f32[32,256]{1,0:T(8,128)S(1)} %add.166), channel_id=1, source_target_pairs={{0,32},{8,40},{16,48},{24,56},{32,0},{40,8},{48,16},{56,24},{64,96... | collective-permute-start | bytes 98312 | tf_op jit(solution)/shard_map/ppermute | solution.py:96
  123.9 5.6 %collective-permute-start.11 = (f32[32,256]{1,0:T(8,128)S(1)}, f32[32,256]{1,0:T(8,128)S(1)}, u32[]{:S(2)}, u32[]{:S(2)}) collective-permute-start(f32[32,256]{1,0:T(8,128)S(1)} %add.167), channel_id=1, source_target_pairs={{0,64},{8,72},{16,80},{24,88},{32,96},{40,104},{48,112},{56,120},{... | collective-permute-start | bytes 98312 | tf_op jit(solution)/shard_map/ppermute | solution.py:96
  129.5 9.0 %collective-permute-start.12 = (f32[32,256]{1,0:T(8,128)S(1)}, f32[32,256]{1,0:T(8,128)S(1)}, u32[]{:S(2)}, u32[]{:S(2)}) collective-permute-start(f32[32,256]{1,0:T(8,128)S(1)} %add.168), channel_id=1, source_target_pairs={{0,128},{8,136},{16,144},{24,152},{32,160},{40,168},{48,176},{56,1... | collective-permute-start | bytes 98312 | tf_op jit(solution)/shard_map/ppermute | solution.py:96
  138.5 14.5 %collective-permute-start.13 = (f32[32,256]{1,0:T(8,128)S(1)}, f32[32,256]{1,0:T(8,128)S(1)}, u32[]{:S(2)}, u32[]{:S(2)}) collective-permute-start(f32[32,256]{1,0:T(8,128)S(1)} %add.169), channel_id=1, source_target_pairs={{0,256},{8,264},{16,272},{24,280},{32,288},{40,296},{48,304},{56,3... | collective-permute-start | bytes 98312 | tf_op jit(solution)/shard_map/ppermute | solution.py:96
  153.0 13.4 %collective-permute-start.14 = (f32[32,256]{1,0:T(8,128)S(1)}, f32[32,256]{1,0:T(8,128)S(1)}, u32[]{:S(2)}, u32[]{:S(2)}) collective-permute-start(f32[32,256]{1,0:T(8,128)S(1)} %add.170), channel_id=1, source_target_pairs={{0,768},{8,776},{16,784},{24,792},{32,800},{40,808},{48,816},{56,8... | collective-permute-start | bytes 98312 | tf_op jit(solution)/shard_map/ppermute | solution.py:96

commit v11 on v9

--- a/solution.py
+++ b/solution.py
@@ -132,7 +132,7 @@
     every_column = lax.all_gather(filtered, "wave", axis=0, tiled=True)
     own_rows = jnp.dot(filtered, every_column.T, preferred_element_type=jnp.float32)
     own_rows = butterfly_sum(own_rows, "space", 4)
-    margin = lax.all_gather(own_rows, "wave", axis=0, tiled=True) / node_total
+    margin = lax.all_gather(own_rows / node_total, "wave", axis=0, tiled=True)
     own_rotation = newton_schulz(margin, lax.axis_index("wave") * column_count, column_count)
     return jnp.dot(own_rotation.T, every_column, preferred_element_type=jnp.float32).astype(
         jnp.bfloat16

time: 192 us -> 192 us (level)
  no operation moved by 1% of the time
where the time goes in v11:
time: 192 us; the launch traced here: 191 us
  waiting for transfers between devices  63.3 us (33%)
  starting transfers between devices  53.5 us (28%)
  blocking collectives  42.4 us (22%)
  matrix products  24.8 us (13%)
  local copies, waits for them, and re-layouts  2.99 us (2%)
  other arithmetic  2.65 us (1%)
    ppermute x7, waiting for transfers between devices, butterfly_sum(): block = block + lax.ppermute(block, axis, pairs)  39.1 us
    ppermute x8, starting transfers between devices, from_behind(): lax.ppermute(shard, axis, [(i, (i + by) % peers) for i in range(peers)])  35 us
    ppermute x8, waiting for transfers between devices, from_behind(): lax.ppermute(shard, axis, [(i, (i + by) % peers) for i in range(peers)])  24.2 us
    all_gather x1, blocking collectives, body(): every_column = lax.all_gather(filtered, 'wave', axis=0, tiled=True)  22.2 us
    all_gather x1, blocking collectives, body(): margin = lax.all_gather(own_rows / node_total, 'wave', axis=0, tiled=True)  20.2 us
    ppermute x7, starting transfers between devices, butterfly_sum(): block = block + lax.ppermute(block, axis, pairs)  18.5 us
    dot_general x4, matrix products, apply_filter(): jnp.dot(stacked, pick[:, node_count:], preferred_element_type=jnp.float32)  5.13 us
    dot_general x4, matrix products, apply_filter(): jnp.dot(stacked, pick[:, :node_count], preferred_element_type=jnp.float32)  3.89 us
  transfers between devices with their start and end apart: 15, of which 14 were waited for; matrix products, arithmetic and copies ran while one was open for 5% of the time, Pallas kernels for 0%

profile of v11, /device:TPU:1, one launch (start us, length us, event | category | flops | bytes accessed | tf_op | source)
XLA Modules:
  0.0 191.0 jit_solution(5830598455673291237)
XLA Ops:
  1.5 21.4 %collective-permute-start = (bf16[32,128]{0,1:T(8,128)(2,1)S(1)}, bf16[32,128]{0,1:T(8,128)(2,1)S(1)}, u32[]{:S(2)}, u32[]{:S(2)}) collective-permute-start(bf16[32,128]{0,1:T(8,128)(2,1)S(1)} %fusion.42), channel_id=1, source_target_pairs={{0,1016},{8,0},{16,8},{24,16},{32,24},{40,32},{48,40},{56,48},{64,... | collective-permute-start | bytes 24584 | tf_op jit(solution)/shard_map/ppermute | solution.py:12
  23.7 1.5 iota_compare_fusion
  29.0 1.9 %collective-permute-start.1 = (f32[32,128]{1,0:T(8,128)S(1)}, f32[32,128]{1,0:T(8,128)S(1)}, u32[]{:S(2)}, u32[]{:S(2)}) collective-permute-start(f32[32,128]{1,0:T(8,128)S(1)} %slice_add_fusion.22), channel_id=1, source_target_pairs={{0,8},{8,16},{16,24},{24,32},{32,40},{40,48},{48,56},{56,64},{64,7... | collective-permute-start | bytes 49160 | tf_op jit(solution)/shard_map/ppermute | solution.py:12
  31.9 4.9 %collective-permute-done.1 = f32[32,128]{1,0:T(8,128)S(1)} collective-permute-done((f32[32,128]{1,0:T(8,128)S(1)}, f32[32,128]{1,0:T(8,128)S(1)}, u32[]{:S(2)}, u32[]{:S(2)}) %collective-permute-start.1) | collective-permute-done | bytes 16416 | tf_op jit(solution)/shard_map/ppermute | solution.py:12
  37.6 1.9 %collective-permute-start.2 = (bf16[32,128]{1,0:T(8,128)(2,1)S(1)}, bf16[32,128]{1,0:T(8,128)(2,1)S(1)}, u32[]{:S(2)}, u32[]{:S(2)}) collective-permute-start(bf16[32,128]{1,0:T(8,128)(2,1)S(1)} %fusion.43), channel_id=1, source_target_pairs={{0,1016},{8,0},{16,8},{24,16},{32,24},{40,32},{48,40},{56,48},{64,... | collective-permute-start | bytes 24584 | tf_op jit(solution)/shard_map/ppermute | solution.py:12
  40.5 1.5 collective-permute-done.2
  44.6 1.9 %collective-permute-start.3 = (f32[32,128]{1,0:T(8,128)S(1)}, f32[32,128]{1,0:T(8,128)S(1)}, u32[]{:S(2)}, u32[]{:S(2)}) collective-permute-start(f32[32,128]{1,0:T(8,128)S(1)} %slice_add_fusion.20), channel_id=1, source_target_pairs={{0,8},{8,16},{16,24},{24,32},{32,40},{40,48},{48,56},{56,64},{64,7... | collective-permute-start | bytes 49160 | tf_op jit(solution)/shard_map/ppermute | solution.py:12
  47.5 4.9 %collective-permute-done.3 = f32[32,128]{1,0:T(8,128)S(1)} collective-permute-done((f32[32,128]{1,0:T(8,128)S(1)}, f32[32,128]{1,0:T(8,128)S(1)}, u32[]{:S(2)}, u32[]{:S(2)}) %collective-permute-start.3) | collective-permute-done | bytes 16416 | tf_op jit(solution)/shard_map/ppermute | solution.py:12
  53.2 1.9 %collective-permute-start.4 = (bf16[32,128]{1,0:T(8,128)(2,1)S(1)}, bf16[32,128]{1,0:T(8,128)(2,1)S(1)}, u32[]{:S(2)}, u32[]{:S(2)}) collective-permute-start(bf16[32,128]{1,0:T(8,128)(2,1)S(1)} %fusion.46), channel_id=1, source_target_pairs={{0,1016},{8,0},{16,8},{24,16},{32,24},{40,32},{48,40},{56,48},{64,... | collective-permute-start | bytes 24584 | tf_op jit(solution)/shard_map/ppermute | solution.py:12
  56.1 1.5 collective-permute-done.4
  60.2 1.9 %collective-permute-start.5 = (f32[32,128]{1,0:T(8,128)S(1)}, f32[32,128]{1,0:T(8,128)S(1)}, u32[]{:S(2)}, u32[]{:S(2)}) collective-permute-start(f32[32,128]{1,0:T(8,128)S(1)} %slice_add_fusion.18), channel_id=1, source_target_pairs={{0,8},{8,16},{16,24},{24,32},{32,40},{40,48},{48,56},{56,64},{64,7... | collective-permute-start | bytes 49160 | tf_op jit(solution)/shard_map/ppermute | solution.py:12
  63.1 4.9 %collective-permute-done.5 = f32[32,128]{1,0:T(8,128)S(1)} collective-permute-done((f32[32,128]{1,0:T(8,128)S(1)}, f32[32,128]{1,0:T(8,128)S(1)}, u32[]{:S(2)}, u32[]{:S(2)}) %collective-permute-start.5) | collective-permute-done | bytes 16416 | tf_op jit(solution)/shard_map/ppermute | solution.py:12
  68.8 2.1 %collective-permute-start.6 = (bf16[32,128]{1,0:T(8,128)(2,1)S(1)}, bf16[32,128]{1,0:T(8,128)(2,1)S(1)}, u32[]{:S(2)}, u32[]{:S(2)}) collective-permute-start(bf16[32,128]{1,0:T(8,128)(2,1)S(1)} %fusion.49), channel_id=1, source_target_pairs={{0,1016},{8,0},{16,8},{24,16},{32,24},{40,32},{48,40},{56,48},{64,... | collective-permute-start | bytes 24584 | tf_op jit(solution)/shard_map/ppermute | solution.py:12
  71.9 1.6 collective-permute-done.6
  76.1 1.9 %collective-permute-start.7 = (f32[32,128]{1,0:T(8,128)S(1)}, f32[32,128]{1,0:T(8,128)S(1)}, u32[]{:S(2)}, u32[]{:S(2)}) collective-permute-start(f32[32,128]{1,0:T(8,128)S(1)} %slice_add_fusion.16), channel_id=1, source_target_pairs={{0,8},{8,16},{16,24},{24,32},{32,40},{40,48},{48,56},{56,64},{64,7... | collective-permute-start | bytes 49160 | tf_op jit(solution)/shard_map/ppermute | solution.py:12
  79.0 4.9 %collective-permute-done.7 = f32[32,128]{1,0:T(8,128)S(1)} collective-permute-done((f32[32,128]{1,0:T(8,128)S(1)}, f32[32,128]{1,0:T(8,128)S(1)}, u32[]{:S(2)}, u32[]{:S(2)}) %collective-permute-start.7) | collective-permute-done | bytes 16416 | tf_op jit(solution)/shard_map/ppermute | solution.py:12
  84.4 22.2 %all_gather.6 = bf16[256,1024]{1,0:T(8,128)(2,1)S(1)} all-gather(bf16[32,1024]{1,0:T(8,128)(2,1)S(1)} %fusion.81), channel_id=1, replica_groups=mesh['space'=128,'wave'=8] {'wave'}, dimensions={0}, use_global_device_ids=true | all-gather | bytes 589824 | tf_op jit(solution)/shard_map/all_gather | solution.py:132
  106.8 1.9 %collective-permute-start.8 = (f32[32,256]{1,0:T(8,128)S(1)}, f32[32,256]{1,0:T(8,128)S(1)}, u32[]{:S(2)}, u32[]{:S(2)}) collective-permute-start(f32[32,256]{1,0:T(8,128)S(1)} %fusion.185), channel_id=1, source_target_pairs={{0,8},{8,0},{16,24},{24,16},{32,40},{40,32},{48,56},{56,48},{64,72... | collective-permute-start | bytes 98312 | tf_op jit(solution)/shard_map/ppermute | solution.py:92
  108.7 2.7 %collective-permute-done.8 = f32[32,256]{1,0:T(8,128)S(1)} collective-permute-done((f32[32,256]{1,0:T(8,128)S(1)}, f32[32,256]{1,0:T(8,128)S(1)}, u32[]{:S(2)}, u32[]{:S(2)}) %collective-permute-start.8) | collective-permute-done | bytes 32800 | tf_op jit(solution)/shard_map/ppermute | solution.py:92
  111.5 1.9 collective-permute-start.9
  113.4 3.9 %collective-permute-done.9 = f32[32,256]{1,0:T(8,128)S(1)} collective-permute-done((f32[32,256]{1,0:T(8,128)S(1)}, f32[32,256]{1,0:T(8,128)S(1)}, u32[]{:S(2)}, u32[]{:S(2)}) %collective-permute-start.9) | collective-permute-done | bytes 32800 | tf_op jit(solution)/shard_map/ppermute | solution.py:92
  117.3 1.9 collective-permute-start.10
  119.3 2.7 %collective-permute-done.10 = f32[32,256]{1,0:T(8,128)S(1)} collective-permute-done((f32[32,256]{1,0:T(8,128)S(1)}, f32[32,256]{1,0:T(8,128)S(1)}, u32[]{:S(2)}, u32[]{:S(2)}) %collective-permute-start.10) | collective-permute-done | bytes 32800 | tf_op jit(solution)/shard_map/ppermute | solution.py:95
  122.0 1.9 collective-permute-start.11
  123.9 3.7 %collective-permute-done.11 = f32[32,256]{1,0:T(8,128)S(1)} collective-permute-done((f32[32,256]{1,0:T(8,128)S(1)}, f32[32,256]{1,0:T(8,128)S(1)}, u32[]{:S(2)}, u32[]{:S(2)}) %collective-permute-start.11) | collective-permute-done | bytes 32800 | tf_op jit(solution)/shard_map/ppermute | solution.py:95
  127.6 1.9 collective-permute-start.12
  129.5 7.1 %collective-permute-done.12 = f32[32,256]{1,0:T(8,128)S(1)} collective-permute-done((f32[32,256]{1,0:T(8,128)S(1)}, f32[32,256]{1,0:T(8,128)S(1)}, u32[]{:S(2)}, u32[]{:S(2)}) %collective-permute-start.12) | collective-permute-done | bytes 32800 | tf_op jit(solution)/shard_map/ppermute | solution.py:95
  136.6 1.9 collective-permute-start.13
  138.5 12.6 %collective-permute-done.13 = f32[32,256]{1,0:T(8,128)S(1)} collective-permute-done((f32[32,256]{1,0:T(8,128)S(1)}, f32[32,256]{1,0:T(8,128)S(1)}, u32[]{:S(2)}, u32[]{:S(2)}) %collective-permute-start.13) | collective-permute-done | bytes 32800 | tf_op jit(solution)/shard_map/ppermute | solution.py:95
  151.1 7.0 %collective-permute-start.14 = (f32[32,256]{1,0:T(8,128)S(1)}, f32[32,256]{1,0:T(8,128)S(1)}, u32[]{:S(2)}, u32[]{:S(2)}) collective-permute-start(f32[32,256]{1,0:T(8,128)S(1)} %add.160), channel_id=1, source_target_pairs={{0,768},{8,776},{16,784},{24,792},{32,800},{40,808},{48,816},{56,8... | collective-permute-start | bytes 98312 | tf_op jit(solution)/shard_map/ppermute | solution.py:95
  158.2 6.3 %collective-permute-done.14 = f32[32,256]{1,0:T(8,128)S(1)} collective-permute-done((f32[32,256]{1,0:T(8,128)S(1)}, f32[32,256]{1,0:T(8,128)S(1)}, u32[]{:S(2)}, u32[]{:S(2)}) %collective-permute-start.14) | collective-permute-done | bytes 32800 | tf_op jit(solution)/shard_map/ppermute | solution.py:95
  164.5 20.2 %all_gather.7 = f32[256,256]{1,0:T(8,128)S(1)} all-gather(f32[32,256]{1,0:T(8,128)S(1)} %add_multiply_fusion), channel_id=1, replica_groups=mesh['space'=128,'wave'=8] {'wave'}, dimensions={0}, use_global_device_ids=true | all-gather | bytes 294912 | tf_op jit(solution)/shard_map/all_gather | solution.py:135
  (94 shorter events, 29.0 us)
Async XLA Ops:
  0.0 26.8 %copy-start = (bf16[2,729,729]{2,0,1:T(2,128)(2,1)S(1)}, bf16[2,729,729]{2,0,1:T(2,128)(2,1)}, u32[]{:S(2)}) copy-start(bf16[2,729,729]{2,0,1:T(2,128)(2,1)} %param.5) | copy-start | bytes 6377296
  0.0 25.1 %copy-start.6 = (bf16[32,1024]{1,0:T(8,128)(2,1)S(1)}, bf16[32,1024]{1,0:T(8,128)(2,1)}, u32[]{:S(2)}) copy-start(bf16[32,1024]{1,0:T(8,128)(2,1)} %param.4) | copy-start | bytes 196612
  1.5 24.7 %collective-permute-start = (bf16[32,128]{0,1:T(8,128)(2,1)S(1)}, bf16[32,128]{0,1:T(8,128)(2,1)S(1)}, u32[]{:S(2)}, u32[]{:S(2)}) collective-permute-start(bf16[32,128]{0,1:T(8,128)(2,1)S(1)} %fusion.42), channel_id=1, source_target_pairs={{0,1016},{8,0},{16,8},{24,16},{32,24},{40,32},{48,40},{56,48},{64,... | collective-permute-start | bytes 24584 | tf_op jit(solution)/shard_map/ppermute | solution.py:12
  25.1 1.2 copy-start.1
  27.6 3.3 %copy-start.2 = (pred[1458,1152]{1,0:T(8,128)(4,1)S(1)}, pred[1458,1152]{1,0:T(8,128)(4,1)}, u32[]{:S(2)}) copy-start(pred[1458,1152]{1,0:T(8,128)(4,1)} %copy-done.1) | copy-start | bytes 5038852
  29.0 7.8 %copy-start.7 = (s32[128]{0:T(128)S(1)}, s32[128]{0:T(128)}, u32[]{:S(2)}) copy-start(s32[128]{0:T(128)} %param.7) | copy-start | bytes 1540
  29.0 7.8 %collective-permute-start.1 = (f32[32,128]{1,0:T(8,128)S(1)}, f32[32,128]{1,0:T(8,128)S(1)}, u32[]{:S(2)}, u32[]{:S(2)}) collective-permute-start(f32[32,128]{1,0:T(8,128)S(1)} %slice_add_fusion.22), channel_id=1, source_target_pairs={{0,8},{8,16},{16,24},{24,32},{32,40},{40,48},{48,56},{56,64},{64,7... | collective-permute-start | bytes 49160 | tf_op jit(solution)/shard_map/ppermute | solution.py:12
  37.6 4.4 %collective-permute-start.2 = (bf16[32,128]{1,0:T(8,128)(2,1)S(1)}, bf16[32,128]{1,0:T(8,128)(2,1)S(1)}, u32[]{:S(2)}, u32[]{:S(2)}) collective-permute-start(bf16[32,128]{1,0:T(8,128)(2,1)S(1)} %fusion.43), channel_id=1, source_target_pairs={{0,1016},{8,0},{16,8},{24,16},{32,24},{40,32},{48,40},{56,48},{64,... | collective-permute-start | bytes 24584 | tf_op jit(solution)/shard_map/ppermute | solution.py:12
  43.3 3.3 %copy-start.3 = (pred[1458,1152]{1,0:T(8,128)(4,1)S(1)}, pred[1458,1152]{1,0:T(8,128)(4,1)}, u32[]{:S(2)}) copy-start(pred[1458,1152]{1,0:T(8,128)(4,1)} %copy-done.1) | copy-start | bytes 5038852
  44.6 7.8 %collective-permute-start.3 = (f32[32,128]{1,0:T(8,128)S(1)}, f32[32,128]{1,0:T(8,128)S(1)}, u32[]{:S(2)}, u32[]{:S(2)}) collective-permute-start(f32[32,128]{1,0:T(8,128)S(1)} %slice_add_fusion.20), channel_id=1, source_target_pairs={{0,8},{8,16},{16,24},{24,32},{32,40},{40,48},{48,56},{56,64},{64,7... | collective-permute-start | bytes 49160 | tf_op jit(solution)/shard_map/ppermute | solution.py:12
  53.2 4.4 %collective-permute-start.4 = (bf16[32,128]{1,0:T(8,128)(2,1)S(1)}, bf16[32,128]{1,0:T(8,128)(2,1)S(1)}, u32[]{:S(2)}, u32[]{:S(2)}) collective-permute-start(bf16[32,128]{1,0:T(8,128)(2,1)S(1)} %fusion.46), channel_id=1, source_target_pairs={{0,1016},{8,0},{16,8},{24,16},{32,24},{40,32},{48,40},{56,48},{64,... | collective-permute-start | bytes 24584 | tf_op jit(solution)/shard_map/ppermute | solution.py:12
  58.9 3.3 %copy-start.4 = (pred[1458,1152]{1,0:T(8,128)(4,1)S(1)}, pred[1458,1152]{1,0:T(8,128)(4,1)}, u32[]{:S(2)}) copy-start(pred[1458,1152]{1,0:T(8,128)(4,1)} %copy-done.1) | copy-start | bytes 5038852
  60.2 7.8 %collective-permute-start.5 = (f32[32,128]{1,0:T(8,128)S(1)}, f32[32,128]{1,0:T(8,128)S(1)}, u32[]{:S(2)}, u32[]{:S(2)}) collective-permute-start(f32[32,128]{1,0:T(8,128)S(1)} %slice_add_fusion.18), channel_id=1, source_target_pairs={{0,8},{8,16},{16,24},{24,32},{32,40},{40,48},{48,56},{56,64},{64,7... | collective-permute-start | bytes 49160 | tf_op jit(solution)/shard_map/ppermute | solution.py:12
  68.8 4.7 %collective-permute-start.6 = (bf16[32,128]{1,0:T(8,128)(2,1)S(1)}, bf16[32,128]{1,0:T(8,128)(2,1)S(1)}, u32[]{:S(2)}, u32[]{:S(2)}) collective-permute-start(bf16[32,128]{1,0:T(8,128)(2,1)S(1)} %fusion.49), channel_id=1, source_target_pairs={{0,1016},{8,0},{16,8},{24,16},{32,24},{40,32},{48,40},{56,48},{64,... | collective-permute-start | bytes 24584 | tf_op jit(solution)/shard_map/ppermute | solution.py:12
  74.8 3.3 %copy-start.5 = (pred[1458,1152]{1,0:T(8,128)(4,1)S(1)}, pred[1458,1152]{1,0:T(8,128)(4,1)}, u32[]{:S(2)}) copy-start(pred[1458,1152]{1,0:T(8,128)(4,1)} %copy-done.1) | copy-start | bytes 5038852
  76.1 7.8 %collective-permute-start.7 = (f32[32,128]{1,0:T(8,128)S(1)}, f32[32,128]{1,0:T(8,128)S(1)}, u32[]{:S(2)}, u32[]{:S(2)}) collective-permute-start(f32[32,128]{1,0:T(8,128)S(1)} %slice_add_fusion.16), channel_id=1, source_target_pairs={{0,8},{8,16},{16,24},{24,32},{32,40},{40,48},{48,56},{56,64},{64,7... | collective-permute-start | bytes 49160 | tf_op jit(solution)/shard_map/ppermute | solution.py:12
  106.8 4.7 %collective-permute-start.8 = (f32[32,256]{1,0:T(8,128)S(1)}, f32[32,256]{1,0:T(8,128)S(1)}, u32[]{:S(2)}, u32[]{:S(2)}) collective-permute-start(f32[32,256]{1,0:T(8,128)S(1)} %fusion.185), channel_id=1, source_target_pairs={{0,8},{8,0},{16,24},{24,16},{32,40},{40,32},{48,56},{56,48},{64,72... | collective-permute-start | bytes 98312 | tf_op jit(solution)/shard_map/ppermute | solution.py:92
  111.5 5.9 %collective-permute-start.9 = (f32[32,256]{1,0:T(8,128)S(1)}, f32[32,256]{1,0:T(8,128)S(1)}, u32[]{:S(2)}, u32[]{:S(2)}) collective-permute-start(f32[32,256]{1,0:T(8,128)S(1)} %add.155), channel_id=1, source_target_pairs={{0,24},{8,16},{16,8},{24,0},{32,56},{40,48},{48,40},{56,32},{64,88... | collective-permute-start | bytes 98312 | tf_op jit(solution)/shard_map/ppermute | solution.py:92
  117.3 4.6 %collective-permute-start.10 = (f32[32,256]{1,0:T(8,128)S(1)}, f32[32,256]{1,0:T(8,128)S(1)}, u32[]{:S(2)}, u32[]{:S(2)}) collective-permute-start(f32[32,256]{1,0:T(8,128)S(1)} %add.156), channel_id=1, source_target_pairs={{0,32},{8,40},{16,48},{24,56},{32,0},{40,8},{48,16},{56,24},{64,96... | collective-permute-start | bytes 98312 | tf_op jit(solution)/shard_map/ppermute | solution.py:95
  122.0 5.6 %collective-permute-start.11 = (f32[32,256]{1,0:T(8,128)S(1)}, f32[32,256]{1,0:T(8,128)S(1)}, u32[]{:S(2)}, u32[]{:S(2)}) collective-permute-start(f32[32,256]{1,0:T(8,128)S(1)} %add.157), channel_id=1, source_target_pairs={{0,64},{8,72},{16,80},{24,88},{32,96},{40,104},{48,112},{56,120},{... | collective-permute-start | bytes 98312 | tf_op jit(solution)/shard_map/ppermute | solution.py:95
  127.6 9.0 %collective-permute-start.12 = (f32[32,256]{1,0:T(8,128)S(1)}, f32[32,256]{1,0:T(8,128)S(1)}, u32[]{:S(2)}, u32[]{:S(2)}) collective-permute-start(f32[32,256]{1,0:T(8,128)S(1)} %add.158), channel_id=1, source_target_pairs={{0,128},{8,136},{16,144},{24,152},{32,160},{40,168},{48,176},{56,1... | collective-permute-start | bytes 98312 | tf_op jit(solution)/shard_map/ppermute | solution.py:95
  136.6 14.5 %collective-permute-start.13 = (f32[32,256]{1,0:T(8,128)S(1)}, f32[32,256]{1,0:T(8,128)S(1)}, u32[]{:S(2)}, u32[]{:S(2)}) collective-permute-start(f32[32,256]{1,0:T(8,128)S(1)} %add.159), channel_id=1, source_target_pairs={{0,256},{8,264},{16,272},{24,280},{32,288},{40,296},{48,304},{56,3... | collective-permute-start | bytes 98312 | tf_op jit(solution)/shard_map/ppermute | solution.py:95
  151.1 13.4 %collective-permute-start.14 = (f32[32,256]{1,0:T(8,128)S(1)}, f32[32,256]{1,0:T(8,128)S(1)}, u32[]{:S(2)}, u32[]{:S(2)}) collective-permute-start(f32[32,256]{1,0:T(8,128)S(1)} %add.160), channel_id=1, source_target_pairs={{0,768},{8,776},{16,784},{24,792},{32,800},{40,808},{48,816},{56,8... | collective-permute-start | bytes 98312 | tf_op jit(solution)/shard_map/ppermute | solution.py:95
